TPU v7x, 32 devices: a whole 2x2x4 slice. The times are simulated.
32 devices in a mesh: grp: 2 (over y), wide: 4 (over z), col: 2 (over x), inc: 2 (over core).
Axes of the slice: x: 2, y: 2, z: 4, core: 2. Of those that a mesh axis runs over, the one named last changes fastest.
Arguments:
- values_in: bfloat16 [32, 64, 256, 512], P(('grp', 'col'), 'inc', 'wide'), parts along dimension 0, may hold values from -6 to 6
- shock_load: float32 [32], P(('grp', 'col')), parts along dimension 0, may hold values from -4 to 4
- price_field: float32 [128, 256, 512], P(('grp', 'inc'), 'wide'), parts along dimension 0, may hold values from -6 to 6
- rate_liquid: float32 [128, 256, 512], P(('grp', 'inc'), 'wide'), parts along dimension 0, may hold values from 0.05 to 0.5
- rate_illiquid: float32 [128, 256, 512], P(('grp', 'inc'), 'wide'), parts along dimension 0, may hold values from 0.05 to 0.5
- mask_liquid: int32 [128, 256, 512], P(('grp', 'inc'), 'wide'), parts along dimension 0, may hold values 0 or 1
- mask_illiquid: int32 [128, 256, 512], P(('grp', 'inc'), 'wide'), parts along dimension 0, may hold values 0 or 1
- jump_inverse: float32 [128, 64], P('grp'), parts along dimension 0, may hold values from -0.07 to 0.87
- coef_liquid: int32 [4096], replicated, may hold values from 0 to 127, as said below
- coef_illiquid: int32 [4096], replicated, may hold values from 0 to 255
- coef_income: int32 [4096], replicated, may hold values from 0 to 63
- owner: int32 [4096], replicated, may hold values from 0 to 7, as said below
Outputs:
- reduced: float32 [32, 8192], P(('grp', 'col'), ('wide', 'inc')), parts along dimension 0
There are 2 independent parts, one for each index of `grp`. A program takes and returns all parts, laid end to end along the dimension named above; an argument that names none is the same for every part. Nothing has to cross between parts.
Inputs may be any that keep to these rules, and one draw needn't show every extreme that they name: `coef_liquid`: every retained coefficient has liquid frequency below 128. No owner has more than 1024 rows, and some owner has exactly 1024.
All inputs are finite; a program needn't handle non-finite values. No bound on the sum of `mask_liquid` or of `mask_illiquid` on one device may be relied on, other than what follows from the above.
Results may differ from a plain program's by a relative error of at most 0.0003.
Values may be sent and summed in bfloat16 or wider, within the bound.
No kernel may reach another device: no remote copies, remote signals or barrier semaphores. Data moves between devices by JAX's collectives and lax.ppermute only.
A program may use at most 256 MiB of HBM per device.

v0:
```python
import jax
import jax.numpy as jnp
from jax import lax
from jax.sharding import PartitionSpec as P

NB = 512
NA = 256
NZ = 64
KBLOW = 128


def padded_2(cells, sides, width):
    for axis, dim in sides:
        count = lax.axis_size(axis)
        ends = count - 1
        head = lax.slice_in_dim(cells, 0, width, axis=dim)
        tail = lax.slice_in_dim(cells, cells.shape[dim] - width, cells.shape[dim], axis=dim)
        cells = jnp.concatenate(
            [
                lax.ppermute(tail, axis, [(i, (i + 1) % count) for i in range(ends)]),
                cells,
                lax.ppermute(head, axis, [((i + 1) % count, i) for i in range(ends)]),
            ],
            axis=dim,
        )
    return cells


def cosine_table(count):
    freq = jnp.arange(count, dtype=jnp.int32)[:, None]
    cell = jnp.arange(count, dtype=jnp.int32)[None, :]
    phase = (2 * cell + 1) * freq % (4 * count)
    angle = jnp.pi * phase.astype(jnp.float32) / (2.0 * count)
    first = jnp.where(freq == 0, jnp.sqrt(jnp.float32(0.5)), jnp.float32(1.0))
    return jnp.cos(angle) * jnp.sqrt(jnp.float32(2.0 / count)) * first


def slot_targets(owner, owners, capacity):
    onehot = (owner[:, None] == jnp.arange(owners, dtype=jnp.int32)[None, :]).astype(jnp.int32)
    before = jnp.cumsum(onehot, axis=0) - onehot
    slot = jnp.sum(before * onehot, axis=1)
    return owner * capacity + slot


def body(
    values_in,
    shock_load,
    price_field,
    rate_liquid,
    rate_illiquid,
    mask_liquid,
    mask_illiquid,
    jump_inverse,
    coef_liquid,
    coef_illiquid,
    coef_income,
    owner,
):
    high = lax.Precision.HIGHEST
    columns = values_in.shape[0]
    wide_pos = lax.axis_index("wide")
    wide_count = lax.axis_size("wide")
    padded = padded_2(values_in, (("wide", 2),), 1).astype(jnp.float32)
    center = padded[:, :, 1:-1]
    lower = jnp.where(wide_pos == 0, center[:, :, 0:1], padded[:, :, 0:1])
    upper = jnp.where(wide_pos == wide_count - 1, center[:, :, -1:], padded[:, :, -1:])
    fwd_a = jnp.concatenate([center[:, :, 1:], upper], axis=2) - center
    bwd_a = center - jnp.concatenate([lower, center[:, :, :-1]], axis=2)
    step_b = center[:, :, :, 1:] - center[:, :, :, :-1]
    zero_b = jnp.zeros(center.shape[:3] + (1,), jnp.float32)
    fwd_b = jnp.concatenate([step_b, zero_b], axis=3)
    bwd_b = jnp.concatenate([zero_b, step_b], axis=3)
    mask_b = mask_liquid.astype(jnp.float32)
    mask_a = mask_illiquid.astype(jnp.float32)
    load = shock_load[:, None, None, None]
    explicit = (
        center
        + rate_liquid * (mask_b * fwd_b - (1.0 - mask_b) * bwd_b)
        + rate_illiquid * (mask_a * fwd_a - (1.0 - mask_a) * bwd_a)
        + load * price_field
    )
    freq_rows = KBLOW
    table_b = cosine_table(NB)[:freq_rows]
    liquid_part = jnp.einsum("kb,czab->czak", table_b, explicit, precision=high)
    table_z = cosine_table(NZ)
    table_a = cosine_table(NA)
    owners = lax.axis_size(("wide", "inc"))
    capacity = 2 * owner.shape[0] // owners
    targets = slot_targets(owner, owners, capacity)
    blocks = lax.all_to_all(
        lax.all_to_all(liquid_part, "wide", split_axis=3, concat_axis=2, tiled=True),
        "inc",
        split_axis=3,
        concat_axis=1,
        tiled=True,
    )
    folded = jnp.dot(table_z, jump_inverse, precision=high)
    income_part = jnp.einsum("yz,czak->cyak", folded, blocks, precision=high)
    spectrum = jnp.einsum("ia,cjak->cjik", table_a, income_part, precision=high)
    local_rows = spectrum.shape[3]
    start = lax.axis_index(("wide", "inc")) * local_rows
    mine = (coef_liquid >= start) & (coef_liquid < start + local_rows)
    offset = jnp.clip(coef_liquid - start, 0, local_rows - 1)
    position = (coef_income * NA + coef_illiquid) * local_rows + offset
    flat = spectrum.reshape(columns, -1)
    kept = jnp.where(mine[None, :], jnp.take(flat, position, axis=1), jnp.float32(0.0))
    placed = jnp.zeros((columns, owners * capacity), jnp.float32).at[:, targets].set(kept)
    return lax.psum_scatter(placed, ("wide", "inc"), scatter_dimension=1, tiled=True)


def solution(mesh):
    placed = (
        P(("grp", "col"), "inc", "wide", None),
        P(("grp", "col")),
        P(("grp", "inc"), "wide", None),
        P(("grp", "inc"), "wide", None),
        P(("grp", "inc"), "wide", None),
        P(("grp", "inc"), "wide", None),
        P(("grp", "inc"), "wide", None),
        P("grp", None),
        P(),
        P(),
        P(),
        P(),
    )
    return jax.shard_map(
        body,
        mesh=mesh,
        in_specs=placed,
        out_specs=P(("grp", "col"), ("wide", "inc")),
        check_vma=False,
    )
```

profile of v0, /device:TPU:0, one launch (start us, length us, event | category | flops | bytes accessed | tf_op | source)
XLA Modules:
  0.0 726.5 jit_solution(2988138333981204830)
XLA Ops:
  6.5 3.4 fusion.115
  10.0 4.9 collective-permute-start
  16.3 4.9 convert_element_type.28
  21.3 8.5 %broadcast_subtract_fusion = (f32[32,64,512]{2,1,0:T(8,128)}, f32[32,64,512]{2,1,0:T(8,128)}) fusion(s32[32,64,512]{2,1,0:T(8,128)} %param.18, s32[32,64,512]{2,1,0:T(8,128)} %param.17), kind=kLoop, calls=%fused_computation.43 | loop fusion | flops 4194304 | bytes 16777216 | tf_op jit(solution)/shard_map/sub | solution.py:79
  34.0 21.0 %maximum_convert_fusion = f32[8,32,66,512]{3,2,1,0:T(8,128)} fusion(bf16[8,32,1,512]{3,2,1,0:T(2,128)(2,1)S(1)} %copy.23, bf16[8,32,64,512]{3,2,1,0:T(8,128)(2,1)} %param.12, bf16[8,32,1,512]{3,2,1,0:T(2,128)(2,1)S(1)} %copy.22), kind=kLoop, calls=%fused_computation.25 | loop fusion | flops 51904512 | bytes 51904512 | tf_op jit(solution)/shard_map/convert_element_type | solution.py:63
  55.0 47.7 %fusion.114 = (f32[8,32,63,512]{3,2,1,0:T(8,128)}, f32[8,32,63,512]{3,2,1,0:T(8,128)}) fusion(f32[8,32,66,512]{3,2,1,0:T(8,128)} %maximum_convert_fusion), kind=kLoop, calls=%fused_computation.141 | loop fusion | bytes 132120576 | tf_op jit(solution)/shard_map/slice | solution.py:68
  102.7 36.6 %slice_subtract_fusion = f32[8,32,64,511]{3,2,1,0:T(8,128)} fusion(f32[8,32,66,512]{3,2,1,0:T(8,128)} %maximum_convert_fusion), kind=kLoop, calls=%fused_computation.2 | loop fusion | flops 8372224 | bytes 100466688 | tf_op jit(solution)/shard_map/sub | solution.py:69
  139.4 4.9 broadcast_select_fusion
  144.3 74.5 %fusion.5 = f32[8,32,64,128]{3,2,1,0:T(8,128)} fusion(f32[8,32,1,512]{3,2,1,0:T(1,128)S(1)} %get-tuple-element.10, f32[8,32,63,512]{3,2,1,0:T(8,128)} %get-tuple-element.8, f32[8,32,63,512]{3,2,1,0:T(8,128)} %get-tuple-element.7, f32[8,32,1,512]{3,2,1,0:T(1,128)S(1)} %get-tuple-element.9, f32[8,32,66,512]{3,2,1,0:T(8,128)} %maximum_convert_fusion, ...), kind=kOutput, calls=%fused_computation.9 | convolution fusion | flops 13019512832 | bytes 173409280 | tf_op jit(solution)/shard_map/kb,czab->czak/dot_general | solution.py:84
  218.8 16.7 %copy.24 = f32[8,32,64,128]{2,1,0,3:T(8,128)} copy(f32[8,32,64,128]{3,2,1,0:T(8,128)} %fusion.5) | data formatting | bytes 16777216 | tf_op jit(solution)/shard_map/kb,czab->czak/dot_general | solution.py:84
  235.5 14.4 %reshape.110 = f32[4,1,524288]{2,1,0:T(1,128)} reshape(f32[128,8,32,64]{3,2,1,0:T(8,128)} %bitcast.55) | data formatting | bytes 16777216
  249.9 5.9 all-to-all-start
  259.3 180.0 %all-to-all-done = f32[4,1,524288]{2,1,0:T(1,128)} async-done(((f32[4,1,524288]{2,1,0:T(1,128)}), f32[4,1,524288]{2,1,0:T(1,128)}, u32[]{:S(2)}, u32[]{:S(2)}) %all-to-all-start) | async-done | bytes 8388640 | tf_op jit(solution)/shard_map/all_to_all | solution.py:91
  439.9 28.4 %reduce.2 = f32[4,524288]{1,0:T(4,128)} reduce(f32[4,1,524288]{2,1,0:T(1,128)} %all-to-all-done, f32[]{:T(128)} %broadcast.191), dimensions={1}, to_apply=%all_to_all.26.reduce_sub_computation | reduce | bytes 16777220 | tf_op jit(solution)/shard_map/all_to_all | solution.py:91
  468.3 16.8 %reshape.111 = f32[128,8,32,64]{3,2,1,0:T(8,128)} reshape(f32[4,524288]{1,0:T(4,128)} %reduce.2) | data formatting | bytes 16777216
  485.0 21.0 %copy.39 = f32[8,32,4,64,32]{3,2,1,0,4:T(4,128)} copy(f32[8,32,4,64,32]{3,1,0,4,2:T(8,128)} %bitcast.56) | data formatting | bytes 16777216 | tf_op jit(solution)/shard_map/all_to_all | solution.py:91
  506.0 15.9 %reshape.98 = f32[8,32,256,32]{2,1,0,3:T(8,128)} reshape(f32[8,32,4,64,32]{3,2,1,0,4:T(4,128)} %copy.39) | data formatting | bytes 16777216 | tf_op jit(solution)/shard_map/all_to_all | solution.py:91
  521.9 12.1 %all_to_all.36 = f32[8,32,256,32]{2,1,0,3:T(8,128)S(1)} all-to-all(f32[8,32,256,32]{2,1,0,3:T(8,128)} %reshape.98), channel_id=1, replica_groups=mesh['grp'=2,'wide'=4,'col'=2,'inc'=2] {'inc'}, dimensions={3} | all-to-all | bytes 16777216 | tf_op jit(solution)/shard_map/all_to_all | solution.py:90
  534.0 6.7 copy.29
  540.6 13.7 %fusion.37 = f32[8,64,256,16]{2,1,3,0:T(8,128)S(1)} fusion(f32[64,64,1,1]{1,0,3,2:T(8,128)S(1)} %convolution_bitcast_fusion, f32[8,64,256,16]{2,3,1,0:T(8,128)S(1)} %bitcast.57), kind=kOutput, calls=%fused_computation.39 | convolution fusion | flops 1610612736 | bytes 16793600 | tf_op jit(solution)/shard_map/yz,czak->cyak/dot_general | solution.py:98
  554.4 13.7 %fusion.34 = f32[8,64,256,16]{2,3,1,0:T(8,128)} fusion(f32[8,64,256,16]{2,1,3,0:T(8,128)S(1)} %fusion.37, f32[256]{0:T(256)S(1)} %fusion.99, s32[256]{0:T(256)S(1)} %multiply_add_fusion.1), kind=kOutput, calls=%fused_computation.38 | convolution fusion | flops 6443433984 | bytes 16779264 | tf_op jit(solution)/shard_map/ia,cjak->cjik/dot_general | solution.py:99
  568.1 61.8 %copy.41 = f32[8,64,256,16]{0,3,2,1:T(8,128)} copy(f32[8,64,256,16]{2,3,1,0:T(8,128)} %fusion.34) | data formatting | bytes 16777216 | tf_op jit(solution)/shard_map/reshape | solution.py:105
  629.9 38.6 %scatter_custom_fusion = f32[8,8192]{0,1:T(8,128)} fusion(s32[4096]{0:T(1024)S(1)} %get-tuple-element.17, f32[]{:T(128)} %constant.42.clone.1, f32[]{:T(128)} %constant.125.clone.1, pred[4096]{0:T(1024)(128)(4,1)S(1)} %compare_and_fusion.1, pred[4096]{0:T(1024)(128)(4,1)S(1)} %compare_and_fusion, f32[8,262144]{0,1:T(8,128)} %bitcast.17, ...), kind=kCustom, calls=%fused_computation.40 | custom fusion | flops 65536 | bytes 134505984 | tf_op jit(solution)/shard_map/scatter | solution.py:107
  668.5 49.1 %reduce-scatter.2.cloned.1.call-done = f32[8,1024]{0,1:T(8,128)} async-done(((f32[8,8192]{0,1:T(8,128)}), f32[8,1024]{0,1:T(8,128)}) %reduce-scatter.2.cloned.1.call-update) | async-done | bytes 32784 | tf_op jit(solution)/shard_map/reduce_scatter | solution.py:108
  (50 shorter events, 11.3 us)
Async XLA Ops:
  6.5 252.2 %copy-start = (f32[64,64]{1,0:T(8,128)S(1)}, f32[64,64]{1,0:T(8,128)}, u32[]{:S(2)}) copy-start(f32[64,64]{1,0:T(8,128)} %param.19) | copy-start | bytes 49156
  6.5 23.2 %copy-start.2 = (s32[32,64,512]{2,1,0:T(8,128)S(1)}, s32[32,64,512]{2,1,0:T(8,128)}, u32[]{:S(2)}) copy-start(s32[32,64,512]{2,1,0:T(8,128)} %param.18) | copy-start | bytes 12582916
  10.0 23.1 %collective-permute-start = (bf16[8,32,1,512]{3,1,2,0:T(8,128)(2,1)S(1)}, bf16[8,32,1,512]{3,1,2,0:T(8,128)(2,1)S(1)}, u32[]{:S(2)}, u32[]{:S(2)}) collective-permute-start(bf16[8,32,1,512]{3,1,2,0:T(8,128)(2,1)S(1)} %copy.44), channel_id=1, source_target_pairs={{0,4},{4,8},{8,12},{1,5},{5,9},{9,13},{2,6},{6,10},{10,14},{3,7},{... | collective-permute-start | bytes 786440 | tf_op jit(solution)/shard_map/ppermute | solution.py:20
  15.0 18.6 %collective-permute-start.1 = (bf16[8,32,1,512]{3,1,2,0:T(8,128)(2,1)S(1)}, bf16[8,32,1,512]{3,1,2,0:T(8,128)(2,1)S(1)}, u32[]{:S(2)}, u32[]{:S(2)}) collective-permute-start(bf16[8,32,1,512]{3,1,2,0:T(8,128)(2,1)S(1)} %copy.45), channel_id=1, source_target_pairs={{4,0},{8,4},{12,8},{5,1},{9,5},{13,9},{6,2},{10,6},{14,10},{7,3},{... | collective-permute-start | bytes 786440 | tf_op jit(solution)/shard_map/ppermute | solution.py:22
  32.3 22.7 %copy-start.8 = (f32[512]{0:T(512)}, f32[512]{0:T(512)S(1)}, u32[]{:S(2)}) copy-start(f32[512]{0:T(512)S(1)} %select_multiply_fusion) | copy-start | bytes 6148
  139.4 4.9 copy-start.1
  139.4 4.9 copy-start.5
  139.4 4.9 slice-start
  235.5 20.3 %copy-start.3 = (s32[4096]{0:T(1024)S(1)}, s32[4096]{0:T(1024)}, u32[]{:S(2)}) copy-start(s32[4096]{0:T(1024)} %param.23) | copy-start | bytes 49156
  235.5 23.7 %copy-start.4 = (s32[4096]{0:T(1024)S(1)}, s32[4096]{0:T(1024)}, u32[]{:S(2)}) copy-start(s32[4096]{0:T(1024)} %param.20) | copy-start | bytes 49156
  235.5 23.8 %copy-start.6 = (s32[4096]{0:T(1024)S(1)}, s32[4096]{0:T(1024)}, u32[]{:S(2)}) copy-start(s32[4096]{0:T(1024)} %param.21) | copy-start | bytes 49156
  235.5 23.8 %copy-start.7 = (s32[4096]{0:T(1024)S(1)}, s32[4096]{0:T(1024)}, u32[]{:S(2)}) copy-start(s32[4096]{0:T(1024)} %param.22) | copy-start | bytes 49156
  249.9 189.4 %all-to-all-start = ((f32[4,1,524288]{2,1,0:T(1,128)}), f32[4,1,524288]{2,1,0:T(1,128)}, u32[]{:S(2)}, u32[]{:S(2)}) async-start(f32[4,1,524288]{2,1,0:T(1,128)} %reshape.110), calls=%async_computation | async-start | bytes 16777216 | tf_op jit(solution)/shard_map/all_to_all | solution.py:91
  255.9 461.7 %reduce-scatter.2.cloned.1.call-start = ((), (), s32[]{:S(2)}) async-start(), calls=%async_computation.3 | async-start | bytes 4718592 | tf_op jit(solution)/shard_map/reduce_scatter | solution.py:108
Sparse Core Ops, SparseCore 0:
  668.6 48.9 reduce-scatter.1
where the time goes:
time: 733 us; the launch traced here: 726 us
  waiting for transfers between devices  229 us (31%)
  local copies, waits for them, and re-layouts  208 us (28%)
  other arithmetic  149 us (20%)
  matrix products  102 us (14%)
  between operations  13.8 us (2%)
  starting transfers between devices  12.2 us (2%)
  blocking collectives  12.1 us (2%)
    all_to_all x1, waiting for transfers between devices, body(): lax.all_to_all(liquid_part, 'wide', split_axis=3, concat_axis=2, tiled=True)  180 us
    dot_general x1, matrix products, body(): liquid_part = jnp.einsum('kb,czab->czak', table_b, explicit, precision=high)  74.5 us
    reshape x1, local copies, waits for them, and re-layouts, body(): flat = spectrum.reshape(columns, -1)  61.8 us
    reduce_scatter x1, waiting for transfers between devices, body(): lax.psum_scatter(placed, ('wide', 'inc'), scatter_dimension=1, tiled=True)  49.1 us
    slice x1, local copies, waits for them, and re-layouts, body(): bwd_a = center - jnp.concatenate([lower, center[:, :, :-1]], axis=2)  47.7 us
    scatter x1, other arithmetic, body(): jnp.zeros((columns, owners * capacity), jnp.float32).at[:, targets]  38.6 us
    all_to_all x3, local copies, waits for them, and re-layouts, body(): lax.all_to_all(liquid_part, 'wide', split_axis=3, concat_axis=2, tiled=True)  37.4 us
    sub x1, other arithmetic, body(): step_b = center[:, :, :, 1:] - center[:, :, :, :-1]  36.6 us
  transfers between devices with their start and end apart: 4, of which 2 were waited for; matrix products, arithmetic and copies ran while one was open for 3% of the time, Pallas kernels for 0%

commit v1 on v0

--- a/solution.py
+++ b/solution.py
@@ -56,9 +56,10 @@
     coef_income,
     owner,
 ):
-    high = lax.Precision.HIGHEST
-    columns = values_in.shape[0]
+    high = lax.Precision.HIGH
+    columns, nz_loc, na_loc, _ = values_in.shape
     wide_pos = lax.axis_index("wide")
+    inc_pos = lax.axis_index("inc")
     wide_count = lax.axis_size("wide")
     padded = padded_2(values_in, (("wide", 2),), 1).astype(jnp.float32)
     center = padded[:, :, 1:-1]
@@ -79,33 +80,25 @@
         + rate_illiquid * (mask_a * fwd_a - (1.0 - mask_a) * bwd_a)
         + load * price_field
     )
-    freq_rows = KBLOW
-    table_b = cosine_table(NB)[:freq_rows]
+    table_b = cosine_table(NB)[:KBLOW]
     liquid_part = jnp.einsum("kb,czab->czak", table_b, explicit, precision=high)
-    table_z = cosine_table(NZ)
-    table_a = cosine_table(NA)
+    table_a = lax.dynamic_slice_in_dim(cosine_table(NA), wide_pos * na_loc, na_loc, axis=1)
+    illiquid_part = jnp.einsum("ja,czak->jkcz", table_a, liquid_part, precision=high)
+    rows = illiquid_part.reshape(NA * KBLOW, columns * nz_loc)
+    picked = jnp.take(rows, coef_illiquid * KBLOW + coef_liquid, axis=0)
+    folded = jnp.dot(cosine_table(NZ), jump_inverse, precision=lax.Precision.HIGHEST)
+    folded = lax.dynamic_slice_in_dim(folded, inc_pos * nz_loc, nz_loc, axis=1)
+    weight = jnp.take(folded, coef_income, axis=0)
+    partial = jnp.sum(picked.reshape(-1, columns, nz_loc) * weight[:, None, :], axis=2)
+    kept = lax.psum(partial, ("wide", "inc"))
     owners = lax.axis_size(("wide", "inc"))
-    capacity = 2 * owner.shape[0] // owners
+    count = owner.shape[0]
+    capacity = 2 * count // owners
     targets = slot_targets(owner, owners, capacity)
-    blocks = lax.all_to_all(
-        lax.all_to_all(liquid_part, "wide", split_axis=3, concat_axis=2, tiled=True),
-        "inc",
-        split_axis=3,
-        concat_axis=1,
-        tiled=True,
-    )
-    folded = jnp.dot(table_z, jump_inverse, precision=high)
-    income_part = jnp.einsum("yz,czak->cyak", folded, blocks, precision=high)
-    spectrum = jnp.einsum("ia,cjak->cjik", table_a, income_part, precision=high)
-    local_rows = spectrum.shape[3]
-    start = lax.axis_index(("wide", "inc")) * local_rows
-    mine = (coef_liquid >= start) & (coef_liquid < start + local_rows)
-    offset = jnp.clip(coef_liquid - start, 0, local_rows - 1)
-    position = (coef_income * NA + coef_illiquid) * local_rows + offset
-    flat = spectrum.reshape(columns, -1)
-    kept = jnp.where(mine[None, :], jnp.take(flat, position, axis=1), jnp.float32(0.0))
-    placed = jnp.zeros((columns, owners * capacity), jnp.float32).at[:, targets].set(kept)
-    return lax.psum_scatter(placed, ("wide", "inc"), scatter_dimension=1, tiled=True)
+    source = jnp.full((owners * capacity,), count, jnp.int32).at[targets].set(jnp.arange(count, dtype=jnp.int32))
+    mine = lax.dynamic_slice_in_dim(source, lax.axis_index(("wide", "inc")) * capacity, capacity)
+    gathered = jnp.take(kept, jnp.minimum(mine, count - 1), axis=0)
+    return jnp.where((mine < count)[None, :], gathered.T, jnp.float32(0.0))
 
 
 def solution(mesh):

time: 733 us -> 502 us (0.68)
  waiting for transfers between devices: 229 us -> 66.7 us
  other arithmetic: 149 us -> 96.1 us
  local copies, waits for them, and re-layouts: 208 us -> 222 us
  blocking collectives: 12.1 us -> 0 us
    all_to_all x1 -> x0, waiting for transfers between devices: 180 us -> none  [body(): lax.all_to_all(liquid_part, 'wide', split_axis=3, concat_axis=2, tiled=True)]
    psum x0 -> x1, waiting for transfers between devices: none -> 66.6 us  [body(): kept = lax.psum(partial, ('wide', 'inc'))]
    gather x0 -> x4, local copies, waits for them, and re-layouts: none -> 50.8 us  [the longest x2 32.3 us: body(): picked = jnp.take(rows, coef_illiquid * KBLOW + coef_liquid, axis=0)]
    reduce_scatter x1 -> x0, waiting for transfers between devices: 49.1 us -> none  [body(): lax.psum_scatter(placed, ('wide', 'inc'), scatter_dimension=1, tiled=True)]
    all_to_all x4 -> x0, local copies, waits for them, and re-layouts: 44 us -> none  [the longest x3 37.4 us: body(): lax.all_to_all(liquid_part, 'wide', split_axis=3, concat_axis=2, tiled=True)]
    scatter x1 -> x0, other arithmetic: 38.6 us -> none  [body(): jnp.zeros((columns, owners * capacity), jnp.float32).at[:, targets]]
    transpose x0 -> x1, local copies, waits for them, and re-layouts: none -> 31.1 us  [body(): jnp.einsum('ja,czak->jkcz', table_a, liquid_part, precision=high)]
    reshape x1, local copies, waits for them, and re-layouts: 61.8 us -> 33.4 us  [body(): rows = illiquid_part.reshape(NA * KBLOW, columns * nz_loc)]
  transfers between devices with their start and end apart: 4 -> 3, of which waited for: 2 -> 1; matrix products, arithmetic and copies ran while one was open for 3% -> 13% of each run, Pallas kernels for 0% -> 0%
where the time goes in v1:
time: 502 us; the launch traced here: 500 us
  local copies, waits for them, and re-layouts  222 us (44%)
  other arithmetic  96.1 us (19%)
  matrix products  95.4 us (19%)
  waiting for transfers between devices  66.7 us (13%)
  between operations  13.7 us (3%)
  starting transfers between devices  6.96 us (1%)
    dot_general x1, matrix products, body(): liquid_part = jnp.einsum('kb,czab->czak', table_b, explicit, precision=high)  73 us
    psum x1, waiting for transfers between devices, body(): kept = lax.psum(partial, ('wide', 'inc'))  66.6 us
    slice x1, local copies, waits for them, and re-layouts, body(): bwd_a = center - jnp.concatenate([lower, center[:, :, :-1]], axis=2)  47.7 us
    sub x1, other arithmetic, body(): step_b = center[:, :, :, 1:] - center[:, :, :, :-1]  36.7 us
    reshape x1, local copies, waits for them, and re-layouts, body(): rows = illiquid_part.reshape(NA * KBLOW, columns * nz_loc)  33.4 us
    unnamed x33, local copies, waits for them, and re-layouts  32.6 us
    gather x2, local copies, waits for them, and re-layouts, body(): picked = jnp.take(rows, coef_illiquid * KBLOW + coef_liquid, axis=0)  32.3 us
    transpose x1, local copies, waits for them, and re-layouts, body(): jnp.einsum('ja,czak->jkcz', table_a, liquid_part, precision=high)  31.1 us
  transfers between devices with their start and end apart: 3, of which 1 were waited for; matrix products, arithmetic and copies ran while one was open for 13% of the time, Pallas kernels for 0%

profile of v1, /device:TPU:0, one launch (start us, length us, event | category | flops | bytes accessed | tf_op | source)
XLA Modules:
  0.0 500.5 jit_solution(14844286475312916411)
XLA Ops:
  6.6 3.3 fusion.94
  9.9 5.6 %collective-permute-start = (bf16[8,32,1,512]{3,1,2,0:T(8,128)(2,1)S(1)}, bf16[8,32,1,512]{3,1,2,0:T(8,128)(2,1)}, u32[]{:S(2)}, u32[]{:S(2)}) collective-permute-start(bf16[8,32,1,512]{3,1,2,0:T(8,128)(2,1)S(1)} %copy.34), channel_id=1, source_target_pairs={{0,4},{4,8},{8,12},{1,5},{5,9},{9,13},{2,6},{6,10},{10,14},{3,7},{... | collective-permute-start | bytes 786440 | tf_op jit(solution)/shard_map/ppermute | solution.py:20
  17.6 4.9 convert_element_type.28
  22.6 8.5 %broadcast_subtract_fusion = (f32[32,64,512]{2,1,0:T(8,128)}, f32[32,64,512]{2,1,0:T(8,128)}) fusion(s32[32,64,512]{2,1,0:T(8,128)} %param.18, s32[32,64,512]{2,1,0:T(8,128)} %param.17), kind=kLoop, calls=%fused_computation.39 | loop fusion | flops 4194304 | bytes 16777216 | tf_op jit(solution)/shard_map/sub | solution.py:80
  31.1 4.9 convert_element_type.29
  40.3 14.1 %gather_fusion.1 = f32[4096,32]{1,0:T(8,128)} fusion(f32[64,32]{1,0:T(8,128)S(1)} %copy.28, s32[4096]{0:T(1024)S(1)} %fusion.78), kind=kCustom, calls=%fused_computation.1 | custom fusion | bytes 1064960 | tf_op jit(solution)/shard_map/jit(_take)/gather | solution.py:91
  54.4 3.6 broadcast_select_fusion
  59.4 2.3 reduce-window.6
  62.5 15.5 %scatter_custom_fusion = s32[8192]{0:T(1024)S(1)} fusion(s32[4096]{0:T(1024)S(1)} %compare_select_fusion.2, s32[4096]{0:T(1024)S(1)} %iota.47, s32[]{:T(128)} %constant.66.clone.1), kind=kCustom, calls=%fused_computation.109 | custom fusion | bytes 32772 | tf_op jit(solution)/shard_map/scatter | solution.py:98
  82.0 20.9 %maximum_convert_fusion = f32[8,32,66,512]{3,2,1,0:T(8,128)} fusion(bf16[8,32,1,512]{3,2,1,0:T(2,128)(2,1)S(1)} %copy.24, bf16[8,32,64,512]{3,2,1,0:T(8,128)(2,1)} %param.12, bf16[8,32,1,512]{3,2,1,0:T(2,128)(2,1)S(1)} %copy.23), kind=kLoop, calls=%fused_computation.28 | loop fusion | flops 51904512 | bytes 51904512 | tf_op jit(solution)/shard_map/convert_element_type | solution.py:64
  102.9 47.7 %fusion.93 = (f32[8,32,63,512]{3,2,1,0:T(8,128)}, f32[8,32,63,512]{3,2,1,0:T(8,128)}) fusion(f32[8,32,66,512]{3,2,1,0:T(8,128)} %maximum_convert_fusion), kind=kLoop, calls=%fused_computation.140 | loop fusion | bytes 132120576 | tf_op jit(solution)/shard_map/slice | solution.py:69
  150.6 36.7 %slice_subtract_fusion = f32[8,32,64,511]{3,2,1,0:T(8,128)} fusion(f32[8,32,66,512]{3,2,1,0:T(8,128)} %maximum_convert_fusion), kind=kLoop, calls=%fused_computation.5 | loop fusion | flops 8372224 | bytes 100466688 | tf_op jit(solution)/shard_map/sub | solution.py:70
  187.3 4.8 broadcast_select_fusion.1
  192.2 73.0 %fusion.5 = f32[8,32,64,128]{3,2,1,0:T(8,128)} fusion(f32[8,32,1,512]{3,2,1,0:T(1,128)S(1)} %get-tuple-element.8, f32[8,32,63,512]{3,2,1,0:T(8,128)} %get-tuple-element.6, f32[8,32,63,512]{3,2,1,0:T(8,128)} %get-tuple-element.5, f32[8,32,1,512]{3,2,1,0:T(1,128)S(1)} %get-tuple-element.7, f32[8,32,66,512]{3,2,1,0:T(8,128)} %maximum_convert_fusion, ...), kind=kOutput, calls=%fused_computation.12 | convolution fusion | flops 6577061888 | bytes 173409280 | tf_op jit(solution)/shard_map/kb,czab->czak/dot_general | solution.py:84
  265.2 22.0 %convolution_bitcast_fusion = f32[256,128,8,32]{0,1,3,2:T(8,128)} fusion(f32[8,32,64,128]{3,2,1,0:T(8,128)} %fusion.5, s32[256,256]{0,1:T(8,128)} %negate_select_fusion.2, s32[]{:T(128)S(6)} %select_n.124, pred[256,256]{0,1:T(32,128)(4,1)} %get-tuple-element.16, pred[256,256]{0,1:T(32,128)(4,1)} %get-tuple-element.15, f32[256]{0:T(256)S(1)} %copy-done.14), kind=kOutput, calls=%fused_computation.37 | convolution fusion | flops 3221323776 | bytes 42042372 | tf_op jit(solution)/shard_map/ja,czak->jkcz/dot_general | solution.py:86
  287.3 31.1 %copy.25 = f32[256,128,8,32]{1,0,3,2:T(8,128)} copy(f32[256,128,8,32]{0,1,3,2:T(8,128)} %convolution_bitcast_fusion) | data formatting | bytes 67108864 | tf_op jit(solution)/shard_map/ja,czak->jkcz/transpose | solution.py:86
  318.4 31.8 %copy.40 = f32[32,8,256,128]{3,1,2,0:T(8,128)} copy(f32[32,8,256,128]{3,2,1,0:T(8,128)} %bitcast.48) | data formatting | bytes 67108864
  350.1 33.4 %copy.26 = f32[32768,256]{1,0:T(8,128)} copy(f32[32768,256]{0,1:T(8,128)} %bitcast.49) | data formatting | bytes 67108864 | tf_op jit(solution)/shard_map/reshape | solution.py:87
  383.6 26.7 %gather_fusion = f32[4096,256]{1,0:T(8,128)} fusion(f32[32768,256]{1,0:T(8,128)} %copy.26, s32[4096]{0:T(1024)S(1)} %copy-done.5), kind=kCustom, calls=%fused_computation | custom fusion | bytes 8404992 | tf_op jit(solution)/shard_map/jit(_take)/gather | solution.py:88
  410.3 5.6 %copy.27 = f32[4096,256]{0,1:T(8,128)} copy(f32[4096,256]{1,0:T(8,128)} %gather_fusion) | data formatting | bytes 8388608 | tf_op jit(solution)/shard_map/jit(_take)/gather | solution.py:88
  415.9 2.9 multiply_reduce_fusion
  418.8 1.9 copy.30
  421.5 66.6 %all-reduce.4.cloned.1.call-done = f32[4096,8]{1,0:T(8,128)} async-done(((f32[4096,8]{1,0:T(8,128)}), f32[4096,8]{1,0:T(8,128)}) %all-reduce.4.cloned.1.call-update) | async-done | bytes 131088 | tf_op jit(solution)/shard_map/psum | solution.py:93
  488.1 4.4 gather_fusion.2
  (70 shorter events, 14.3 us)
Async XLA Ops:
  6.5 33.3 %copy-start = (f32[64,64]{1,0:T(8,128)S(1)}, f32[64,64]{1,0:T(8,128)}, u32[]{:S(2)}) copy-start(f32[64,64]{1,0:T(8,128)} %param.19) | copy-start | bytes 49156
  6.5 31.8 %copy-start.8 = (s32[4096]{0:T(1024)S(1)}, s32[4096]{0:T(1024)}, u32[]{:S(2)}) copy-start(s32[4096]{0:T(1024)} %param.22) | copy-start | bytes 49156
  6.5 31.8 %copy-start.6 = (s32[4096]{0:T(1024)S(1)}, s32[4096]{0:T(1024)}, u32[]{:S(2)}) copy-start(s32[4096]{0:T(1024)} %param.20) | copy-start | bytes 49156
  6.5 31.8 %copy-start.7 = (s32[4096]{0:T(1024)S(1)}, s32[4096]{0:T(1024)}, u32[]{:S(2)}) copy-start(s32[4096]{0:T(1024)} %param.21) | copy-start | bytes 49156
  6.5 52.9 %copy-start.4 = (s32[4096]{0:T(1024)S(1)}, s32[4096]{0:T(1024)}, u32[]{:S(2)}) copy-start(s32[4096]{0:T(1024)} %param.23) | copy-start | bytes 49156
  6.5 481.5 %all-reduce.4.cloned.1.call-start = ((), (), s32[]{:S(2)}) async-start(), calls=%async_computation | async-start | bytes 4194304 | tf_op jit(solution)/shard_map/psum | solution.py:93
  9.9 69.3 %collective-permute-start = (bf16[8,32,1,512]{3,1,2,0:T(8,128)(2,1)S(1)}, bf16[8,32,1,512]{3,1,2,0:T(8,128)(2,1)}, u32[]{:S(2)}, u32[]{:S(2)}) collective-permute-start(bf16[8,32,1,512]{3,1,2,0:T(8,128)(2,1)S(1)} %copy.34), channel_id=1, source_target_pairs={{0,4},{4,8},{8,12},{1,5},{5,9},{9,13},{2,6},{6,10},{10,14},{3,7},{... | collective-permute-start | bytes 786440 | tf_op jit(solution)/shard_map/ppermute | solution.py:20
  16.3 64.3 %collective-permute-start.1 = (bf16[8,32,1,512]{3,1,2,0:T(8,128)(2,1)}, bf16[8,32,1,512]{3,1,2,0:T(8,128)(2,1)}, u32[]{:S(2)}, u32[]{:S(2)}) collective-permute-start(bf16[8,32,1,512]{3,1,2,0:T(8,128)(2,1)} %copy.35), channel_id=1, source_target_pairs={{4,0},{8,4},{12,8},{5,1},{9,5},{13,9},{6,2},{10,6},{14,10},{7,3},{... | collective-permute-start | bytes 786440 | tf_op jit(solution)/shard_map/ppermute | solution.py:22
  36.0 66.9 %copy-start.13 = (f32[512]{0:T(512)}, f32[512]{0:T(512)S(1)}, u32[]{:S(2)}) copy-start(f32[512]{0:T(512)S(1)} %select_multiply_fusion) | copy-start | bytes 6148
  78.0 72.6 %copy-start.9 = (s32[8192]{0:T(1024)}, s32[8192]{0:T(1024)S(1)}, u32[]{:S(2)}) copy-start(s32[8192]{0:T(1024)S(1)} %scatter_custom_fusion) | copy-start | bytes 98308
  150.6 41.6 %copy-start.10 = (f32[8]{0:T(128)S(1)}, f32[8]{0:T(128)}, u32[]{:S(2)}) copy-start(f32[8]{0:T(128)} %param.13) | copy-start | bytes 100
  150.6 41.6 %slice-start = ((f32[512]{0:T(512)}), f32[128]{0:T(128)S(1)}, s32[]{:S(2)}) async-start(f32[512]{0:T(512)} %copy-done.13), calls=%async_computation.1 | async-start | bytes 1024 | tf_op jit(solution)/shard_map/slice | solution.py:83
  187.3 4.9 copy-start.2
  192.2 73.0 %copy-start.14 = (f32[256]{0:T(256)S(1)}, f32[256]{0:T(256)}, u32[]{:S(2)}) copy-start(f32[256]{0:T(256)} %fusion.80) | copy-start | bytes 3076
  350.1 33.4 %copy-start.5 = (s32[4096]{0:T(1024)S(1)}, s32[4096]{0:T(1024)}, u32[]{:S(2)}) copy-start(s32[4096]{0:T(1024)} %broadcast_clamp_fusion) | copy-start | bytes 49156
  350.1 143.5 %copy-start.1 = (f32[64,64]{1,0:T(8,128)S(1)}, f32[64,64]{1,0:T(8,128)}, u32[]{:S(2)}) copy-start(f32[64,64]{1,0:T(8,128)} %param.19) | copy-start | bytes 49156
  383.6 32.3 %copy-start.3 = (f32[4096,32]{0,1:T(8,128)S(1)}, f32[4096,32]{0,1:T(8,128)}, u32[]{:S(2)}) copy-start(f32[4096,32]{0,1:T(8,128)} %copy.29) | copy-start | bytes 1572868
  383.6 32.3 %copy-start.11 = (pred[4096]{0:T(1024)(128)(4,1)S(1)}, pred[4096]{0:T(1024)(128)(4,1)}, u32[]{:S(2)}) copy-start(pred[4096]{0:T(1024)(128)(4,1)} %compare_and_fusion.1) | copy-start | bytes 12292
  383.6 104.5 %copy-start.12 = (s32[1024]{0:T(1024)S(1)}, s32[1024]{0:T(1024)}, u32[]{:S(2)}) copy-start(s32[1024]{0:T(1024)} %fusion.79) | copy-start | bytes 12292
Sparse Core Ops, SparseCore 0:
  420.9 67.1 all-reduce.3

commit v2 on v1

v2 whole, which is shorter than its diff:
```python
import functools
import jax
import jax.numpy as jnp
from jax import lax
from jax.experimental import pallas as pl
from jax.experimental.pallas import tpu as pltpu
from jax.sharding import PartitionSpec as P

NB = 512
NA = 256
NZ = 64
KBLOW = 128
Z_BLOCK = 8


def cosine_table(count):
    freq = jnp.arange(count, dtype=jnp.int32)[:, None]
    cell = jnp.arange(count, dtype=jnp.int32)[None, :]
    phase = (2 * cell + 1) * freq % (4 * count)
    angle = jnp.pi * phase.astype(jnp.float32) / (2.0 * count)
    first = jnp.where(freq == 0, jnp.sqrt(jnp.float32(0.5)), jnp.float32(1.0))
    return jnp.cos(angle) * jnp.sqrt(jnp.float32(2.0 / count)) * first


def slot_targets(owner, owners, capacity):
    onehot = (owner[:, None] == jnp.arange(owners, dtype=jnp.int32)[None, :]).astype(jnp.int32)
    before = jnp.cumsum(onehot, axis=0) - onehot
    slot = jnp.sum(before * onehot, axis=1)
    return owner * capacity + slot


def split_bf16(x):
    hi = x.astype(jnp.bfloat16)
    return hi, (x - hi.astype(jnp.float32)).astype(jnp.bfloat16)


def step_kernel(load_ref, vals_ref, lo_ref, up_ref, rl_ref, ri_ref, pf_ref, ml_ref, mi_ref, tb_ref, out_ref):
    columns = vals_ref.shape[0]
    zb, na, nb = rl_ref.shape
    kb = tb_ref.shape[1]
    rows = zb * na
    rl = rl_ref[...].reshape(rows, nb)
    ri = ri_ref[...].reshape(rows, nb)
    pf = pf_ref[...].reshape(rows, nb)
    mb = ml_ref[...].reshape(rows, nb) != 0
    ma = mi_ref[...].reshape(rows, nb) != 0
    col = lax.broadcasted_iota(jnp.int32, (rows, nb), 1)
    arow = lax.broadcasted_iota(jnp.int32, (zb, na, nb), 1).reshape(rows, nb)
    th, tl = split_bf16(tb_ref[...])

    def per_column(c, carry):
        v = vals_ref[c].reshape(rows, nb).astype(jnp.float32)
        lo = jnp.broadcast_to(lo_ref[c][:, None, :], (zb, na, nb)).reshape(rows, nb)
        up = jnp.broadcast_to(up_ref[c][:, None, :], (zb, na, nb)).reshape(rows, nb)
        fwd_b = jnp.where(col == nb - 1, 0.0, pltpu.roll(v, nb - 1, 1) - v)
        bwd_b = jnp.where(col == 0, 0.0, v - pltpu.roll(v, 1, 1))
        fwd_a = jnp.where(arow == na - 1, up, pltpu.roll(v, rows - 1, 0)) - v
        bwd_a = v - jnp.where(arow == 0, lo, pltpu.roll(v, 1, 0))
        sel_b = jnp.where(mb, fwd_b, -bwd_b)
        sel_a = jnp.where(ma, fwd_a, -bwd_a)
        explicit = v + rl * sel_b + ri * sel_a + load_ref[c] * pf
        hi, low = split_bf16(explicit)
        acc = jnp.dot(low, th, preferred_element_type=jnp.float32)
        acc = acc + jnp.dot(hi, tl, preferred_element_type=jnp.float32)
        acc = acc + jnp.dot(hi, th, preferred_element_type=jnp.float32)
        out_ref[c] = acc.reshape(zb, na, kb)
        return carry

    lax.fori_loop(0, columns, per_column, 0)


def liquid_step(load, vals, lower, upper, rl, ri, pf, ml, mi, tb):
    columns, nz, na, nb = vals.shape
    kb = tb.shape[1]
    zb = min(Z_BLOCK, nz)
    field = pl.BlockSpec((zb, na, nb), lambda j: (j, 0, 0))
    edge = pl.BlockSpec((columns, zb, nb), lambda j: (0, j, 0))
    table = pl.BlockSpec((nb, kb), lambda j: (0, 0))
    return pl.pallas_call(
        step_kernel,
        grid=(nz // zb,),
        in_specs=[
            pl.BlockSpec(memory_space=pltpu.SMEM),
            pl.BlockSpec((columns, zb, na, nb), lambda j: (0, j, 0, 0)),
            edge,
            edge,
            field,
            field,
            field,
            field,
            field,
            table,
        ],
        out_specs=pl.BlockSpec((columns, zb, na, kb), lambda j: (0, j, 0, 0)),
        out_shape=jax.ShapeDtypeStruct((columns, nz, na, kb), jnp.float32),
        compiler_params=pltpu.CompilerParams(vmem_limit_bytes=56 * 1024 * 1024),
    )(load, vals, lower, upper, rl, ri, pf, ml, mi, tb)


def edges(values, axis, dim):
    count = lax.axis_size(axis)
    pos = lax.axis_index(axis)
    ends = count - 1
    head = lax.index_in_dim(values, 0, axis=dim, keepdims=False)
    tail = lax.index_in_dim(values, values.shape[dim] - 1, axis=dim, keepdims=False)
    below = lax.ppermute(tail, axis, [(i, (i + 1) % count) for i in range(ends)])
    above = lax.ppermute(head, axis, [((i + 1) % count, i) for i in range(ends)])
    lower = jnp.where(pos == 0, head, below).astype(jnp.float32)
    upper = jnp.where(pos == ends, tail, above).astype(jnp.float32)
    return lower, upper


def body(
    values_in,
    shock_load,
    price_field,
    rate_liquid,
    rate_illiquid,
    mask_liquid,
    mask_illiquid,
    jump_inverse,
    coef_liquid,
    coef_illiquid,
    coef_income,
    owner,
):
    high = lax.Precision.HIGH
    columns, nz_loc, na_loc, _ = values_in.shape
    wide_pos = lax.axis_index("wide")
    inc_pos = lax.axis_index("inc")
    lower, upper = edges(values_in, "wide", 2)
    liquid_part = liquid_step(
        shock_load, values_in, lower, upper, rate_liquid, rate_illiquid, price_field,
        mask_liquid, mask_illiquid, cosine_table(NB)[:KBLOW].T,
    )
    liquid_part = jnp.transpose(liquid_part, (2, 3, 0, 1)).reshape(na_loc, KBLOW * columns * nz_loc)
    table_a = lax.dynamic_slice_in_dim(cosine_table(NA), wide_pos * na_loc, na_loc, axis=1)
    illiquid_part = jnp.dot(table_a, liquid_part, precision=high)
    rows = illiquid_part.reshape(NA * KBLOW, columns * nz_loc)
    picked = jnp.take(rows, coef_illiquid * KBLOW + coef_liquid, axis=0)
    folded = jnp.dot(cosine_table(NZ), jump_inverse, precision=lax.Precision.HIGHEST)
    folded = lax.dynamic_slice_in_dim(folded, inc_pos * nz_loc, nz_loc, axis=1)
    weight = jnp.take(folded, coef_income, axis=0)
    partial = jnp.sum(picked.reshape(-1, columns, nz_loc) * weight[:, None, :], axis=2)
    kept = lax.psum(partial.T, ("wide", "inc"))
    owners = lax.axis_size(("wide", "inc"))
    count = owner.shape[0]
    capacity = 2 * count // owners
    targets = slot_targets(owner, owners, capacity)
    source = jnp.full((owners * capacity,), count, jnp.int32).at[targets].set(jnp.arange(count, dtype=jnp.int32))
    mine = lax.dynamic_slice_in_dim(source, lax.axis_index(("wide", "inc")) * capacity, capacity)
    gathered = jnp.take(kept, jnp.minimum(mine, count - 1), axis=1)
    return jnp.where((mine < count)[None, :], gathered, jnp.float32(0.0))


def solution(mesh):
    placed = (
        P(("grp", "col"), "inc", "wide", None),
        P(("grp", "col")),
        P(("grp", "inc"), "wide", None),
        P(("grp", "inc"), "wide", None),
        P(("grp", "inc"), "wide", None),
        P(("grp", "inc"), "wide", None),
        P(("grp", "inc"), "wide", None),
        P("grp", None),
        P(),
        P(),
        P(),
        P(),
    )
    return jax.shard_map(
        body,
        mesh=mesh,
        in_specs=placed,
        out_specs=P(("grp", "col"), ("wide", "inc")),
        check_vma=False,
    )
```

time: 502 us -> 323 us (0.64)
  local copies, waits for them, and re-layouts: 222 us -> 126 us
  other arithmetic: 96.1 us -> 23.4 us
  matrix products: 95.4 us -> 28 us
  Pallas kernels: 0 us -> 53.1 us
    dot_general x2 -> x1, matrix products: 95.1 us -> 27.7 us  [body(): illiquid_part = jnp.dot(table_a, liquid_part, precision=high)]
    pallas_call x0 -> x1, Pallas kernels: none -> 53.1 us  [liquid_step(): pl.pallas_call(step_kernel, grid=(nz // zb,), in_specs=[pl.BlockSpec(memo...]
    slice x5 -> x3, local copies, waits for them, and re-layouts: 51.2 us -> 3.58 us  [the longest x1 3.27 us: edges(): lax.index_in_dim(values, values.shape[dim] - 1, axis=dim, keepdims=False)]
    sub x2 -> x0, other arithmetic: 45.2 us -> none  [the longest x1 36.7 us: body(): step_b = center[:, :, :, 1:] - center[:, :, :, :-1]]
    unnamed x33 -> x17, local copies, waits for them, and re-layouts: 32.6 us -> 0.78 us
    convert_element_type x3 -> x2, other arithmetic: 30.8 us -> 2.86 us  [the longest x1 1.93 us: edges(): upper = jnp.where(pos == ends, tail, above).astype(jnp.float32)]
    transpose x1, local copies, waits for them, and re-layouts: 31.1 us -> 16.2 us  [body(): jnp.transpose(liquid_part, (2, 3, 0, 1))]
  transfers between devices with their start and end apart: 3 -> 3, of which waited for: 1 -> 2; matrix products, arithmetic and copies ran while one was open for 13% -> 15% of each run, Pallas kernels for 0% -> 0%
where the time goes in v2:
time: 323 us; the launch traced here: 321 us
  local copies, waits for them, and re-layouts  126 us (39%)
  waiting for transfers between devices  70 us (22%)
  Pallas kernels  53.1 us (16%)
  matrix products  28 us (9%)
  other arithmetic  23.4 us (7%)
  between operations  13.6 us (4%)
  starting transfers between devices  7.54 us (2%)
    psum x1, waiting for transfers between devices, body(): kept = lax.psum(partial.T, ('wide', 'inc'))  68 us
    pallas_call x1, Pallas kernels, liquid_step(): pl.pallas_call(step_kernel, grid=(nz // zb,), in_specs=[pl.BlockSpec(memo...  53.1 us
    reshape x1, local copies, waits for them, and re-layouts, body(): rows = illiquid_part.reshape(NA * KBLOW, columns * nz_loc)  35.4 us
    gather x2, local copies, waits for them, and re-layouts, body(): picked = jnp.take(rows, coef_illiquid * KBLOW + coef_liquid, axis=0)  32.3 us
    dot_general x1, matrix products, body(): illiquid_part = jnp.dot(table_a, liquid_part, precision=high)  27.7 us
    transpose x1, local copies, waits for them, and re-layouts, body(): jnp.transpose(liquid_part, (2, 3, 0, 1))  16.2 us
    scatter x1, local copies, waits for them, and re-layouts, body(): jnp.full((owners * capacity,), count, jnp.int32).at[targets]  15.7 us
    gather x1, local copies, waits for them, and re-layouts, body(): weight = jnp.take(folded, coef_income, axis=0)  14.1 us
  transfers between devices with their start and end apart: 3, of which 2 were waited for; matrix products, arithmetic and copies ran while one was open for 15% of the time, Pallas kernels for 0%

profile of v2, /device:TPU:0, one launch (start us, length us, event | category | flops | bytes accessed | tf_op | source)
XLA Modules:
  0.0 321.4 jit_solution(8911435799648007932)
XLA Ops:
  6.5 3.3 %fusion.53 = (bf16[8,32,1,512]{3,2,1,0:T(2,128)(2,1)S(1)}, bf16[8,32,1,512]{3,2,1,0:T(2,128)(2,1)S(1)}) fusion(bf16[8,32,64,512]{3,2,1,0:T(8,128)(2,1)} %vals_ref.1), kind=kLoop, calls=%fused_computation.97 | loop fusion | bytes 1048576 | tf_op jit(solution)/shard_map/slice | solution.py:105
  10.6 1.3 collective-permute-start.1
  15.0 1.3 compare_and_fusion.1
  16.3 1.3 negate_select_fusion
  18.0 2.3 reduce-window.6
  21.7 14.1 %gather_fusion.1 = f32[4096,32]{1,0:T(8,128)} fusion(f32[64,32]{1,0:T(8,128)S(1)} %copy.28, s32[4096]{0:T(1024)S(1)} %fusion.42), kind=kCustom, calls=%fused_computation.1 | custom fusion | bytes 1064960 | tf_op jit(solution)/shard_map/jit(_take)/gather | solution.py:143
  35.8 3.6 %broadcast_select_fusion = f32[4096,32]{1,0:T(8,128)S(1)} fusion(f32[4096,32]{1,0:T(8,128)} %gather_fusion.1, pred[4096]{0:T(1024)(128)(4,1)S(1)} %compare_and_fusion), kind=kLoop, calls=%fused_computation.8 | loop fusion | flops 131072 | bytes 1052672 | tf_op jit(solution)/shard_map/jit(_take)/select_n | solution.py:143
  39.4 15.7 %scatter_custom_fusion = s32[8192]{0:T(1024)S(1)} fusion(s32[4096]{0:T(1024)} %compare_select_fusion.2, s32[4096]{0:T(1024)S(1)} %iota.47, s32[]{:T(128)} %constant.66.clone.1), kind=kCustom, calls=%fused_computation.70 | custom fusion | bytes 33280 | tf_op jit(solution)/shard_map/scatter | solution.py:150
  55.7 1.4 broadcast_compare_fusion.1
  57.1 1.9 select_convert_fusion
  59.0 6.3 %collective-permute-start = (bf16[8,32,512]{2,1,0:T(8,128)(2,1)}, bf16[8,32,512]{2,1,0:T(8,128)(2,1)}, u32[]{:S(2)}, u32[]{:S(2)}) collective-permute-start(bf16[8,32,512]{2,1,0:T(8,128)(2,1)} %get-tuple-element.6), channel_id=1, source_target_pairs={{0,4},{4,8},{8,12},{1,5},{5,9},{9,13},{2,6},{6,10},{10,14},{3,7},{... | collective-permute-start | bytes 786440 | tf_op jit(solution)/shard_map/ppermute | solution.py:106
  65.9 2.6 fusion.6.tb_ref
  68.5 2.0 collective-permute-done
  70.4 0.9 select_convert_fusion.1.lo_ref
  71.4 53.1 %shard_map.118 = f32[8,32,64,128]{3,2,1,0:T(8,128)} custom-call(f32[8]{0:T(128)} %load_ref.1, bf16[8,32,64,512]{3,2,1,0:T(8,128)(2,1)} %vals_ref.1, f32[8,32,512]{2,1,0:T(8,128)} %select_convert_fusion.1.lo_ref, f32[8,32,512]{2,1,0:T(8,128)} %get-tuple-element.5.up_ref, f32[32,64,512]{2,1,0:T(8,128)} %rl_ref.1, f32[32,64,512]{2,1,0:T(8,128)} %ri_ref.1, ...), custom_call_target="tpu_custom_call" | custom-call | tf_op jit(solution)/shard_map/pallas_call | solution.py:79
  124.5 16.2 %copy.26 = f32[64,128,8,32]{0,3,2,1:T(8,128)} copy(f32[64,128,8,32]{1,0,3,2:T(8,128)} %bitcast.40) | data formatting | bytes 16777216 | tf_op jit(solution)/shard_map/transpose | solution.py:136
  140.7 27.7 %fusion.11 = f32[256,32768]{1,0:T(8,128)} fusion(f32[64,32768]{0,1:T(8,128)} %bitcast.39, s32[256,256]{1,0:T(8,128)S(1)} %negate_select_fusion.2, s32[]{:T(128)S(6)} %select_n.113, pred[256,256]{1,0:T(32,128)(4,1)S(1)} %copy-done.3, pred[256,256]{1,0:T(32,128)(4,1)S(1)} %get-tuple-element.13, f32[256]{0:T(256)S(1)} %fusion.44), kind=kOutput, calls=%fused_computation.31 | convolution fusion | flops 3221323776 | bytes 42140676 | tf_op jit(solution)/shard_map/dot_general | solution.py:138
  168.5 35.4 %reshape.102 = f32[32768,256]{1,0:T(8,128)} reshape(f32[256,32768]{1,0:T(8,128)} %fusion.11) | data formatting | bytes 67108864 | tf_op jit(solution)/shard_map/reshape | solution.py:139
  203.9 26.6 %gather_fusion = f32[4096,256]{1,0:T(8,128)} fusion(f32[32768,256]{1,0:T(8,128)} %reshape.102, s32[4096]{0:T(1024)S(1)} %broadcast_clamp_fusion), kind=kCustom, calls=%fused_computation | custom fusion | bytes 8404992 | tf_op jit(solution)/shard_map/jit(_take)/gather | solution.py:140
  230.5 5.6 %copy.27 = f32[4096,256]{0,1:T(8,128)} copy(f32[4096,256]{1,0:T(8,128)} %gather_fusion) | data formatting | bytes 8388608 | tf_op jit(solution)/shard_map/jit(_take)/gather | solution.py:140
  236.2 2.9 multiply_reduce_fusion
  239.1 1.9 copy.30
  241.0 68.0 %all-reduce.2.cloned.1.call-done = f32[8,4096]{0,1:T(8,128)} async-done(((f32[8,4096]{0,1:T(8,128)}), f32[8,4096]{0,1:T(8,128)}) %all-reduce.2.cloned.1.call-update) | async-done | bytes 131088 | tf_op jit(solution)/shard_map/psum | solution.py:145
  309.1 4.4 %gather_fusion.2 = f32[1024,8]{1,0:T(8,128)S(1)} fusion(f32[8,4096]{0,1:T(8,128)} %all-reduce.2.cloned.1.call-done, s32[1024]{0:T(1024)S(1)} %copy-done.6), kind=kCustom, calls=%fused_computation.2 | custom fusion | bytes 69632 | tf_op jit(solution)/shard_map/jit(_take)/gather | solution.py:152
  (47 shorter events, 7.9 us)
Async XLA Ops:
  6.5 11.1 %copy-start = (f32[64,64]{1,0:T(8,128)S(1)}, f32[64,64]{1,0:T(8,128)}, u32[]{:S(2)}) copy-start(f32[64,64]{1,0:T(8,128)} %param.19) | copy-start | bytes 49156
  6.5 11.5 %copy-start.2 = (s32[4096]{0:T(1024)S(1)}, s32[4096]{0:T(1024)}, u32[]{:S(2)}) copy-start(s32[4096]{0:T(1024)} %param.23) | copy-start | bytes 49156
  6.5 302.5 %all-reduce.2.cloned.1.call-start = ((), (), s32[]{:S(2)}) async-start(), calls=%async_computation | async-start | bytes 4194304 | tf_op jit(solution)/shard_map/psum | solution.py:145
  10.6 46.5 %collective-permute-start.1 = (bf16[8,32,512]{2,1,0:T(8,128)(2,1)}, bf16[8,32,512]{2,1,0:T(8,128)(2,1)}, u32[]{:S(2)}, u32[]{:S(2)}) collective-permute-start(bf16[8,32,512]{2,1,0:T(8,128)(2,1)} %bitcast.37), channel_id=1, source_target_pairs={{4,0},{8,4},{12,8},{5,1},{9,5},{13,9},{6,2},{10,6},{14,10},{7,3},{... | collective-permute-start | bytes 786440 | tf_op jit(solution)/shard_map/ppermute | solution.py:107
  11.9 9.0 %copy-start.4 = (s32[512]{0:T(512)}, s32[512]{0:T(512)S(1)}, u32[]{:S(2)}) copy-start(s32[512]{0:T(512)S(1)} %multiply_add_fusion) | copy-start | bytes 6148
  35.8 19.9 %copy-start.5 = (s32[512]{0:T(512)S(1)}, s32[512]{0:T(512)}, u32[]{:S(2)}) copy-start(s32[512]{0:T(512)} %copy-done.4) | copy-start | bytes 6148
  59.0 11.4 %collective-permute-start = (bf16[8,32,512]{2,1,0:T(8,128)(2,1)}, bf16[8,32,512]{2,1,0:T(8,128)(2,1)}, u32[]{:S(2)}, u32[]{:S(2)}) collective-permute-start(bf16[8,32,512]{2,1,0:T(8,128)(2,1)} %get-tuple-element.6), channel_id=1, source_target_pairs={{0,4},{4,8},{8,12},{1,5},{5,9},{9,13},{2,6},{6,10},{10,14},{3,7},{... | collective-permute-start | bytes 786440 | tf_op jit(solution)/shard_map/ppermute | solution.py:106
  124.5 16.2 %copy-start.3 = (pred[256,256]{1,0:T(32,128)(4,1)S(1)}, pred[256,256]{1,0:T(32,128)(4,1)}, u32[]{:S(2)}) copy-start(pred[256,256]{1,0:T(32,128)(4,1)} %get-tuple-element.14) | copy-start | bytes 196612
  230.5 5.7 %copy-start.7 = (pred[4096]{0:T(1024)(128)(4,1)S(1)}, pred[4096]{0:T(1024)(128)(4,1)}, u32[]{:S(2)}) copy-start(pred[4096]{0:T(1024)(128)(4,1)} %compare_and_fusion.1) | copy-start | bytes 12292
  236.2 72.9 %copy-start.6 = (s32[1024]{0:T(1024)S(1)}, s32[1024]{0:T(1024)}, u32[]{:S(2)}) copy-start(s32[1024]{0:T(1024)} %fusion.43) | copy-start | bytes 12292
  236.2 78.4 %copy-start.1 = (f32[64,64]{1,0:T(8,128)S(1)}, f32[64,64]{1,0:T(8,128)}, u32[]{:S(2)}) copy-start(f32[64,64]{1,0:T(8,128)} %param.19) | copy-start | bytes 49156
Sparse Core Ops, SparseCore 0:
  241.1 67.8 all-reduce.1

commit v3 on v2

--- a/solution.py
+++ b/solution.py
@@ -133,24 +133,36 @@
         shock_load, values_in, lower, upper, rate_liquid, rate_illiquid, price_field,
         mask_liquid, mask_illiquid, cosine_table(NB)[:KBLOW].T,
     )
-    liquid_part = jnp.transpose(liquid_part, (2, 3, 0, 1)).reshape(na_loc, KBLOW * columns * nz_loc)
+    liquid_part = jnp.transpose(liquid_part, (3, 2, 0, 1)).reshape(KBLOW, na_loc, columns * nz_loc)
     table_a = lax.dynamic_slice_in_dim(cosine_table(NA), wide_pos * na_loc, na_loc, axis=1)
-    illiquid_part = jnp.dot(table_a, liquid_part, precision=high)
-    rows = illiquid_part.reshape(NA * KBLOW, columns * nz_loc)
-    picked = jnp.take(rows, coef_illiquid * KBLOW + coef_liquid, axis=0)
+    illiquid_part = jnp.einsum("ja,kac->kjc", table_a, liquid_part, precision=high)
+    rows = illiquid_part.reshape(KBLOW * NA, columns * nz_loc)
+    picked = jnp.take(rows, coef_liquid * NA + coef_illiquid, axis=0)
     folded = jnp.dot(cosine_table(NZ), jump_inverse, precision=lax.Precision.HIGHEST)
     folded = lax.dynamic_slice_in_dim(folded, inc_pos * nz_loc, nz_loc, axis=1)
-    weight = jnp.take(folded, coef_income, axis=0)
+    pick_z = (coef_income[:, None] == jnp.arange(NZ, dtype=jnp.int32)[None, :]).astype(jnp.float32)
+    weight = jnp.dot(pick_z, folded, precision=lax.Precision.HIGHEST)
     partial = jnp.sum(picked.reshape(-1, columns, nz_loc) * weight[:, None, :], axis=2)
-    kept = lax.psum(partial.T, ("wide", "inc"))
+    kept = all_sum(partial.T, ("inc", "wide"))
     owners = lax.axis_size(("wide", "inc"))
     count = owner.shape[0]
     capacity = 2 * count // owners
-    targets = slot_targets(owner, owners, capacity)
-    source = jnp.full((owners * capacity,), count, jnp.int32).at[targets].set(jnp.arange(count, dtype=jnp.int32))
-    mine = lax.dynamic_slice_in_dim(source, lax.axis_index(("wide", "inc")) * capacity, capacity)
+    me = lax.axis_index(("wide", "inc"))
+    seen = jnp.cumsum((owner == me).astype(jnp.int32))
+    slots = jnp.arange(1, capacity + 1, dtype=jnp.int32)
+    mine = jnp.sum((seen[None, :] < slots[:, None]).astype(jnp.int32), axis=1)
     gathered = jnp.take(kept, jnp.minimum(mine, count - 1), axis=1)
     return jnp.where((mine < count)[None, :], gathered, jnp.float32(0.0))
+
+
+def all_sum(x, axes):
+    for axis in axes:
+        count = lax.axis_size(axis)
+        step = 1
+        while step < count:
+            x = x + lax.ppermute(x, axis, [(i, i ^ step) for i in range(count)])
+            step *= 2
+    return x
 
 
 def solution(mesh):

time: 323 us -> 169 us (0.52)
  local copies, waits for them, and re-layouts: 126 us -> 49.9 us
  waiting for transfers between devices: 70 us -> 17.1 us
  between operations: 13.6 us -> 0.26 us
  other arithmetic: 23.4 us -> 13.4 us
  matrix products: 28 us -> 23.8 us
    psum x1 -> x0, waiting for transfers between devices: 68 us -> none  [body(): kept = lax.psum(partial.T, ('wide', 'inc'))]
    reshape x1, local copies, waits for them, and re-layouts: 35.4 us -> 9.25 us  [body(): jnp.transpose(liquid_part, (3, 2, 0, 1))]
    transpose x1 -> x0, local copies, waits for them, and re-layouts: 16.2 us -> none  [body(): jnp.transpose(liquid_part, (2, 3, 0, 1))]
    scatter x1 -> x0, local copies, waits for them, and re-layouts: 15.7 us -> none  [body(): jnp.full((owners * capacity,), count, jnp.int32).at[targets]]
    gather x3 -> x2, local copies, waits for them, and re-layouts: 46.3 us -> 32.2 us  [body(): picked = jnp.take(rows, coef_liquid * NA + coef_illiquid, axis=0)]
    ppermute x0 -> x3, waiting for transfers between devices: none -> 11 us  [all_sum(): x = x + lax.ppermute(x, axis, [(i, i ^ step) for i in range(count)])]
    ppermute x0 -> x3, starting transfers between devices: none -> 5.49 us  [all_sum(): x = x + lax.ppermute(x, axis, [(i, i ^ step) for i in range(count)])]
    select_n x2 -> x1, other arithmetic: 4.22 us -> 0.01 us  [body(): gathered = jnp.take(kept, jnp.minimum(mine, count - 1), axis=1)]
  transfers between devices with their start and end apart: 3 -> 5, of which waited for: 2 -> 5; matrix products, arithmetic and copies ran while one was open for 15% -> 5% of each run, Pallas kernels for 0% -> 0%
where the time goes in v3:
time: 169 us; the launch traced here: 168 us
  Pallas kernels  53.1 us (31%)
  local copies, waits for them, and re-layouts  49.9 us (30%)
  matrix products  23.8 us (14%)
  waiting for transfers between devices  17.1 us (10%)
  other arithmetic  13.4 us (8%)
  starting transfers between devices  10.4 us (6%)
    pallas_call x1, Pallas kernels, liquid_step(): pl.pallas_call(step_kernel, grid=(nz // zb,), in_specs=[pl.BlockSpec(memo...  53.1 us
    gather x2, local copies, waits for them, and re-layouts, body(): picked = jnp.take(rows, coef_liquid * NA + coef_illiquid, axis=0)  32.2 us
    dot_general x1, matrix products, body(): jnp.einsum('ja,kac->kjc', table_a, liquid_part, precision=high)  22.1 us
    ppermute x3, waiting for transfers between devices, all_sum(): x = x + lax.ppermute(x, axis, [(i, i ^ step) for i in range(count)])  11 us
    reshape x1, local copies, waits for them, and re-layouts, body(): jnp.transpose(liquid_part, (3, 2, 0, 1))  9.25 us
    ppermute x3, starting transfers between devices, all_sum(): x = x + lax.ppermute(x, axis, [(i, i ^ step) for i in range(count)])  5.49 us
    ppermute x1, starting transfers between devices, edges(): lax.ppermute(tail, axis, [(i, (i + 1) % count) for i in range(ends)])  3.64 us
    ppermute x1, waiting for transfers between devices, edges(): lax.ppermute(tail, axis, [(i, (i + 1) % count) for i in range(ends)])  3.55 us
  transfers between devices with their start and end apart: 5, of which 5 were waited for; matrix products, arithmetic and copies ran while one was open for 5% of the time, Pallas kernels for 0%

profile of v3, /device:TPU:0, one launch (start us, length us, event | category | flops | bytes accessed | tf_op | source)
XLA Modules:
  0.0 168.0 jit_solution(12684836343744479686)
XLA Ops:
  0.0 3.3 %fusion.50 = (bf16[8,32,1,512]{3,2,1,0:T(2,128)(2,1)S(1)}, bf16[8,32,1,512]{3,2,1,0:T(2,128)(2,1)S(1)}) fusion(bf16[8,32,64,512]{3,2,1,0:T(8,128)(2,1)} %vals_ref.1), kind=kLoop, calls=%fused_computation.92 | loop fusion | bytes 1048576 | tf_op jit(solution)/shard_map/slice | solution.py:105
  4.0 1.3 collective-permute-start.1
  5.3 0.8 broadcast_compare_fusion.3
  8.8 1.8 %convert_reduce_fusion = s32[1024]{0:T(1024)S(1)} fusion(s32[4096]{0:T(1024)S(1)} %add_bitcast_fusion, s32[1024]{0:T(1024)S(1)} %iota_add_fusion), kind=kLoop, calls=%fused_computation.2 | loop fusion | flops 12581888 | bytes 24576 | tf_op jit(solution)/shard_map/reduce_sum | solution.py:153
  10.9 1.4 fusion
  13.0 2.6 %collective-permute-done.1 = bf16[8,32,512]{2,1,0:T(8,128)(2,1)} collective-permute-done((bf16[8,32,512]{2,1,0:T(8,128)(2,1)}, bf16[8,32,512]{2,1,0:T(8,128)(2,1)}, u32[]{:S(2)}, u32[]{:S(2)}) %collective-permute-start.1) | collective-permute-done | bytes 262176 | tf_op jit(solution)/shard_map/ppermute | solution.py:107
  15.6 1.9 %select_convert_fusion = (f32[8,32,512]{2,1,0:T(8,128)}, bf16[8,32,512]{2,1,0:T(8,128)(2,1)}) fusion(bf16[8,32,512]{2,1,0:T(8,128)(2,1)} %collective-permute-done.1, pred[]{:T(512)S(6)} %eq.67, bf16[8,32,1,512]{3,2,1,0:T(2,128)(2,1)S(1)} %get-tuple-element.7), kind=kLoop, calls=%fused_computation.24 | loop fusion | flops 262144 | bytes 1310721 | tf_op jit(solution)/shard_map/convert_element_type | solution.py:109
  17.5 3.6 %collective-permute-start = (bf16[8,32,512]{2,1,0:T(8,128)(2,1)}, bf16[8,32,512]{2,1,0:T(8,128)(2,1)S(1)}, u32[]{:S(2)}, u32[]{:S(2)}) collective-permute-start(bf16[8,32,512]{2,1,0:T(8,128)(2,1)} %get-tuple-element.6), channel_id=1, source_target_pairs={{0,4},{4,8},{8,12},{1,5},{5,9},{9,13},{2,6},{6,10},{10,14},{3,7},{... | collective-permute-start | bytes 786440 | tf_op jit(solution)/shard_map/ppermute | solution.py:106
  21.2 1.6 fusion.7.tb_ref
  22.8 3.5 %collective-permute-done = bf16[8,32,512]{2,1,0:T(8,128)(2,1)S(1)} collective-permute-done((bf16[8,32,512]{2,1,0:T(8,128)(2,1)}, bf16[8,32,512]{2,1,0:T(8,128)(2,1)S(1)}, u32[]{:S(2)}, u32[]{:S(2)}) %collective-permute-start) | collective-permute-done | bytes 262176 | tf_op jit(solution)/shard_map/ppermute | solution.py:106
  26.4 0.9 select_convert_fusion.1.lo_ref
  27.3 53.1 %shard_map.118 = f32[8,32,64,128]{3,2,1,0:T(8,128)} custom-call(f32[8]{0:T(128)} %load_ref.1, bf16[8,32,64,512]{3,2,1,0:T(8,128)(2,1)} %vals_ref.1, f32[8,32,512]{2,1,0:T(8,128)} %select_convert_fusion.1.lo_ref, f32[8,32,512]{2,1,0:T(8,128)} %get-tuple-element.5.up_ref, f32[32,64,512]{2,1,0:T(8,128)} %rl_ref.1, f32[32,64,512]{2,1,0:T(8,128)} %ri_ref.1, ...), custom_call_target="tpu_custom_call" | custom-call | tf_op jit(solution)/shard_map/pallas_call | solution.py:79
  80.4 9.3 %copy.49 = f32[128,64,256]{2,1,0:T(8,128)} copy(f32[128,64,256]{0,1,2:T(8,128)} %bitcast.34) | data formatting | bytes 16777216 | tf_op jit(solution)/shard_map/reshape | solution.py:136
  89.7 22.1 %fusion.14 = f32[128,256,256]{1,2,0:T(8,128)} fusion(f32[128,64,256]{2,1,0:T(8,128)} %copy.49, s32[256,256]{0,1:T(8,128)S(1)} %negate_select_fusion.2, s32[]{:T(128)S(6)} %select_n.110, pred[256,256]{0,1:T(32,128)(4,1)} %get-tuple-element.14, pred[256,256]{0,1:T(32,128)(4,1)S(1)} %get-tuple-element.13, f32[256]{0:T(256)S(1)} %fusion.40), kind=kOutput, calls=%fused_computation.35 | convolution fusion | flops 3221323776 | bytes 42042372 | tf_op jit(solution)/shard_map/ja,kac->kjc/dot_general | solution.py:138
  111.7 26.6 %gather_fusion = f32[4096,256]{1,0:T(8,128)} fusion(f32[32768,256]{1,0:T(8,128)} %bitcast.33, s32[4096]{0:T(1024)S(1)} %broadcast_clamp_fusion), kind=kCustom, calls=%fused_computation | custom fusion | bytes 8404992 | tf_op jit(solution)/shard_map/jit(_take)/gather | solution.py:140
  138.4 5.6 %copy.50 = f32[4096,256]{0,1:T(8,128)} copy(f32[4096,256]{1,0:T(8,128)} %gather_fusion) | data formatting | bytes 8388608 | tf_op jit(solution)/shard_map/jit(_take)/gather | solution.py:140
  144.0 2.9 %multiply_reduce_fusion = f32[4096,8]{0,1:T(8,128)S(1)} fusion(f32[4096,32]{0,1:T(8,128)S(1)} %fusion, pred[4096]{0:T(1024)(128)(4,1)S(1)} %compare_and_fusion, f32[4096,256]{0,1:T(8,128)} %copy.50), kind=kLoop, calls=%fused_computation.3 | loop fusion | flops 3112960 | bytes 4853760 | tf_op jit(solution)/shard_map/reduce_sum | solution.py:145
  147.0 1.3 collective-permute-done.2
  148.3 2.4 %collective-permute-start.3 = (f32[8,4096]{1,0:T(8,128)S(1)}, f32[8,4096]{1,0:T(8,128)S(1)}, u32[]{:S(2)}, u32[]{:S(2)}) collective-permute-start(f32[8,4096]{1,0:T(8,128)S(1)} %bitcast_add_fusion), channel_id=1, source_target_pairs={{0,4},{4,0},{8,12},{12,8},{1,5},{5,1},{9,13},{13,9},{2,6},{6,2},{1... | collective-permute-start | bytes 393224 | tf_op jit(solution)/shard_map/ppermute | solution.py:163
  150.8 3.8 %collective-permute-done.3 = f32[8,4096]{1,0:T(8,128)S(1)} collective-permute-done((f32[8,4096]{1,0:T(8,128)S(1)}, f32[8,4096]{1,0:T(8,128)S(1)}, u32[]{:S(2)}, u32[]{:S(2)}) %collective-permute-start.3) | collective-permute-done | bytes 131104 | tf_op jit(solution)/shard_map/ppermute | solution.py:163
  154.6 3.0 %collective-permute-start.4 = (f32[8,4096]{1,0:T(8,128)S(1)}, f32[8,4096]{1,0:T(8,128)S(1)}, u32[]{:S(2)}, u32[]{:S(2)}) collective-permute-start(f32[8,4096]{1,0:T(8,128)S(1)} %add.126), channel_id=1, source_target_pairs={{0,8},{4,12},{8,0},{12,4},{1,9},{5,13},{9,1},{13,5},{2,10},{6,14},... | collective-permute-start | bytes 393224 | tf_op jit(solution)/shard_map/ppermute | solution.py:163
  157.6 5.8 %collective-permute-done.4 = f32[8,4096]{1,0:T(8,128)S(1)} collective-permute-done((f32[8,4096]{1,0:T(8,128)S(1)}, f32[8,4096]{1,0:T(8,128)S(1)}, u32[]{:S(2)}, u32[]{:S(2)}) %collective-permute-start.4) | collective-permute-done | bytes 131104 | tf_op jit(solution)/shard_map/ppermute | solution.py:163
  164.0 2.8 %gather_fusion.1 = f32[1024,8]{1,0:T(8,128)S(1)} fusion(f32[8,4096]{0,1:T(8,128)S(1)} %copy.51, s32[1024]{0:T(1024)S(1)} %broadcast_clamp_fusion.1), kind=kCustom, calls=%fused_computation.1 | custom fusion | bytes 69632 | tf_op jit(solution)/shard_map/jit(_take)/gather | solution.py:154
  167.2 0.8 copy.52
  (39 shorter events, 5.3 us)
Async XLA Ops:
  0.0 10.6 %copy-start = (f32[64,64]{1,0:T(8,128)S(1)}, f32[64,64]{1,0:T(8,128)}, u32[]{:S(2)}) copy-start(f32[64,64]{1,0:T(8,128)} %param.19) | copy-start | bytes 49156
  0.0 8.2 %copy-start.2 = (s32[4096]{0:T(1024)S(1)}, s32[4096]{0:T(1024)}, u32[]{:S(2)}) copy-start(s32[4096]{0:T(1024)} %param.23) | copy-start | bytes 49156
  0.0 10.9 %copy-start.3 = (s32[4096]{0:T(1024)S(1)}, s32[4096]{0:T(1024)}, u32[]{:S(2)}) copy-start(s32[4096]{0:T(1024)} %param.22) | copy-start | bytes 49156
  4.0 11.6 %collective-permute-start.1 = (bf16[8,32,512]{2,1,0:T(8,128)(2,1)}, bf16[8,32,512]{2,1,0:T(8,128)(2,1)}, u32[]{:S(2)}, u32[]{:S(2)}) collective-permute-start(bf16[8,32,512]{2,1,0:T(8,128)(2,1)} %bitcast.32), channel_id=1, source_target_pairs={{4,0},{8,4},{12,8},{5,1},{9,5},{13,9},{6,2},{10,6},{14,10},{7,3},{... | collective-permute-start | bytes 786440 | tf_op jit(solution)/shard_map/ppermute | solution.py:107
  17.5 8.8 %collective-permute-start = (bf16[8,32,512]{2,1,0:T(8,128)(2,1)}, bf16[8,32,512]{2,1,0:T(8,128)(2,1)S(1)}, u32[]{:S(2)}, u32[]{:S(2)}) collective-permute-start(bf16[8,32,512]{2,1,0:T(8,128)(2,1)} %get-tuple-element.6), channel_id=1, source_target_pairs={{0,4},{4,8},{8,12},{1,5},{5,9},{9,13},{2,6},{6,10},{10,14},{3,7},{... | collective-permute-start | bytes 786440 | tf_op jit(solution)/shard_map/ppermute | solution.py:106
  138.4 29.6 %copy-start.1 = (f32[64,64]{1,0:T(8,128)S(1)}, f32[64,64]{1,0:T(8,128)}, u32[]{:S(2)}) copy-start(f32[64,64]{1,0:T(8,128)} %param.19) | copy-start | bytes 49156
  146.9 1.4 collective-permute-start.2
  148.3 6.3 %collective-permute-start.3 = (f32[8,4096]{1,0:T(8,128)S(1)}, f32[8,4096]{1,0:T(8,128)S(1)}, u32[]{:S(2)}, u32[]{:S(2)}) collective-permute-start(f32[8,4096]{1,0:T(8,128)S(1)} %bitcast_add_fusion), channel_id=1, source_target_pairs={{0,4},{4,0},{8,12},{12,8},{1,5},{5,1},{9,13},{13,9},{2,6},{6,2},{1... | collective-permute-start | bytes 393224 | tf_op jit(solution)/shard_map/ppermute | solution.py:163
  154.6 8.8 %collective-permute-start.4 = (f32[8,4096]{1,0:T(8,128)S(1)}, f32[8,4096]{1,0:T(8,128)S(1)}, u32[]{:S(2)}, u32[]{:S(2)}) collective-permute-start(f32[8,4096]{1,0:T(8,128)S(1)} %add.126), channel_id=1, source_target_pairs={{0,8},{4,12},{8,0},{12,4},{1,9},{5,13},{9,1},{13,5},{2,10},{6,14},... | collective-permute-start | bytes 393224 | tf_op jit(solution)/shard_map/ppermute | solution.py:163

commit v4 on v3

--- a/solution.py
+++ b/solution.py
@@ -95,6 +95,31 @@
         out_shape=jax.ShapeDtypeStruct((columns, nz, na, kb), jnp.float32),
         compiler_params=pltpu.CompilerParams(vmem_limit_bytes=56 * 1024 * 1024),
     )(load, vals, lower, upper, rl, ri, pf, ml, mi, tb)
+
+
+def illiquid_kernel(ca_ref, t_ref, out_ref):
+    ch, cl = split_bf16(ca_ref[...])
+    for k in range(t_ref.shape[0]):
+        th, tl = split_bf16(t_ref[k])
+        acc = jnp.dot(cl, th, preferred_element_type=jnp.float32)
+        acc = acc + jnp.dot(ch, tl, preferred_element_type=jnp.float32)
+        out_ref[k] = acc + jnp.dot(ch, th, preferred_element_type=jnp.float32)
+
+
+def illiquid_step(ca, t):
+    kb, na_loc, lanes = t.shape
+    na = ca.shape[0]
+    block = 8
+    return pl.pallas_call(
+        illiquid_kernel,
+        grid=(kb // block,),
+        in_specs=[
+            pl.BlockSpec((na, na_loc), lambda j: (0, 0)),
+            pl.BlockSpec((block, na_loc, lanes), lambda j: (j, 0, 0)),
+        ],
+        out_specs=pl.BlockSpec((block, na, lanes), lambda j: (j, 0, 0)),
+        out_shape=jax.ShapeDtypeStruct((kb, na, lanes), jnp.float32),
+    )(ca, t)
 
 
 def edges(values, axis, dim):
@@ -135,7 +160,7 @@
     )
     liquid_part = jnp.transpose(liquid_part, (3, 2, 0, 1)).reshape(KBLOW, na_loc, columns * nz_loc)
     table_a = lax.dynamic_slice_in_dim(cosine_table(NA), wide_pos * na_loc, na_loc, axis=1)
-    illiquid_part = jnp.einsum("ja,kac->kjc", table_a, liquid_part, precision=high)
+    illiquid_part = illiquid_step(table_a, liquid_part)
     rows = illiquid_part.reshape(KBLOW * NA, columns * nz_loc)
     picked = jnp.take(rows, coef_liquid * NA + coef_illiquid, axis=0)
     folded = jnp.dot(cosine_table(NZ), jump_inverse, precision=lax.Precision.HIGHEST)

time: 169 us -> 169 us (level)
  Pallas kernels: 53.1 us -> 75.2 us
  matrix products: 23.8 us -> 1.77 us
    pallas_call x0 -> x1, Pallas kernels: none -> 22.1 us  [illiquid_step(): pl.pallas_call(illiquid_kernel, grid=(kb // block,), in_specs=[pl.BlockSp...]
    dot_general x1 -> x0, matrix products: 22.1 us -> none  [body(): jnp.einsum('ja,kac->kjc', table_a, liquid_part, precision=high)]
  transfers between devices with their start and end apart: 5 -> 5, of which waited for: 5 -> 5; matrix products, arithmetic and copies ran while one was open for 5% -> 6% of each run, Pallas kernels for 0% -> 0%
where the time goes in v4:
time: 169 us; the launch traced here: 168 us
  Pallas kernels  75.2 us (44%)
  local copies, waits for them, and re-layouts  49.2 us (29%)
  waiting for transfers between devices  16.6 us (10%)
  other arithmetic  13.8 us (8%)
  starting transfers between devices  10.8 us (6%)
  matrix products  1.77 us (1%)
    pallas_call x1, Pallas kernels, liquid_step(): pl.pallas_call(step_kernel, grid=(nz // zb,), in_specs=[pl.BlockSpec(memo...  53.1 us
    gather x2, local copies, waits for them, and re-layouts, body(): picked = jnp.take(rows, coef_liquid * NA + coef_illiquid, axis=0)  32.2 us
    pallas_call x1, Pallas kernels, illiquid_step(): pl.pallas_call(illiquid_kernel, grid=(kb // block,), in_specs=[pl.BlockSp...  22.1 us
    ppermute x3, waiting for transfers between devices, all_sum(): x = x + lax.ppermute(x, axis, [(i, i ^ step) for i in range(count)])  11 us
    reshape x1, local copies, waits for them, and re-layouts, body(): jnp.transpose(liquid_part, (3, 2, 0, 1))  9.25 us
    ppermute x3, starting transfers between devices, all_sum(): x = x + lax.ppermute(x, axis, [(i, i ^ step) for i in range(count)])  5.59 us
    ppermute x1, starting transfers between devices, edges(): lax.ppermute(tail, axis, [(i, (i + 1) % count) for i in range(ends)])  3.9 us
    ppermute x1, waiting for transfers between devices, edges(): lax.ppermute(tail, axis, [(i, (i + 1) % count) for i in range(ends)])  3.7 us
  transfers between devices with their start and end apart: 5, of which 5 were waited for; matrix products, arithmetic and copies ran while one was open for 6% of the time, Pallas kernels for 0%

profile of v4, /device:TPU:0, one launch (start us, length us, event | category | flops | bytes accessed | tf_op | source)
XLA Modules:
  0.0 167.6 jit_solution(16284089397615430616)
XLA Ops:
  0.0 3.3 %fusion.39 = (bf16[8,32,1,512]{3,2,1,0:T(2,128)(2,1)S(1)}, bf16[8,32,1,512]{3,2,1,0:T(2,128)(2,1)S(1)}) fusion(bf16[8,32,64,512]{3,2,1,0:T(8,128)(2,1)} %vals_ref.1), kind=kLoop, calls=%fused_computation.82 | loop fusion | bytes 1048576 | tf_op jit(solution)/shard_map/slice | solution.py:130
  3.3 1.3 collective-permute-start.1
  7.4 1.8 %convert_reduce_fusion = s32[1024]{0:T(1024)S(1)} fusion(s32[4096]{0:T(1024)S(1)} %add_bitcast_fusion, s32[1024]{0:T(1024)S(1)} %iota_add_fusion), kind=kLoop, calls=%fused_computation.2 | loop fusion | flops 12581888 | bytes 24576 | tf_op jit(solution)/shard_map/reduce_sum | solution.py:178
  9.5 1.4 fusion
  11.0 1.3 fusion.12.ca_ref
  12.8 1.9 %collective-permute-done.1 = bf16[8,32,512]{2,1,0:T(8,128)(2,1)} collective-permute-done((bf16[8,32,512]{2,1,0:T(8,128)(2,1)S(1)}, bf16[8,32,512]{2,1,0:T(8,128)(2,1)}, u32[]{:S(2)}, u32[]{:S(2)}) %collective-permute-start.1) | collective-permute-done | bytes 262176 | tf_op jit(solution)/shard_map/ppermute | solution.py:132
  14.7 1.9 %select_convert_fusion = (f32[8,32,512]{2,1,0:T(8,128)}, bf16[8,32,512]{2,1,0:T(8,128)(2,1)S(1)}) fusion(bf16[8,32,512]{2,1,0:T(8,128)(2,1)} %collective-permute-done.1, pred[]{:T(512)S(6)} %eq.69, bf16[8,32,1,512]{3,2,1,0:T(2,128)(2,1)S(1)} %get-tuple-element.7), kind=kLoop, calls=%fused_computation.24 | loop fusion | flops 262144 | bytes 1310721 | tf_op jit(solution)/shard_map/convert_element_type | solution.py:134
  16.5 3.9 %collective-permute-start = (bf16[8,32,512]{2,1,0:T(8,128)(2,1)S(1)}, bf16[8,32,512]{2,1,0:T(8,128)(2,1)S(1)}, u32[]{:S(2)}, u32[]{:S(2)}) collective-permute-start(bf16[8,32,512]{2,1,0:T(8,128)(2,1)S(1)} %get-tuple-element.6), channel_id=1, source_target_pairs={{0,4},{4,8},{8,12},{1,5},{5,9},{9,13},{2,6},{6,10},{10,14},{3,7},{... | collective-permute-start | bytes 786440 | tf_op jit(solution)/shard_map/ppermute | solution.py:131
  20.5 1.6 fusion.8.tb_ref
  22.1 3.7 %collective-permute-done = bf16[8,32,512]{2,1,0:T(8,128)(2,1)S(1)} collective-permute-done((bf16[8,32,512]{2,1,0:T(8,128)(2,1)S(1)}, bf16[8,32,512]{2,1,0:T(8,128)(2,1)S(1)}, u32[]{:S(2)}, u32[]{:S(2)}) %collective-permute-start) | collective-permute-done | bytes 262176 | tf_op jit(solution)/shard_map/ppermute | solution.py:131
  25.8 0.9 select_convert_fusion.1.lo_ref
  26.7 53.1 %shard_map.118 = f32[8,32,64,128]{3,2,1,0:T(8,128)} custom-call(f32[8]{0:T(128)} %load_ref.1, bf16[8,32,64,512]{3,2,1,0:T(8,128)(2,1)} %vals_ref.1, f32[8,32,512]{2,1,0:T(8,128)} %select_convert_fusion.1.lo_ref, f32[8,32,512]{2,1,0:T(8,128)} %get-tuple-element.5.up_ref, f32[32,64,512]{2,1,0:T(8,128)} %rl_ref.1, f32[32,64,512]{2,1,0:T(8,128)} %ri_ref.1, ...), custom_call_target="tpu_custom_call" | custom-call | tf_op jit(solution)/shard_map/pallas_call | solution.py:79
  79.8 9.3 %copy.53.t_ref = f32[128,64,256]{2,1,0:T(8,128)} copy(f32[128,64,256]{0,1,2:T(8,128)} %bitcast.28) | data formatting | bytes 16777216 | tf_op jit(solution)/shard_map/reshape | solution.py:161
  89.1 22.1 %shard_map.119 = f32[128,256,256]{2,1,0:T(8,128)} custom-call(f32[256,64]{1,0:T(8,128)} %fusion.12.ca_ref, f32[128,64,256]{2,1,0:T(8,128)} %copy.53.t_ref), custom_call_target="tpu_custom_call" | custom-call | tf_op jit(solution)/shard_map/pallas_call | solution.py:113
  111.2 26.6 %gather_fusion = f32[4096,256]{1,0:T(8,128)} fusion(f32[32768,256]{1,0:T(8,128)} %bitcast.27, s32[4096]{0:T(1024)S(1)} %broadcast_clamp_fusion), kind=kCustom, calls=%fused_computation | custom fusion | bytes 8404992 | tf_op jit(solution)/shard_map/jit(_take)/gather | solution.py:165
  137.8 5.6 %copy.54 = f32[4096,256]{0,1:T(8,128)} copy(f32[4096,256]{1,0:T(8,128)} %gather_fusion) | data formatting | bytes 8388608 | tf_op jit(solution)/shard_map/jit(_take)/gather | solution.py:165
  143.4 2.9 %multiply_reduce_fusion = f32[4096,8]{0,1:T(8,128)S(1)} fusion(f32[4096,32]{0,1:T(8,128)S(1)} %fusion, pred[4096]{0:T(1024)(128)(4,1)S(1)} %compare_and_fusion, f32[4096,256]{0,1:T(8,128)} %copy.54), kind=kLoop, calls=%fused_computation.3 | loop fusion | flops 3112960 | bytes 4853760 | tf_op jit(solution)/shard_map/reduce_sum | solution.py:170
  146.4 1.3 collective-permute-done.2
  147.8 2.6 %collective-permute-start.3 = (f32[8,4096]{1,0:T(8,128)S(1)}, f32[8,4096]{1,0:T(8,128)S(1)}, u32[]{:S(2)}, u32[]{:S(2)}) collective-permute-start(f32[8,4096]{1,0:T(8,128)S(1)} %bitcast_add_fusion), channel_id=1, source_target_pairs={{0,4},{4,0},{8,12},{12,8},{1,5},{5,1},{9,13},{13,9},{2,6},{6,2},{1... | collective-permute-start | bytes 393224 | tf_op jit(solution)/shard_map/ppermute | solution.py:188
  150.4 3.8 %collective-permute-done.3 = f32[8,4096]{1,0:T(8,128)S(1)} collective-permute-done((f32[8,4096]{1,0:T(8,128)S(1)}, f32[8,4096]{1,0:T(8,128)S(1)}, u32[]{:S(2)}, u32[]{:S(2)}) %collective-permute-start.3) | collective-permute-done | bytes 131104 | tf_op jit(solution)/shard_map/ppermute | solution.py:188
  154.2 2.9 %collective-permute-start.4 = (f32[8,4096]{1,0:T(8,128)S(1)}, f32[8,4096]{1,0:T(8,128)S(1)}, u32[]{:S(2)}, u32[]{:S(2)}) collective-permute-start(f32[8,4096]{1,0:T(8,128)S(1)} %add.126), channel_id=1, source_target_pairs={{0,8},{4,12},{8,0},{12,4},{1,9},{5,13},{9,1},{13,5},{2,10},{6,14},... | collective-permute-start | bytes 393224 | tf_op jit(solution)/shard_map/ppermute | solution.py:188
  157.1 5.9 %collective-permute-done.4 = f32[8,4096]{1,0:T(8,128)S(1)} collective-permute-done((f32[8,4096]{1,0:T(8,128)S(1)}, f32[8,4096]{1,0:T(8,128)S(1)}, u32[]{:S(2)}, u32[]{:S(2)}) %collective-permute-start.4) | collective-permute-done | bytes 131104 | tf_op jit(solution)/shard_map/ppermute | solution.py:188
  163.6 2.8 %gather_fusion.1 = f32[1024,8]{1,0:T(8,128)S(1)} fusion(f32[8,4096]{0,1:T(8,128)S(1)} %copy.55, s32[1024]{0:T(1024)S(1)} %broadcast_clamp_fusion.1), kind=kCustom, calls=%fused_computation.1 | custom fusion | bytes 69632 | tf_op jit(solution)/shard_map/jit(_take)/gather | solution.py:179
  166.8 0.8 copy.56
  (40 shorter events, 4.7 us)
Async XLA Ops:
  0.0 9.2 %copy-start = (f32[64,64]{1,0:T(8,128)S(1)}, f32[64,64]{1,0:T(8,128)}, u32[]{:S(2)}) copy-start(f32[64,64]{1,0:T(8,128)} %param.19) | copy-start | bytes 49156
  0.0 6.8 %copy-start.2 = (s32[4096]{0:T(1024)S(1)}, s32[4096]{0:T(1024)}, u32[]{:S(2)}) copy-start(s32[4096]{0:T(1024)} %param.23) | copy-start | bytes 49156
  0.0 9.5 %copy-start.3 = (s32[4096]{0:T(1024)S(1)}, s32[4096]{0:T(1024)}, u32[]{:S(2)}) copy-start(s32[4096]{0:T(1024)} %param.22) | copy-start | bytes 49156
  3.3 11.4 %collective-permute-start.1 = (bf16[8,32,512]{2,1,0:T(8,128)(2,1)S(1)}, bf16[8,32,512]{2,1,0:T(8,128)(2,1)}, u32[]{:S(2)}, u32[]{:S(2)}) collective-permute-start(bf16[8,32,512]{2,1,0:T(8,128)(2,1)S(1)} %bitcast.30), channel_id=1, source_target_pairs={{4,0},{8,4},{12,8},{5,1},{9,5},{13,9},{6,2},{10,6},{14,10},{7,3},{... | collective-permute-start | bytes 786440 | tf_op jit(solution)/shard_map/ppermute | solution.py:132
  16.5 9.3 %collective-permute-start = (bf16[8,32,512]{2,1,0:T(8,128)(2,1)S(1)}, bf16[8,32,512]{2,1,0:T(8,128)(2,1)S(1)}, u32[]{:S(2)}, u32[]{:S(2)}) collective-permute-start(bf16[8,32,512]{2,1,0:T(8,128)(2,1)S(1)} %get-tuple-element.6), channel_id=1, source_target_pairs={{0,4},{4,8},{8,12},{1,5},{5,9},{9,13},{2,6},{6,10},{10,14},{3,7},{... | collective-permute-start | bytes 786440 | tf_op jit(solution)/shard_map/ppermute | solution.py:131
  137.8 29.8 %copy-start.1 = (f32[64,64]{1,0:T(8,128)S(1)}, f32[64,64]{1,0:T(8,128)}, u32[]{:S(2)}) copy-start(f32[64,64]{1,0:T(8,128)} %param.19) | copy-start | bytes 49156
  146.3 1.4 collective-permute-start.2
  147.8 6.4 %collective-permute-start.3 = (f32[8,4096]{1,0:T(8,128)S(1)}, f32[8,4096]{1,0:T(8,128)S(1)}, u32[]{:S(2)}, u32[]{:S(2)}) collective-permute-start(f32[8,4096]{1,0:T(8,128)S(1)} %bitcast_add_fusion), channel_id=1, source_target_pairs={{0,4},{4,0},{8,12},{12,8},{1,5},{5,1},{9,13},{13,9},{2,6},{6,2},{1... | collective-permute-start | bytes 393224 | tf_op jit(solution)/shard_map/ppermute | solution.py:188
  154.2 8.8 %collective-permute-start.4 = (f32[8,4096]{1,0:T(8,128)S(1)}, f32[8,4096]{1,0:T(8,128)S(1)}, u32[]{:S(2)}, u32[]{:S(2)}) collective-permute-start(f32[8,4096]{1,0:T(8,128)S(1)} %add.126), channel_id=1, source_target_pairs={{0,8},{4,12},{8,0},{12,4},{1,9},{5,13},{9,1},{13,5},{2,10},{6,14},... | collective-permute-start | bytes 393224 | tf_op jit(solution)/shard_map/ppermute | solution.py:188

commit v5 on v3

--- a/solution.py
+++ b/solution.py
@@ -95,6 +95,47 @@
         out_shape=jax.ShapeDtypeStruct((columns, nz, na, kb), jnp.float32),
         compiler_params=pltpu.CompilerParams(vmem_limit_bytes=56 * 1024 * 1024),
     )(load, vals, lower, upper, rl, ri, pf, ml, mi, tb)
+
+
+def illiquid_kernel(kb_ref, ka_ref, ca_ref, t_ref, out_ref, spectrum):
+    j = pl.program_id(0)
+    block = t_ref.shape[0]
+    ch, cl = split_bf16(ca_ref[...])
+    for k in range(block):
+        th, tl = split_bf16(t_ref[k])
+        acc = jnp.dot(cl, th, preferred_element_type=jnp.float32)
+        acc = acc + jnp.dot(ch, tl, preferred_element_type=jnp.float32)
+        spectrum[j * block + k] = acc + jnp.dot(ch, th, preferred_element_type=jnp.float32)
+
+    @pl.when(j == pl.num_programs(0) - 1)
+    def _():
+        def pick(i, carry):
+            out_ref[pl.ds(i, 1), :] = spectrum[kb_ref[i], pl.ds(ka_ref[i], 1), :]
+            return carry
+
+        lax.fori_loop(0, out_ref.shape[0], pick, 0, unroll=8)
+
+
+def illiquid_pick(ca, t, kb_index, ka_index):
+    kb, na_loc, lanes = t.shape
+    na = ca.shape[0]
+    count = kb_index.shape[0]
+    block = 8
+    return pl.pallas_call(
+        illiquid_kernel,
+        grid_spec=pltpu.PrefetchScalarGridSpec(
+            num_scalar_prefetch=2,
+            grid=(kb // block,),
+            in_specs=[
+                pl.BlockSpec((na, na_loc), lambda j, *_: (0, 0)),
+                pl.BlockSpec((block, na_loc, lanes), lambda j, *_: (j, 0, 0)),
+            ],
+            out_specs=pl.BlockSpec((count, lanes), lambda j, *_: (0, 0)),
+            scratch_shapes=[pltpu.VMEM((kb, na, lanes), jnp.float32)],
+        ),
+        out_shape=jax.ShapeDtypeStruct((count, lanes), jnp.float32),
+        compiler_params=pltpu.CompilerParams(vmem_limit_bytes=60 * 1024 * 1024),
+    )(kb_index, ka_index, ca, t)
 
 
 def edges(values, axis, dim):
@@ -135,9 +176,9 @@
     )
     liquid_part = jnp.transpose(liquid_part, (3, 2, 0, 1)).reshape(KBLOW, na_loc, columns * nz_loc)
     table_a = lax.dynamic_slice_in_dim(cosine_table(NA), wide_pos * na_loc, na_loc, axis=1)
-    illiquid_part = jnp.einsum("ja,kac->kjc", table_a, liquid_part, precision=high)
-    rows = illiquid_part.reshape(KBLOW * NA, columns * nz_loc)
-    picked = jnp.take(rows, coef_liquid * NA + coef_illiquid, axis=0)
+    picked = illiquid_pick(
+        table_a, liquid_part, jnp.clip(coef_liquid, 0, KBLOW - 1), jnp.clip(coef_illiquid, 0, NA - 1)
+    )
     folded = jnp.dot(cosine_table(NZ), jump_inverse, precision=lax.Precision.HIGHEST)
     folded = lax.dynamic_slice_in_dim(folded, inc_pos * nz_loc, nz_loc, axis=1)
     pick_z = (coef_income[:, None] == jnp.arange(NZ, dtype=jnp.int32)[None, :]).astype(jnp.float32)

time: 169 us -> 158 us (0.935)
  Pallas kernels: 53.1 us -> 92 us
  local copies, waits for them, and re-layouts: 49.9 us -> 22.7 us
  matrix products: 23.8 us -> 1.77 us
    pallas_call x0 -> x1, Pallas kernels: none -> 38.9 us  [illiquid_pick(): pl.pallas_call(illiquid_kernel, grid_spec=pltpu.PrefetchScalarGridSpec(nu...]
    gather x2 -> x0, local copies, waits for them, and re-layouts: 32.2 us -> none  [body(): picked = jnp.take(rows, coef_liquid * NA + coef_illiquid, axis=0)]
    dot_general x1 -> x0, matrix products: 22.1 us -> none  [body(): jnp.einsum('ja,kac->kjc', table_a, liquid_part, precision=high)]
    pallas_call x0 -> x1, local copies, waits for them, and re-layouts: none -> 5.67 us  [illiquid_pick(): pl.pallas_call(illiquid_kernel, grid_spec=pltpu.PrefetchScalarGridSpec(nu...]
  transfers between devices with their start and end apart: 5 -> 5, of which waited for: 5 -> 5; matrix products, arithmetic and copies ran while one was open for 5% -> 6% of each run, Pallas kernels for 0% -> 0%
where the time goes in v5:
time: 158 us; the launch traced here: 157 us
  Pallas kernels  92 us (58%)
  local copies, waits for them, and re-layouts  22.7 us (14%)
  waiting for transfers between devices  16.6 us (11%)
  other arithmetic  12.8 us (8%)
  starting transfers between devices  10.7 us (7%)
  matrix products  1.77 us (1%)
    pallas_call x1, Pallas kernels, liquid_step(): pl.pallas_call(step_kernel, grid=(nz // zb,), in_specs=[pl.BlockSpec(memo...  53.2 us
    pallas_call x1, Pallas kernels, illiquid_pick(): pl.pallas_call(illiquid_kernel, grid_spec=pltpu.PrefetchScalarGridSpec(nu...  38.9 us
    ppermute x3, waiting for transfers between devices, all_sum(): x = x + lax.ppermute(x, axis, [(i, i ^ step) for i in range(count)])  11 us
    reshape x1, local copies, waits for them, and re-layouts, body(): jnp.transpose(liquid_part, (3, 2, 0, 1))  9.24 us
    pallas_call x1, local copies, waits for them, and re-layouts, illiquid_pick(): pl.pallas_call(illiquid_kernel, grid_spec=pltpu.PrefetchScalarGridSpec(nu...  5.67 us
    ppermute x3, starting transfers between devices, all_sum(): x = x + lax.ppermute(x, axis, [(i, i ^ step) for i in range(count)])  5.59 us
    ppermute x1, starting transfers between devices, edges(): lax.ppermute(tail, axis, [(i, (i + 1) % count) for i in range(ends)])  3.82 us
    slice x1, local copies, waits for them, and re-layouts, edges(): lax.index_in_dim(values, values.shape[dim] - 1, axis=dim, keepdims=False)  3.32 us
  transfers between devices with their start and end apart: 5, of which 5 were waited for; matrix products, arithmetic and copies ran while one was open for 6% of the time, Pallas kernels for 0%

profile of v5, /device:TPU:0, one launch (start us, length us, event | category | flops | bytes accessed | tf_op | source)
XLA Modules:
  0.0 156.9 jit_solution(10664423962265434485)
XLA Ops:
  0.0 3.3 %fusion.39 = (bf16[8,32,1,512]{3,2,1,0:T(2,128)(2,1)S(1)}, bf16[8,32,1,512]{3,2,1,0:T(2,128)(2,1)S(1)}) fusion(bf16[8,32,64,512]{3,2,1,0:T(8,128)(2,1)} %vals_ref.1), kind=kLoop, calls=%fused_computation.80 | loop fusion | bytes 1048576 | tf_op jit(solution)/shard_map/slice | solution.py:146
  3.4 1.3 collective-permute-start.1
  5.9 0.6 broadcast_clamp_fusion
  6.6 1.8 %convert_reduce_fusion = s32[1024]{0:T(1024)S(1)} fusion(s32[4096]{0:T(1024)S(1)} %add_bitcast_fusion, s32[1024]{0:T(1024)S(1)} %iota_add_fusion), kind=kLoop, calls=%fused_computation.1 | loop fusion | flops 12581888 | bytes 24576 | tf_op jit(solution)/shard_map/reduce_sum | solution.py:194
  8.7 1.4 fusion
  10.1 1.3 fusion.12.ca_ref
  12.0 2.7 %collective-permute-done.1 = bf16[8,32,512]{2,1,0:T(8,128)(2,1)} collective-permute-done((bf16[8,32,512]{2,1,0:T(8,128)(2,1)S(1)}, bf16[8,32,512]{2,1,0:T(8,128)(2,1)}, u32[]{:S(2)}, u32[]{:S(2)}) %collective-permute-start.1) | collective-permute-done | bytes 262176 | tf_op jit(solution)/shard_map/ppermute | solution.py:148
  14.7 1.9 %select_convert_fusion = (f32[8,32,512]{2,1,0:T(8,128)}, bf16[8,32,512]{2,1,0:T(8,128)(2,1)S(1)}) fusion(bf16[8,32,512]{2,1,0:T(8,128)(2,1)} %collective-permute-done.1, pred[]{:T(512)S(6)} %eq.69, bf16[8,32,1,512]{3,2,1,0:T(2,128)(2,1)S(1)} %get-tuple-element.7), kind=kLoop, calls=%fused_computation.23 | loop fusion | flops 262144 | bytes 1310721 | tf_op jit(solution)/shard_map/convert_element_type | solution.py:150
  16.6 3.8 %collective-permute-start = (bf16[8,32,512]{2,1,0:T(8,128)(2,1)S(1)}, bf16[8,32,512]{2,1,0:T(8,128)(2,1)S(1)}, u32[]{:S(2)}, u32[]{:S(2)}) collective-permute-start(bf16[8,32,512]{2,1,0:T(8,128)(2,1)S(1)} %get-tuple-element.6), channel_id=1, source_target_pairs={{0,4},{4,8},{8,12},{1,5},{5,9},{9,13},{2,6},{6,10},{10,14},{3,7},{... | collective-permute-start | bytes 786440 | tf_op jit(solution)/shard_map/ppermute | solution.py:147
  20.4 1.6 %fusion.8.tb_ref = f32[512,128]{1,0:T(8,128)} fusion(s32[512,512]{0,1:T(8,128)S(1)} %negate_select_fusion, pred[512,512]{0,1:T(8,128)(4,1)S(1)} %get-tuple-element.12, pred[512,512]{0,1:T(8,128)(4,1)S(1)} %get-tuple-element.11, f32[128]{0:T(128)S(1)} %slice.28), kind=kLoop, calls=%fused_computation.20 | loop fusion | flops 393216 | bytes 655872 | tf_op jit(solution)/shard_map/transpose | solution.py:175
  22.1 2.9 %collective-permute-done = bf16[8,32,512]{2,1,0:T(8,128)(2,1)S(1)} collective-permute-done((bf16[8,32,512]{2,1,0:T(8,128)(2,1)S(1)}, bf16[8,32,512]{2,1,0:T(8,128)(2,1)S(1)}, u32[]{:S(2)}, u32[]{:S(2)}) %collective-permute-start) | collective-permute-done | bytes 262176 | tf_op jit(solution)/shard_map/ppermute | solution.py:147
  25.0 0.9 select_convert_fusion.1.lo_ref
  25.9 53.2 %shard_map.118 = f32[8,32,64,128]{3,2,1,0:T(8,128)} custom-call(f32[8]{0:T(128)} %load_ref.1, bf16[8,32,64,512]{3,2,1,0:T(8,128)(2,1)} %vals_ref.1, f32[8,32,512]{2,1,0:T(8,128)} %select_convert_fusion.1.lo_ref, f32[8,32,512]{2,1,0:T(8,128)} %get-tuple-element.5.up_ref, f32[32,64,512]{2,1,0:T(8,128)} %rl_ref.1, f32[32,64,512]{2,1,0:T(8,128)} %ri_ref.1, ...), custom_call_target="tpu_custom_call" | custom-call | tf_op jit(solution)/shard_map/pallas_call | solution.py:79
  79.0 9.2 %copy.53.t_ref = f32[128,64,256]{2,1,0:T(8,128)} copy(f32[128,64,256]{0,1,2:T(8,128)} %bitcast.26) | data formatting | bytes 16777216 | tf_op jit(solution)/shard_map/reshape | solution.py:177
  88.3 38.9 %shard_map.119 = f32[4096,256]{1,0:T(8,128)} custom-call(s32[4096]{0:T(1024)} %get-tuple-element.16.kb_ref, s32[4096]{0:T(1024)} %get-tuple-element.15.ka_ref, f32[256,64]{1,0:T(8,128)} %fusion.12.ca_ref, f32[128,64,256]{2,1,0:T(8,128)} %copy.53.t_ref), custom_call_target="tpu_custom_call" | custom-call | tf_op jit(solution)/shard_map/pallas_call | solution.py:124
  127.2 5.7 %copy.54 = f32[4096,256]{0,1:T(8,128)} copy(f32[4096,256]{1,0:T(8,128)} %shard_map.119) | data formatting | bytes 8388608 | tf_op jit(solution)/shard_map/pallas_call | solution.py:124
  132.8 2.8 %multiply_reduce_fusion = f32[4096,8]{0,1:T(8,128)S(1)} fusion(f32[4096,32]{0,1:T(8,128)S(1)} %fusion, f32[4096,256]{0,1:T(8,128)} %copy.54), kind=kLoop, calls=%fused_computation.2 | loop fusion | flops 2064384 | bytes 4849664 | tf_op jit(solution)/shard_map/reduce_sum | solution.py:186
  135.8 1.3 collective-permute-done.2
  137.1 2.6 %collective-permute-start.3 = (f32[8,4096]{1,0:T(8,128)S(1)}, f32[8,4096]{1,0:T(8,128)S(1)}, u32[]{:S(2)}, u32[]{:S(2)}) collective-permute-start(f32[8,4096]{1,0:T(8,128)S(1)} %bitcast_add_fusion), channel_id=1, source_target_pairs={{0,4},{4,0},{8,12},{12,8},{1,5},{5,1},{9,13},{13,9},{2,6},{6,2},{1... | collective-permute-start | bytes 393224 | tf_op jit(solution)/shard_map/ppermute | solution.py:204
  139.7 3.8 %collective-permute-done.3 = f32[8,4096]{1,0:T(8,128)S(1)} collective-permute-done((f32[8,4096]{1,0:T(8,128)S(1)}, f32[8,4096]{1,0:T(8,128)S(1)}, u32[]{:S(2)}, u32[]{:S(2)}) %collective-permute-start.3) | collective-permute-done | bytes 131104 | tf_op jit(solution)/shard_map/ppermute | solution.py:204
  143.5 3.0 %collective-permute-start.4 = (f32[8,4096]{1,0:T(8,128)S(1)}, f32[8,4096]{1,0:T(8,128)S(1)}, u32[]{:S(2)}, u32[]{:S(2)}) collective-permute-start(f32[8,4096]{1,0:T(8,128)S(1)} %add.112), channel_id=1, source_target_pairs={{0,8},{4,12},{8,0},{12,4},{1,9},{5,13},{9,1},{13,5},{2,10},{6,14},... | collective-permute-start | bytes 393224 | tf_op jit(solution)/shard_map/ppermute | solution.py:204
  146.5 5.8 %collective-permute-done.4 = f32[8,4096]{1,0:T(8,128)S(1)} collective-permute-done((f32[8,4096]{1,0:T(8,128)S(1)}, f32[8,4096]{1,0:T(8,128)S(1)}, u32[]{:S(2)}, u32[]{:S(2)}) %collective-permute-start.4) | collective-permute-done | bytes 131104 | tf_op jit(solution)/shard_map/ppermute | solution.py:204
  152.9 2.8 %gather_fusion = f32[1024,8]{1,0:T(8,128)S(1)} fusion(f32[8,4096]{0,1:T(8,128)S(1)} %copy.55, s32[1024]{0:T(1024)S(1)} %broadcast_clamp_fusion.2), kind=kCustom, calls=%fused_computation | custom fusion | bytes 69632 | tf_op jit(solution)/shard_map/jit(_take)/gather | solution.py:195
  156.1 0.8 copy.56
  (42 shorter events, 3.2 us)
Async XLA Ops:
  0.0 8.3 %copy-start = (f32[64,64]{1,0:T(8,128)S(1)}, f32[64,64]{1,0:T(8,128)}, u32[]{:S(2)}) copy-start(f32[64,64]{1,0:T(8,128)} %param.19) | copy-start | bytes 49156
  0.0 5.3 %copy-start.2 = (s32[4096]{0:T(1024)S(1)}, s32[4096]{0:T(1024)}, u32[]{:S(2)}) copy-start(s32[4096]{0:T(1024)} %param.23) | copy-start | bytes 49156
  0.0 5.9 %copy-start.4 = (s32[4096]{0:T(1024)S(1)}, s32[4096]{0:T(1024)}, u32[]{:S(2)}) copy-start(s32[4096]{0:T(1024)} %param.20) | copy-start | bytes 49156
  0.0 5.9 %copy-start.3 = (s32[4096]{0:T(1024)S(1)}, s32[4096]{0:T(1024)}, u32[]{:S(2)}) copy-start(s32[4096]{0:T(1024)} %param.21) | copy-start | bytes 49156
  0.0 8.7 %copy-start.5 = (s32[4096]{0:T(1024)S(1)}, s32[4096]{0:T(1024)}, u32[]{:S(2)}) copy-start(s32[4096]{0:T(1024)} %param.22) | copy-start | bytes 49156
  3.4 11.3 %collective-permute-start.1 = (bf16[8,32,512]{2,1,0:T(8,128)(2,1)S(1)}, bf16[8,32,512]{2,1,0:T(8,128)(2,1)}, u32[]{:S(2)}, u32[]{:S(2)}) collective-permute-start(bf16[8,32,512]{2,1,0:T(8,128)(2,1)S(1)} %bitcast.28), channel_id=1, source_target_pairs={{4,0},{8,4},{12,8},{5,1},{9,5},{13,9},{6,2},{10,6},{14,10},{7,3},{... | collective-permute-start | bytes 786440 | tf_op jit(solution)/shard_map/ppermute | solution.py:148
  16.6 8.4 %collective-permute-start = (bf16[8,32,512]{2,1,0:T(8,128)(2,1)S(1)}, bf16[8,32,512]{2,1,0:T(8,128)(2,1)S(1)}, u32[]{:S(2)}, u32[]{:S(2)}) collective-permute-start(bf16[8,32,512]{2,1,0:T(8,128)(2,1)S(1)} %get-tuple-element.6), channel_id=1, source_target_pairs={{0,4},{4,8},{8,12},{1,5},{5,9},{9,13},{2,6},{6,10},{10,14},{3,7},{... | collective-permute-start | bytes 786440 | tf_op jit(solution)/shard_map/ppermute | solution.py:147
  127.2 29.7 %copy-start.1 = (f32[64,64]{1,0:T(8,128)S(1)}, f32[64,64]{1,0:T(8,128)}, u32[]{:S(2)}) copy-start(f32[64,64]{1,0:T(8,128)} %param.19) | copy-start | bytes 49156
  135.7 1.4 collective-permute-start.2
  137.1 6.4 %collective-permute-start.3 = (f32[8,4096]{1,0:T(8,128)S(1)}, f32[8,4096]{1,0:T(8,128)S(1)}, u32[]{:S(2)}, u32[]{:S(2)}) collective-permute-start(f32[8,4096]{1,0:T(8,128)S(1)} %bitcast_add_fusion), channel_id=1, source_target_pairs={{0,4},{4,0},{8,12},{12,8},{1,5},{5,1},{9,13},{13,9},{2,6},{6,2},{1... | collective-permute-start | bytes 393224 | tf_op jit(solution)/shard_map/ppermute | solution.py:204
  143.5 8.8 %collective-permute-start.4 = (f32[8,4096]{1,0:T(8,128)S(1)}, f32[8,4096]{1,0:T(8,128)S(1)}, u32[]{:S(2)}, u32[]{:S(2)}) collective-permute-start(f32[8,4096]{1,0:T(8,128)S(1)} %add.112), channel_id=1, source_target_pairs={{0,8},{4,12},{8,0},{12,4},{1,9},{5,13},{9,1},{13,5},{2,10},{6,14},... | collective-permute-start | bytes 393224 | tf_op jit(solution)/shard_map/ppermute | solution.py:204

commit v6 on v5

--- a/solution.py
+++ b/solution.py
@@ -46,24 +46,30 @@
     ma = mi_ref[...].reshape(rows, nb) != 0
     col = lax.broadcasted_iota(jnp.int32, (rows, nb), 1)
     arow = lax.broadcasted_iota(jnp.int32, (zb, na, nb), 1).reshape(rows, nb)
+    next_b = mb & (col != nb - 1)
+    prev_b = jnp.logical_not(mb) & (col != 0)
+    top = arow == na - 1
+    bottom = arow == 0
     th, tl = split_bf16(tb_ref[...])
+    pf_hi, pf_lo = split_bf16(pf)
+    price = jnp.dot(pf_lo, th, preferred_element_type=jnp.float32)
+    price = price + jnp.dot(pf_hi, tl, preferred_element_type=jnp.float32)
+    price = price + jnp.dot(pf_hi, th, preferred_element_type=jnp.float32)
 
     def per_column(c, carry):
         v = vals_ref[c].reshape(rows, nb).astype(jnp.float32)
         lo = jnp.broadcast_to(lo_ref[c][:, None, :], (zb, na, nb)).reshape(rows, nb)
         up = jnp.broadcast_to(up_ref[c][:, None, :], (zb, na, nb)).reshape(rows, nb)
-        fwd_b = jnp.where(col == nb - 1, 0.0, pltpu.roll(v, nb - 1, 1) - v)
-        bwd_b = jnp.where(col == 0, 0.0, v - pltpu.roll(v, 1, 1))
-        fwd_a = jnp.where(arow == na - 1, up, pltpu.roll(v, rows - 1, 0)) - v
-        bwd_a = v - jnp.where(arow == 0, lo, pltpu.roll(v, 1, 0))
-        sel_b = jnp.where(mb, fwd_b, -bwd_b)
-        sel_a = jnp.where(ma, fwd_a, -bwd_a)
-        explicit = v + rl * sel_b + ri * sel_a + load_ref[c] * pf
+        side_b = jnp.where(next_b, pltpu.roll(v, nb - 1, 1), jnp.where(prev_b, pltpu.roll(v, 1, 1), v))
+        above = jnp.where(top, up, pltpu.roll(v, rows - 1, 0))
+        below = jnp.where(bottom, lo, pltpu.roll(v, 1, 0))
+        side_a = jnp.where(ma, above, below)
+        explicit = v + rl * (side_b - v) + ri * (side_a - v)
         hi, low = split_bf16(explicit)
         acc = jnp.dot(low, th, preferred_element_type=jnp.float32)
         acc = acc + jnp.dot(hi, tl, preferred_element_type=jnp.float32)
         acc = acc + jnp.dot(hi, th, preferred_element_type=jnp.float32)
-        out_ref[c] = acc.reshape(zb, na, kb)
+        out_ref[c] = (acc + load_ref[c] * price).reshape(zb, na, kb)
         return carry
 
     lax.fori_loop(0, columns, per_column, 0)

time: 158 us -> 156 us (0.987)
  Pallas kernels: 92 us -> 89.9 us
    pallas_call x1, Pallas kernels: 53.2 us -> 51 us  [liquid_step(): pl.pallas_call(step_kernel, grid=(nz // zb,), in_specs=[pl.BlockSpec(memo...]
where the time goes in v6:
time: 156 us; the launch traced here: 155 us
  Pallas kernels  89.9 us (58%)
  local copies, waits for them, and re-layouts  22.7 us (15%)
  waiting for transfers between devices  16.6 us (11%)
  other arithmetic  12.8 us (8%)
  starting transfers between devices  10.7 us (7%)
  matrix products  1.77 us (1%)
    pallas_call x1, Pallas kernels, liquid_step(): pl.pallas_call(step_kernel, grid=(nz // zb,), in_specs=[pl.BlockSpec(memo...  51 us
    pallas_call x1, Pallas kernels, illiquid_pick(): pl.pallas_call(illiquid_kernel, grid_spec=pltpu.PrefetchScalarGridSpec(nu...  38.9 us
    ppermute x3, waiting for transfers between devices, all_sum(): x = x + lax.ppermute(x, axis, [(i, i ^ step) for i in range(count)])  10.9 us
    reshape x1, local copies, waits for them, and re-layouts, body(): jnp.transpose(liquid_part, (3, 2, 0, 1))  9.24 us
    pallas_call x1, local copies, waits for them, and re-layouts, illiquid_pick(): pl.pallas_call(illiquid_kernel, grid_spec=pltpu.PrefetchScalarGridSpec(nu...  5.67 us
    ppermute x3, starting transfers between devices, all_sum(): x = x + lax.ppermute(x, axis, [(i, i ^ step) for i in range(count)])  5.59 us
    ppermute x1, starting transfers between devices, edges(): lax.ppermute(tail, axis, [(i, (i + 1) % count) for i in range(ends)])  3.82 us
    slice x1, local copies, waits for them, and re-layouts, edges(): lax.index_in_dim(values, values.shape[dim] - 1, axis=dim, keepdims=False)  3.32 us
  transfers between devices with their start and end apart: 5, of which 5 were waited for; matrix products, arithmetic and copies ran while one was open for 6% of the time, Pallas kernels for 0%

profile of v6, /device:TPU:0, one launch (start us, length us, event | category | flops | bytes accessed | tf_op | source)
XLA Modules:
  0.0 154.7 jit_solution(16894487609279794987)
XLA Ops:
  0.0 3.3 %fusion.39 = (bf16[8,32,1,512]{3,2,1,0:T(2,128)(2,1)S(1)}, bf16[8,32,1,512]{3,2,1,0:T(2,128)(2,1)S(1)}) fusion(bf16[8,32,64,512]{3,2,1,0:T(8,128)(2,1)} %vals_ref.1), kind=kLoop, calls=%fused_computation.80 | loop fusion | bytes 1048576 | tf_op jit(solution)/shard_map/slice | solution.py:152
  3.4 1.3 collective-permute-start.1
  5.9 0.6 broadcast_clamp_fusion
  6.6 1.8 %convert_reduce_fusion = s32[1024]{0:T(1024)S(1)} fusion(s32[4096]{0:T(1024)S(1)} %add_bitcast_fusion, s32[1024]{0:T(1024)S(1)} %iota_add_fusion), kind=kLoop, calls=%fused_computation.1 | loop fusion | flops 12581888 | bytes 24576 | tf_op jit(solution)/shard_map/reduce_sum | solution.py:200
  8.7 1.4 fusion
  10.1 1.3 fusion.12.ca_ref
  12.0 2.7 %collective-permute-done.1 = bf16[8,32,512]{2,1,0:T(8,128)(2,1)} collective-permute-done((bf16[8,32,512]{2,1,0:T(8,128)(2,1)S(1)}, bf16[8,32,512]{2,1,0:T(8,128)(2,1)}, u32[]{:S(2)}, u32[]{:S(2)}) %collective-permute-start.1) | collective-permute-done | bytes 262176 | tf_op jit(solution)/shard_map/ppermute | solution.py:154
  14.7 1.9 %select_convert_fusion = (f32[8,32,512]{2,1,0:T(8,128)}, bf16[8,32,512]{2,1,0:T(8,128)(2,1)S(1)}) fusion(bf16[8,32,512]{2,1,0:T(8,128)(2,1)} %collective-permute-done.1, pred[]{:T(512)S(6)} %eq.69, bf16[8,32,1,512]{3,2,1,0:T(2,128)(2,1)S(1)} %get-tuple-element.7), kind=kLoop, calls=%fused_computation.23 | loop fusion | flops 262144 | bytes 1310721 | tf_op jit(solution)/shard_map/convert_element_type | solution.py:156
  16.6 3.8 %collective-permute-start = (bf16[8,32,512]{2,1,0:T(8,128)(2,1)S(1)}, bf16[8,32,512]{2,1,0:T(8,128)(2,1)S(1)}, u32[]{:S(2)}, u32[]{:S(2)}) collective-permute-start(bf16[8,32,512]{2,1,0:T(8,128)(2,1)S(1)} %get-tuple-element.6), channel_id=1, source_target_pairs={{0,4},{4,8},{8,12},{1,5},{5,9},{9,13},{2,6},{6,10},{10,14},{3,7},{... | collective-permute-start | bytes 786440 | tf_op jit(solution)/shard_map/ppermute | solution.py:153
  20.4 1.6 %fusion.8.tb_ref = f32[512,128]{1,0:T(8,128)} fusion(s32[512,512]{0,1:T(8,128)S(1)} %negate_select_fusion, pred[512,512]{0,1:T(8,128)(4,1)S(1)} %get-tuple-element.12, pred[512,512]{0,1:T(8,128)(4,1)S(1)} %get-tuple-element.11, f32[128]{0:T(128)S(1)} %slice.28), kind=kLoop, calls=%fused_computation.20 | loop fusion | flops 393216 | bytes 655872 | tf_op jit(solution)/shard_map/transpose | solution.py:181
  22.1 2.9 %collective-permute-done = bf16[8,32,512]{2,1,0:T(8,128)(2,1)S(1)} collective-permute-done((bf16[8,32,512]{2,1,0:T(8,128)(2,1)S(1)}, bf16[8,32,512]{2,1,0:T(8,128)(2,1)S(1)}, u32[]{:S(2)}, u32[]{:S(2)}) %collective-permute-start) | collective-permute-done | bytes 262176 | tf_op jit(solution)/shard_map/ppermute | solution.py:153
  25.0 0.9 select_convert_fusion.1.lo_ref
  25.9 51.0 %shard_map.118 = f32[8,32,64,128]{3,2,1,0:T(8,128)} custom-call(f32[8]{0:T(128)} %load_ref.1, bf16[8,32,64,512]{3,2,1,0:T(8,128)(2,1)} %vals_ref.1, f32[8,32,512]{2,1,0:T(8,128)} %select_convert_fusion.1.lo_ref, f32[8,32,512]{2,1,0:T(8,128)} %get-tuple-element.5.up_ref, f32[32,64,512]{2,1,0:T(8,128)} %rl_ref.1, f32[32,64,512]{2,1,0:T(8,128)} %ri_ref.1, ...), custom_call_target="tpu_custom_call" | custom-call | tf_op jit(solution)/shard_map/pallas_call | solution.py:85
  76.9 9.2 %copy.53.t_ref = f32[128,64,256]{2,1,0:T(8,128)} copy(f32[128,64,256]{0,1,2:T(8,128)} %bitcast.26) | data formatting | bytes 16777216 | tf_op jit(solution)/shard_map/reshape | solution.py:183
  86.1 38.9 %shard_map.119 = f32[4096,256]{1,0:T(8,128)} custom-call(s32[4096]{0:T(1024)} %get-tuple-element.16.kb_ref, s32[4096]{0:T(1024)} %get-tuple-element.15.ka_ref, f32[256,64]{1,0:T(8,128)} %fusion.12.ca_ref, f32[128,64,256]{2,1,0:T(8,128)} %copy.53.t_ref), custom_call_target="tpu_custom_call" | custom-call | tf_op jit(solution)/shard_map/pallas_call | solution.py:130
  125.0 5.7 %copy.54 = f32[4096,256]{0,1:T(8,128)} copy(f32[4096,256]{1,0:T(8,128)} %shard_map.119) | data formatting | bytes 8388608 | tf_op jit(solution)/shard_map/pallas_call | solution.py:130
  130.7 2.8 %multiply_reduce_fusion = f32[4096,8]{0,1:T(8,128)S(1)} fusion(f32[4096,32]{0,1:T(8,128)S(1)} %fusion, f32[4096,256]{0,1:T(8,128)} %copy.54), kind=kLoop, calls=%fused_computation.2 | loop fusion | flops 2064384 | bytes 4849664 | tf_op jit(solution)/shard_map/reduce_sum | solution.py:192
  133.6 1.3 collective-permute-done.2
  134.9 2.5 %collective-permute-start.3 = (f32[8,4096]{1,0:T(8,128)S(1)}, f32[8,4096]{1,0:T(8,128)S(1)}, u32[]{:S(2)}, u32[]{:S(2)}) collective-permute-start(f32[8,4096]{1,0:T(8,128)S(1)} %bitcast_add_fusion), channel_id=1, source_target_pairs={{0,4},{4,0},{8,12},{12,8},{1,5},{5,1},{9,13},{13,9},{2,6},{6,2},{1... | collective-permute-start | bytes 393224 | tf_op jit(solution)/shard_map/ppermute | solution.py:210
  137.5 3.8 %collective-permute-done.3 = f32[8,4096]{1,0:T(8,128)S(1)} collective-permute-done((f32[8,4096]{1,0:T(8,128)S(1)}, f32[8,4096]{1,0:T(8,128)S(1)}, u32[]{:S(2)}, u32[]{:S(2)}) %collective-permute-start.3) | collective-permute-done | bytes 131104 | tf_op jit(solution)/shard_map/ppermute | solution.py:210
  141.3 3.0 %collective-permute-start.4 = (f32[8,4096]{1,0:T(8,128)S(1)}, f32[8,4096]{1,0:T(8,128)S(1)}, u32[]{:S(2)}, u32[]{:S(2)}) collective-permute-start(f32[8,4096]{1,0:T(8,128)S(1)} %add.112), channel_id=1, source_target_pairs={{0,8},{4,12},{8,0},{12,4},{1,9},{5,13},{9,1},{13,5},{2,10},{6,14},... | collective-permute-start | bytes 393224 | tf_op jit(solution)/shard_map/ppermute | solution.py:210
  144.3 5.8 %collective-permute-done.4 = f32[8,4096]{1,0:T(8,128)S(1)} collective-permute-done((f32[8,4096]{1,0:T(8,128)S(1)}, f32[8,4096]{1,0:T(8,128)S(1)}, u32[]{:S(2)}, u32[]{:S(2)}) %collective-permute-start.4) | collective-permute-done | bytes 131104 | tf_op jit(solution)/shard_map/ppermute | solution.py:210
  150.7 2.8 %gather_fusion = f32[1024,8]{1,0:T(8,128)S(1)} fusion(f32[8,4096]{0,1:T(8,128)S(1)} %copy.55, s32[1024]{0:T(1024)S(1)} %broadcast_clamp_fusion.2), kind=kCustom, calls=%fused_computation | custom fusion | bytes 69632 | tf_op jit(solution)/shard_map/jit(_take)/gather | solution.py:201
  153.9 0.8 copy.56
  (42 shorter events, 3.2 us)
Async XLA Ops:
  0.0 8.3 %copy-start = (f32[64,64]{1,0:T(8,128)S(1)}, f32[64,64]{1,0:T(8,128)}, u32[]{:S(2)}) copy-start(f32[64,64]{1,0:T(8,128)} %param.19) | copy-start | bytes 49156
  0.0 5.3 %copy-start.2 = (s32[4096]{0:T(1024)S(1)}, s32[4096]{0:T(1024)}, u32[]{:S(2)}) copy-start(s32[4096]{0:T(1024)} %param.23) | copy-start | bytes 49156
  0.0 5.9 %copy-start.4 = (s32[4096]{0:T(1024)S(1)}, s32[4096]{0:T(1024)}, u32[]{:S(2)}) copy-start(s32[4096]{0:T(1024)} %param.20) | copy-start | bytes 49156
  0.0 5.9 %copy-start.3 = (s32[4096]{0:T(1024)S(1)}, s32[4096]{0:T(1024)}, u32[]{:S(2)}) copy-start(s32[4096]{0:T(1024)} %param.21) | copy-start | bytes 49156
  0.0 8.7 %copy-start.5 = (s32[4096]{0:T(1024)S(1)}, s32[4096]{0:T(1024)}, u32[]{:S(2)}) copy-start(s32[4096]{0:T(1024)} %param.22) | copy-start | bytes 49156
  3.4 11.3 %collective-permute-start.1 = (bf16[8,32,512]{2,1,0:T(8,128)(2,1)S(1)}, bf16[8,32,512]{2,1,0:T(8,128)(2,1)}, u32[]{:S(2)}, u32[]{:S(2)}) collective-permute-start(bf16[8,32,512]{2,1,0:T(8,128)(2,1)S(1)} %bitcast.28), channel_id=1, source_target_pairs={{4,0},{8,4},{12,8},{5,1},{9,5},{13,9},{6,2},{10,6},{14,10},{7,3},{... | collective-permute-start | bytes 786440 | tf_op jit(solution)/shard_map/ppermute | solution.py:154
  16.6 8.4 %collective-permute-start = (bf16[8,32,512]{2,1,0:T(8,128)(2,1)S(1)}, bf16[8,32,512]{2,1,0:T(8,128)(2,1)S(1)}, u32[]{:S(2)}, u32[]{:S(2)}) collective-permute-start(bf16[8,32,512]{2,1,0:T(8,128)(2,1)S(1)} %get-tuple-element.6), channel_id=1, source_target_pairs={{0,4},{4,8},{8,12},{1,5},{5,9},{9,13},{2,6},{6,10},{10,14},{3,7},{... | collective-permute-start | bytes 786440 | tf_op jit(solution)/shard_map/ppermute | solution.py:153
  125.0 29.7 %copy-start.1 = (f32[64,64]{1,0:T(8,128)S(1)}, f32[64,64]{1,0:T(8,128)}, u32[]{:S(2)}) copy-start(f32[64,64]{1,0:T(8,128)} %param.19) | copy-start | bytes 49156
  133.5 1.4 collective-permute-start.2
  134.9 6.4 %collective-permute-start.3 = (f32[8,4096]{1,0:T(8,128)S(1)}, f32[8,4096]{1,0:T(8,128)S(1)}, u32[]{:S(2)}, u32[]{:S(2)}) collective-permute-start(f32[8,4096]{1,0:T(8,128)S(1)} %bitcast_add_fusion), channel_id=1, source_target_pairs={{0,4},{4,0},{8,12},{12,8},{1,5},{5,1},{9,13},{13,9},{2,6},{6,2},{1... | collective-permute-start | bytes 393224 | tf_op jit(solution)/shard_map/ppermute | solution.py:210
  141.3 8.8 %collective-permute-start.4 = (f32[8,4096]{1,0:T(8,128)S(1)}, f32[8,4096]{1,0:T(8,128)S(1)}, u32[]{:S(2)}, u32[]{:S(2)}) collective-permute-start(f32[8,4096]{1,0:T(8,128)S(1)} %add.112), channel_id=1, source_target_pairs={{0,8},{4,12},{8,0},{12,4},{1,9},{5,13},{9,1},{13,5},{2,10},{6,14},... | collective-permute-start | bytes 393224 | tf_op jit(solution)/shard_map/ppermute | solution.py:210

commit v7 on v6

--- a/solution.py
+++ b/solution.py
@@ -11,6 +11,7 @@
 NZ = 64
 KBLOW = 128
 Z_BLOCK = 8
+CHUNK = 16
 
 
 def cosine_table(count):
@@ -34,39 +35,53 @@
     return hi, (x - hi.astype(jnp.float32)).astype(jnp.bfloat16)
 
 
-def step_kernel(load_ref, vals_ref, lo_ref, up_ref, rl_ref, ri_ref, pf_ref, ml_ref, mi_ref, tb_ref, out_ref):
-    columns = vals_ref.shape[0]
-    zb, na, nb = rl_ref.shape
+def step_kernel(load_ref, vals_ref, lo_ref, up_ref, rl_ref, ri_ref, pf_ref, ml_ref, mi_ref, tb_ref, out_ref, ex_hi, ex_lo):
+    columns, zb, na, nb = vals_ref.shape
     kb = tb_ref.shape[1]
     rows = zb * na
-    rl = rl_ref[...].reshape(rows, nb)
-    ri = ri_ref[...].reshape(rows, nb)
-    pf = pf_ref[...].reshape(rows, nb)
-    mb = ml_ref[...].reshape(rows, nb) != 0
-    ma = mi_ref[...].reshape(rows, nb) != 0
-    col = lax.broadcasted_iota(jnp.int32, (rows, nb), 1)
-    arow = lax.broadcasted_iota(jnp.int32, (zb, na, nb), 1).reshape(rows, nb)
-    next_b = mb & (col != nb - 1)
-    prev_b = jnp.logical_not(mb) & (col != 0)
-    top = arow == na - 1
-    bottom = arow == 0
+    depth = CHUNK if na % CHUNK == 0 else na
+    chunks = na // depth
+    col = lax.broadcasted_iota(jnp.int32, (depth, nb), 1)
+    row = lax.broadcasted_iota(jnp.int32, (depth, nb), 0)
+
+    def per_slab(index, carry):
+        c = index // zb
+        z = index % zb
+        lo_row = lo_ref[c, pl.ds(z, 1), :]
+        up_row = up_ref[c, pl.ds(z, 1), :]
+        parts = [vals_ref[c, z, pl.ds(k * depth, depth), :].astype(jnp.float32) for k in range(chunks)]
+        for k in range(chunks):
+            v = parts[k]
+            nxt = parts[k + 1][0:1] if k + 1 < chunks else up_row
+            prv = parts[k - 1][depth - 1:depth] if k > 0 else lo_row
+            above = jnp.where(row == depth - 1, nxt, pltpu.roll(v, depth - 1, 0))
+            below = jnp.where(row == 0, prv, pltpu.roll(v, 1, 0))
+            span = pl.ds(k * depth, depth)
+            mb = ml_ref[z, span, :] != 0
+            ma = mi_ref[z, span, :] != 0
+            side_b = jnp.where(
+                mb & (col != nb - 1),
+                pltpu.roll(v, nb - 1, 1),
+                jnp.where(jnp.logical_not(mb) & (col != 0), pltpu.roll(v, 1, 1), v),
+            )
+            side_a = jnp.where(ma, above, below)
+            explicit = v + rl_ref[z, span, :] * (side_b - v) + ri_ref[z, span, :] * (side_a - v)
+            hi, low = split_bf16(explicit)
+            start = pl.multiple_of(z * na + k * depth, depth)
+            ex_hi[c, pl.ds(start, depth), :] = hi
+            ex_lo[c, pl.ds(start, depth), :] = low
+        return carry
+
+    lax.fori_loop(0, columns * zb, per_slab, 0)
     th, tl = split_bf16(tb_ref[...])
-    pf_hi, pf_lo = split_bf16(pf)
+    pf_hi, pf_lo = split_bf16(pf_ref[...].reshape(rows, nb))
     price = jnp.dot(pf_lo, th, preferred_element_type=jnp.float32)
     price = price + jnp.dot(pf_hi, tl, preferred_element_type=jnp.float32)
     price = price + jnp.dot(pf_hi, th, preferred_element_type=jnp.float32)
 
     def per_column(c, carry):
-        v = vals_ref[c].reshape(rows, nb).astype(jnp.float32)
-        lo = jnp.broadcast_to(lo_ref[c][:, None, :], (zb, na, nb)).reshape(rows, nb)
-        up = jnp.broadcast_to(up_ref[c][:, None, :], (zb, na, nb)).reshape(rows, nb)
-        side_b = jnp.where(next_b, pltpu.roll(v, nb - 1, 1), jnp.where(prev_b, pltpu.roll(v, 1, 1), v))
-        above = jnp.where(top, up, pltpu.roll(v, rows - 1, 0))
-        below = jnp.where(bottom, lo, pltpu.roll(v, 1, 0))
-        side_a = jnp.where(ma, above, below)
-        explicit = v + rl * (side_b - v) + ri * (side_a - v)
-        hi, low = split_bf16(explicit)
-        acc = jnp.dot(low, th, preferred_element_type=jnp.float32)
+        hi = ex_hi[c]
+        acc = jnp.dot(ex_lo[c], th, preferred_element_type=jnp.float32)
         acc = acc + jnp.dot(hi, tl, preferred_element_type=jnp.float32)
         acc = acc + jnp.dot(hi, th, preferred_element_type=jnp.float32)
         out_ref[c] = (acc + load_ref[c] * price).reshape(zb, na, kb)
@@ -99,6 +114,7 @@
         ],
         out_specs=pl.BlockSpec((columns, zb, na, kb), lambda j: (0, j, 0, 0)),
         out_shape=jax.ShapeDtypeStruct((columns, nz, na, kb), jnp.float32),
+        scratch_shapes=[pltpu.VMEM((columns, zb * na, nb), jnp.bfloat16)] * 2,
         compiler_params=pltpu.CompilerParams(vmem_limit_bytes=56 * 1024 * 1024),
     )(load, vals, lower, upper, rl, ri, pf, ml, mi, tb)
 

time: 156 us -> 169 us (1.083)
  Pallas kernels: 89.9 us -> 103 us
    pallas_call x1, Pallas kernels: 51 us -> 64.2 us  [liquid_step(): pl.pallas_call(step_kernel, grid=(nz // zb,), in_specs=[pl.BlockSpec(memo...]
  transfers between devices with their start and end apart: 5 -> 5, of which waited for: 5 -> 5; matrix products, arithmetic and copies ran while one was open for 6% -> 5% of each run, Pallas kernels for 0% -> 0%
where the time goes in v7:
time: 169 us; the launch traced here: 168 us
  Pallas kernels  103 us (61%)
  local copies, waits for them, and re-layouts  22.7 us (13%)
  waiting for transfers between devices  16.8 us (10%)
  other arithmetic  12.8 us (8%)
  starting transfers between devices  10.5 us (6%)
  matrix products  1.77 us (1%)
    pallas_call x1, Pallas kernels, liquid_step(): pl.pallas_call(step_kernel, grid=(nz // zb,), in_specs=[pl.BlockSpec(memo...  64.2 us
    pallas_call x1, Pallas kernels, illiquid_pick(): pl.pallas_call(illiquid_kernel, grid_spec=pltpu.PrefetchScalarGridSpec(nu...  38.9 us
    ppermute x3, waiting for transfers between devices, all_sum(): x = x + lax.ppermute(x, axis, [(i, i ^ step) for i in range(count)])  10.9 us
    reshape x1, local copies, waits for them, and re-layouts, body(): jnp.transpose(liquid_part, (3, 2, 0, 1))  9.24 us
    pallas_call x1, local copies, waits for them, and re-layouts, illiquid_pick(): pl.pallas_call(illiquid_kernel, grid_spec=pltpu.PrefetchScalarGridSpec(nu...  5.67 us
    ppermute x3, starting transfers between devices, all_sum(): x = x + lax.ppermute(x, axis, [(i, i ^ step) for i in range(count)])  5.6 us
    ppermute x1, starting transfers between devices, edges(): lax.ppermute(tail, axis, [(i, (i + 1) % count) for i in range(ends)])  3.64 us
  transfers between devices with their start and end apart: 5, of which 5 were waited for; matrix products, arithmetic and copies ran while one was open for 5% of the time, Pallas kernels for 0%

profile of v7, /device:TPU:0, one launch (start us, length us, event | category | flops | bytes accessed | tf_op | source)
XLA Modules:
  0.0 167.9 jit_solution(15790183847205509578)
XLA Ops:
  0.0 3.3 %fusion.39 = (bf16[8,32,1,512]{3,2,1,0:T(2,128)(2,1)S(1)}, bf16[8,32,1,512]{3,2,1,0:T(2,128)(2,1)S(1)}) fusion(bf16[8,32,64,512]{3,2,1,0:T(8,128)(2,1)} %vals_ref.1), kind=kLoop, calls=%fused_computation.80 | loop fusion | bytes 1048576 | tf_op jit(solution)/shard_map/slice | solution.py:168
  3.4 1.3 collective-permute-start.1
  5.9 0.6 broadcast_clamp_fusion
  6.6 1.8 %convert_reduce_fusion = s32[1024]{0:T(1024)S(1)} fusion(s32[4096]{0:T(1024)S(1)} %add_bitcast_fusion, s32[1024]{0:T(1024)S(1)} %iota_add_fusion), kind=kLoop, calls=%fused_computation.1 | loop fusion | flops 12581888 | bytes 24576 | tf_op jit(solution)/shard_map/reduce_sum | solution.py:216
  8.7 1.4 fusion
  10.1 1.3 fusion.12.ca_ref
  12.0 2.7 %collective-permute-done.1 = bf16[8,32,512]{2,1,0:T(8,128)(2,1)} collective-permute-done((bf16[8,32,512]{2,1,0:T(8,128)(2,1)S(1)}, bf16[8,32,512]{2,1,0:T(8,128)(2,1)}, u32[]{:S(2)}, u32[]{:S(2)}) %collective-permute-start.1) | collective-permute-done | bytes 262176 | tf_op jit(solution)/shard_map/ppermute | solution.py:170
  14.7 1.9 %select_convert_fusion = (f32[8,32,512]{2,1,0:T(8,128)}, bf16[8,32,512]{2,1,0:T(8,128)(2,1)S(1)}) fusion(bf16[8,32,512]{2,1,0:T(8,128)(2,1)} %collective-permute-done.1, pred[]{:T(512)S(6)} %eq.69, bf16[8,32,1,512]{3,2,1,0:T(2,128)(2,1)S(1)} %get-tuple-element.7), kind=kLoop, calls=%fused_computation.23 | loop fusion | flops 262144 | bytes 1310721 | tf_op jit(solution)/shard_map/convert_element_type | solution.py:172
  16.6 3.6 %collective-permute-start = (bf16[8,32,512]{2,1,0:T(8,128)(2,1)S(1)}, bf16[8,32,512]{2,1,0:T(8,128)(2,1)S(1)}, u32[]{:S(2)}, u32[]{:S(2)}) collective-permute-start(bf16[8,32,512]{2,1,0:T(8,128)(2,1)S(1)} %get-tuple-element.6), channel_id=1, source_target_pairs={{0,4},{4,8},{8,12},{1,5},{5,9},{9,13},{2,6},{6,10},{10,14},{3,7},{... | collective-permute-start | bytes 786440 | tf_op jit(solution)/shard_map/ppermute | solution.py:169
  20.3 1.6 fusion.8.tb_ref
  21.9 3.1 %collective-permute-done = bf16[8,32,512]{2,1,0:T(8,128)(2,1)S(1)} collective-permute-done((bf16[8,32,512]{2,1,0:T(8,128)(2,1)S(1)}, bf16[8,32,512]{2,1,0:T(8,128)(2,1)S(1)}, u32[]{:S(2)}, u32[]{:S(2)}) %collective-permute-start) | collective-permute-done | bytes 262176 | tf_op jit(solution)/shard_map/ppermute | solution.py:169
  25.0 0.9 select_convert_fusion.1.lo_ref
  25.9 64.2 %shard_map.118 = f32[8,32,64,128]{3,2,1,0:T(8,128)} custom-call(f32[8]{0:T(128)} %load_ref.1, bf16[8,32,64,512]{3,2,1,0:T(8,128)(2,1)} %vals_ref.1, f32[8,32,512]{2,1,0:T(8,128)} %select_convert_fusion.1.lo_ref, f32[8,32,512]{2,1,0:T(8,128)} %get-tuple-element.5.up_ref, f32[32,64,512]{2,1,0:T(8,128)} %rl_ref.1, f32[32,64,512]{2,1,0:T(8,128)} %ri_ref.1, ...), custom_call_target="tpu_custom_call" | custom-call | tf_op jit(solution)/shard_map/pallas_call | solution.py:100
  90.0 9.2 %copy.53.t_ref = f32[128,64,256]{2,1,0:T(8,128)} copy(f32[128,64,256]{0,1,2:T(8,128)} %bitcast.26) | data formatting | bytes 16777216 | tf_op jit(solution)/shard_map/reshape | solution.py:199
  99.3 38.9 %shard_map.119 = f32[4096,256]{1,0:T(8,128)} custom-call(s32[4096]{0:T(1024)} %get-tuple-element.16.kb_ref, s32[4096]{0:T(1024)} %get-tuple-element.15.ka_ref, f32[256,64]{1,0:T(8,128)} %fusion.12.ca_ref, f32[128,64,256]{2,1,0:T(8,128)} %copy.53.t_ref), custom_call_target="tpu_custom_call" | custom-call | tf_op jit(solution)/shard_map/pallas_call | solution.py:146
  138.2 5.7 %copy.54 = f32[4096,256]{0,1:T(8,128)} copy(f32[4096,256]{1,0:T(8,128)} %shard_map.119) | data formatting | bytes 8388608 | tf_op jit(solution)/shard_map/pallas_call | solution.py:146
  143.8 2.8 %multiply_reduce_fusion = f32[4096,8]{0,1:T(8,128)S(1)} fusion(f32[4096,32]{0,1:T(8,128)S(1)} %fusion, f32[4096,256]{0,1:T(8,128)} %copy.54), kind=kLoop, calls=%fused_computation.2 | loop fusion | flops 2064384 | bytes 4849664 | tf_op jit(solution)/shard_map/reduce_sum | solution.py:208
  146.8 1.3 collective-permute-done.2
  148.1 2.6 %collective-permute-start.3 = (f32[8,4096]{1,0:T(8,128)S(1)}, f32[8,4096]{1,0:T(8,128)S(1)}, u32[]{:S(2)}, u32[]{:S(2)}) collective-permute-start(f32[8,4096]{1,0:T(8,128)S(1)} %bitcast_add_fusion), channel_id=1, source_target_pairs={{0,4},{4,0},{8,12},{12,8},{1,5},{5,1},{9,13},{13,9},{2,6},{6,2},{1... | collective-permute-start | bytes 393224 | tf_op jit(solution)/shard_map/ppermute | solution.py:226
  150.7 3.8 %collective-permute-done.3 = f32[8,4096]{1,0:T(8,128)S(1)} collective-permute-done((f32[8,4096]{1,0:T(8,128)S(1)}, f32[8,4096]{1,0:T(8,128)S(1)}, u32[]{:S(2)}, u32[]{:S(2)}) %collective-permute-start.3) | collective-permute-done | bytes 131104 | tf_op jit(solution)/shard_map/ppermute | solution.py:226
  154.5 3.0 %collective-permute-start.4 = (f32[8,4096]{1,0:T(8,128)S(1)}, f32[8,4096]{1,0:T(8,128)S(1)}, u32[]{:S(2)}, u32[]{:S(2)}) collective-permute-start(f32[8,4096]{1,0:T(8,128)S(1)} %add.112), channel_id=1, source_target_pairs={{0,8},{4,12},{8,0},{12,4},{1,9},{5,13},{9,1},{13,5},{2,10},{6,14},... | collective-permute-start | bytes 393224 | tf_op jit(solution)/shard_map/ppermute | solution.py:226
  157.5 5.8 %collective-permute-done.4 = f32[8,4096]{1,0:T(8,128)S(1)} collective-permute-done((f32[8,4096]{1,0:T(8,128)S(1)}, f32[8,4096]{1,0:T(8,128)S(1)}, u32[]{:S(2)}, u32[]{:S(2)}) %collective-permute-start.4) | collective-permute-done | bytes 131104 | tf_op jit(solution)/shard_map/ppermute | solution.py:226
  163.9 2.8 %gather_fusion = f32[1024,8]{1,0:T(8,128)S(1)} fusion(f32[8,4096]{0,1:T(8,128)S(1)} %copy.55, s32[1024]{0:T(1024)S(1)} %broadcast_clamp_fusion.2), kind=kCustom, calls=%fused_computation | custom fusion | bytes 69632 | tf_op jit(solution)/shard_map/jit(_take)/gather | solution.py:217
  167.1 0.8 copy.56
  (42 shorter events, 3.2 us)
Async XLA Ops:
  0.0 8.3 %copy-start = (f32[64,64]{1,0:T(8,128)S(1)}, f32[64,64]{1,0:T(8,128)}, u32[]{:S(2)}) copy-start(f32[64,64]{1,0:T(8,128)} %param.19) | copy-start | bytes 49156
  0.0 5.3 %copy-start.2 = (s32[4096]{0:T(1024)S(1)}, s32[4096]{0:T(1024)}, u32[]{:S(2)}) copy-start(s32[4096]{0:T(1024)} %param.23) | copy-start | bytes 49156
  0.0 5.9 %copy-start.4 = (s32[4096]{0:T(1024)S(1)}, s32[4096]{0:T(1024)}, u32[]{:S(2)}) copy-start(s32[4096]{0:T(1024)} %param.20) | copy-start | bytes 49156
  0.0 5.9 %copy-start.3 = (s32[4096]{0:T(1024)S(1)}, s32[4096]{0:T(1024)}, u32[]{:S(2)}) copy-start(s32[4096]{0:T(1024)} %param.21) | copy-start | bytes 49156
  0.0 8.7 %copy-start.5 = (s32[4096]{0:T(1024)S(1)}, s32[4096]{0:T(1024)}, u32[]{:S(2)}) copy-start(s32[4096]{0:T(1024)} %param.22) | copy-start | bytes 49156
  3.4 11.3 %collective-permute-start.1 = (bf16[8,32,512]{2,1,0:T(8,128)(2,1)S(1)}, bf16[8,32,512]{2,1,0:T(8,128)(2,1)}, u32[]{:S(2)}, u32[]{:S(2)}) collective-permute-start(bf16[8,32,512]{2,1,0:T(8,128)(2,1)S(1)} %bitcast.28), channel_id=1, source_target_pairs={{4,0},{8,4},{12,8},{5,1},{9,5},{13,9},{6,2},{10,6},{14,10},{7,3},{... | collective-permute-start | bytes 786440 | tf_op jit(solution)/shard_map/ppermute | solution.py:170
  16.6 8.4 %collective-permute-start = (bf16[8,32,512]{2,1,0:T(8,128)(2,1)S(1)}, bf16[8,32,512]{2,1,0:T(8,128)(2,1)S(1)}, u32[]{:S(2)}, u32[]{:S(2)}) collective-permute-start(bf16[8,32,512]{2,1,0:T(8,128)(2,1)S(1)} %get-tuple-element.6), channel_id=1, source_target_pairs={{0,4},{4,8},{8,12},{1,5},{5,9},{9,13},{2,6},{6,10},{10,14},{3,7},{... | collective-permute-start | bytes 786440 | tf_op jit(solution)/shard_map/ppermute | solution.py:169
  138.2 29.7 %copy-start.1 = (f32[64,64]{1,0:T(8,128)S(1)}, f32[64,64]{1,0:T(8,128)}, u32[]{:S(2)}) copy-start(f32[64,64]{1,0:T(8,128)} %param.19) | copy-start | bytes 49156
  146.7 1.4 collective-permute-start.2
  148.1 6.4 %collective-permute-start.3 = (f32[8,4096]{1,0:T(8,128)S(1)}, f32[8,4096]{1,0:T(8,128)S(1)}, u32[]{:S(2)}, u32[]{:S(2)}) collective-permute-start(f32[8,4096]{1,0:T(8,128)S(1)} %bitcast_add_fusion), channel_id=1, source_target_pairs={{0,4},{4,0},{8,12},{12,8},{1,5},{5,1},{9,13},{13,9},{2,6},{6,2},{1... | collective-permute-start | bytes 393224 | tf_op jit(solution)/shard_map/ppermute | solution.py:226
  154.5 8.8 %collective-permute-start.4 = (f32[8,4096]{1,0:T(8,128)S(1)}, f32[8,4096]{1,0:T(8,128)S(1)}, u32[]{:S(2)}, u32[]{:S(2)}) collective-permute-start(f32[8,4096]{1,0:T(8,128)S(1)} %add.112), channel_id=1, source_target_pairs={{0,8},{4,12},{8,0},{12,4},{1,9},{5,13},{9,1},{13,5},{2,10},{6,14},... | collective-permute-start | bytes 393224 | tf_op jit(solution)/shard_map/ppermute | solution.py:226

commit v8 on v6

--- a/solution.py
+++ b/solution.py
@@ -1,4 +1,5 @@
 import functools
+import numpy as np
 import jax
 import jax.numpy as jnp
 from jax import lax
@@ -20,6 +21,14 @@
     angle = jnp.pi * phase.astype(jnp.float32) / (2.0 * count)
     first = jnp.where(freq == 0, jnp.sqrt(jnp.float32(0.5)), jnp.float32(1.0))
     return jnp.cos(angle) * jnp.sqrt(jnp.float32(2.0 / count)) * first
+
+
+def cosine_constant(count):
+    freq = np.arange(count)[:, None]
+    cell = np.arange(count)[None, :]
+    table = np.cos(np.pi * ((2 * cell + 1) * freq % (4 * count)) / (2.0 * count)) * np.sqrt(2.0 / count)
+    table[0] *= np.sqrt(0.5)
+    return table.astype(np.float32)
 
 
 def slot_targets(owner, owners, capacity):
@@ -175,17 +184,29 @@
     columns, nz_loc, na_loc, _ = values_in.shape
     wide_pos = lax.axis_index("wide")
     inc_pos = lax.axis_index("inc")
+    head = values_in[:, :, 0, :].astype(jnp.float32)
+    tail = values_in[:, :, na_loc - 1, :].astype(jnp.float32)
     lower, upper = edges(values_in, "wide", 2)
+    table_b = cosine_constant(NB)[:KBLOW]
     liquid_part = liquid_step(
-        shock_load, values_in, lower, upper, rate_liquid, rate_illiquid, price_field,
-        mask_liquid, mask_illiquid, cosine_table(NB)[:KBLOW].T,
-    )
+        shock_load, values_in, head, tail, rate_liquid, rate_illiquid, price_field,
+        mask_liquid, mask_illiquid, jnp.asarray(table_b.T),
+    )
+    rim = jnp.stack(
+        [
+            jnp.where(mask_illiquid[:, 0, :] == 0, rate_illiquid[:, 0, :] * (lower - head), 0.0),
+            jnp.where(mask_illiquid[:, na_loc - 1, :] != 0, rate_illiquid[:, na_loc - 1, :] * (upper - tail), 0.0),
+        ],
+        axis=2,
+    )
+    rim = jnp.einsum("kb,czeb->czek", jnp.asarray(table_b), rim, precision=high)
+    liquid_part = liquid_part.at[:, :, 0, :].add(rim[:, :, 0]).at[:, :, na_loc - 1, :].add(rim[:, :, 1])
     liquid_part = jnp.transpose(liquid_part, (3, 2, 0, 1)).reshape(KBLOW, na_loc, columns * nz_loc)
-    table_a = lax.dynamic_slice_in_dim(cosine_table(NA), wide_pos * na_loc, na_loc, axis=1)
+    table_a = lax.dynamic_slice_in_dim(jnp.asarray(cosine_constant(NA)), wide_pos * na_loc, na_loc, axis=1)
     picked = illiquid_pick(
         table_a, liquid_part, jnp.clip(coef_liquid, 0, KBLOW - 1), jnp.clip(coef_illiquid, 0, NA - 1)
     )
-    folded = jnp.dot(cosine_table(NZ), jump_inverse, precision=lax.Precision.HIGHEST)
+    folded = jnp.dot(jnp.asarray(cosine_constant(NZ)), jump_inverse, precision=lax.Precision.HIGHEST)
     folded = lax.dynamic_slice_in_dim(folded, inc_pos * nz_loc, nz_loc, axis=1)
     pick_z = (coef_income[:, None] == jnp.arange(NZ, dtype=jnp.int32)[None, :]).astype(jnp.float32)
     weight = jnp.dot(pick_z, folded, precision=lax.Precision.HIGHEST)

time: 156 us -> 163 us (1.045)
  local copies, waits for them, and re-layouts: 22.7 us -> 34.9 us
  waiting for transfers between devices: 16.6 us -> 11.1 us
    scatter-add x0 -> x2, local copies, waits for them, and re-layouts: none -> 9.03 us  [body(): liquid_part.at[:, :, 0, :].add(rim[:, :, 0]).at[:, :, na_loc - 1, :]]
    ppermute x1, waiting for transfers between devices: 2.92 us -> 0.01 us  [edges(): lax.ppermute(tail, axis, [(i, (i + 1) % count) for i in range(ends)])]
    ppermute x1, waiting for transfers between devices: 2.73 us -> 0.01 us  [edges(): lax.ppermute(head, axis, [((i + 1) % count, i) for i in range(ends)])]
    add x3 -> x2, other arithmetic: 0.01 us -> 2.74 us  [body(): liquid_part.at[:, :, 0, :].add(rim[:, :, 0]).at[:, :, na_loc - 1, :]]
    slice x3 -> x4, local copies, waits for them, and re-layouts: 3.4 us -> 5.76 us  [the longest x1 3.1 us: body(): head = values_in[:, :, 0, :].astype(jnp.float32)]
  transfers between devices with their start and end apart: 5 -> 5, of which waited for: 5 -> 3; matrix products, arithmetic and copies ran while one was open for 6% -> 6% of each run, Pallas kernels for 0% -> 31%
where the time goes in v8:
time: 163 us; the launch traced here: 162 us
  Pallas kernels  89.9 us (55%)
  local copies, waits for them, and re-layouts  34.9 us (21%)
  starting transfers between devices  12 us (7%)
  other arithmetic  11.5 us (7%)
  waiting for transfers between devices  11.1 us (7%)
  matrix products  2.26 us (1%)
    pallas_call x1, Pallas kernels, liquid_step(): pl.pallas_call(step_kernel, grid=(nz // zb,), in_specs=[pl.BlockSpec(memo...  51 us
    pallas_call x1, Pallas kernels, illiquid_pick(): pl.pallas_call(illiquid_kernel, grid_spec=pltpu.PrefetchScalarGridSpec(nu...  38.9 us
    ppermute x3, waiting for transfers between devices, all_sum(): x = x + lax.ppermute(x, axis, [(i, i ^ step) for i in range(count)])  11.1 us
    reshape x1, local copies, waits for them, and re-layouts, body(): jnp.transpose(liquid_part, (3, 2, 0, 1))  9.25 us
    scatter-add x2, local copies, waits for them, and re-layouts, body(): liquid_part.at[:, :, 0, :].add(rim[:, :, 0]).at[:, :, na_loc - 1, :]  9.03 us
    pallas_call x1, local copies, waits for them, and re-layouts, illiquid_pick(): pl.pallas_call(illiquid_kernel, grid_spec=pltpu.PrefetchScalarGridSpec(nu...  5.64 us
    ppermute x3, starting transfers between devices, all_sum(): x = x + lax.ppermute(x, axis, [(i, i ^ step) for i in range(count)])  5.59 us
    ppermute x1, starting transfers between devices, edges(): lax.ppermute(tail, axis, [(i, (i + 1) % count) for i in range(ends)])  4.95 us
  transfers between devices with their start and end apart: 5, of which 3 were waited for; matrix products, arithmetic and copies ran while one was open for 6% of the time, Pallas kernels for 31%

profile of v8, /device:TPU:0, one launch (start us, length us, event | category | flops | bytes accessed | tf_op | source)
XLA Modules:
  0.0 162.0 jit_solution(2816562595243512012)
XLA Ops:
  0.0 3.1 %fusion.9 = (bf16[8,32,1,512]{3,2,1,0:T(2,128)(2,1)S(1)}, bf16[8,32,1,512]{3,2,1,0:T(2,128)(2,1)S(1)}) fusion(bf16[8,32,64,512]{3,2,1,0:T(8,128)(2,1)} %vals_ref.1), kind=kLoop, calls=%fused_computation.39 | loop fusion | bytes 1048576 | tf_op jit(solution)/shard_map/slice | solution.py:187
  3.1 0.9 fusion.8
  4.0 4.9 %collective-permute-start = (bf16[8,32,512]{2,1,0:T(8,128)(2,1)S(1)}, bf16[8,32,512]{2,1,0:T(8,128)(2,1)S(1)}, u32[]{:S(2)}, u32[]{:S(2)}) collective-permute-start(bf16[8,32,512]{2,1,0:T(8,128)(2,1)S(1)} %get-tuple-element.32), channel_id=1, source_target_pairs={{0,4},{4,8},{8,12},{1,5},{5,9},{9,13},{2,6},{6,10},{10,14},{3,7},{... | collective-permute-start | bytes 786440 | tf_op jit(solution)/shard_map/ppermute | solution.py:162
  9.0 1.3 fusion.11
  10.3 1.3 fusion.10
  13.6 1.8 %convert_reduce_fusion = s32[1024]{0:T(1024)S(1)} fusion(s32[4096]{0:T(1024)S(1)} %add_bitcast_fusion, s32[1024]{0:T(1024)S(1)} %iota_add_fusion), kind=kLoop, calls=%fused_computation.1 | loop fusion | flops 12581888 | bytes 24576 | tf_op jit(solution)/shard_map/reduce_sum | solution.py:221
  15.9 1.5 collective-permute-start.1
  18.1 1.4 fusion
  19.6 0.9 convert_element_type.18.lo_ref
  20.4 51.0 %shard_map.154 = f32[8,32,64,128]{3,2,1,0:T(8,128)} custom-call(f32[8]{0:T(128)} %load_ref.1, bf16[8,32,64,512]{3,2,1,0:T(8,128)(2,1)} %vals_ref.1, f32[8,32,512]{2,1,0:T(8,128)} %convert_element_type.18.lo_ref, f32[8,32,512]{2,1,0:T(8,128)} %get-tuple-element.31.up_ref, f32[32,64,512]{2,1,0:T(8,128)} %rl_ref.1, f32[32,64,512]{2,1,0:T(8,128)} %ri_ref.1, ...), custom_call_target="tpu_custom_call" | custom-call | tf_op jit(solution)/shard_map/pallas_call | solution.py:94
  72.2 1.3 slice_add_fusion.1
  73.6 4.5 %scatter-add.6 = f32[8,32,64,128]{3,2,1,0:T(8,128)} dynamic-update-slice(f32[8,32,64,128]{3,2,1,0:T(8,128)} %shard_map.154, f32[8,32,1,128]{3,2,1,0:T(1,128)S(1)} %slice_add_fusion.1, s32[]{:T(128)} %constant.99.clone.1, s32[]{:T(128)} %constant.99.clone.1, s32[]{:T(128)} %constant.99.clone.1, s32[]{:T(128)} %constant.99.clone.1) | dynamic-update-slice | bytes 262148 | tf_op jit(solution)/shard_map/scatter-add | solution.py:203
  78.1 1.4 slice_add_fusion
  79.5 4.5 %scatter-add.9 = f32[8,32,64,128]{3,2,1,0:T(8,128)} dynamic-update-slice(f32[8,32,64,128]{3,2,1,0:T(8,128)} %scatter-add.6, f32[8,32,1,128]{3,2,1,0:T(1,128)S(1)} %slice_add_fusion, s32[]{:T(128)} %constant.99.clone.1, s32[]{:T(128)} %constant.99.clone.1, s32[]{:T(128)} %constant.109.clone.1, s32[]{:T(128)} %constant.99.clone.1) | dynamic-update-slice | bytes 262148 | tf_op jit(solution)/shard_map/scatter-add | solution.py:203
  84.0 9.2 %copy.88.t_ref = f32[128,64,256]{2,1,0:T(8,128)} copy(f32[128,64,256]{0,1,2:T(8,128)} %bitcast.43) | data formatting | bytes 16777216 | tf_op jit(solution)/shard_map/reshape | solution.py:204
  93.2 38.9 %shard_map.155 = f32[4096,256]{1,0:T(8,128)} custom-call(s32[4096]{0:T(1024)} %get-tuple-element.44.kb_ref, s32[4096]{0:T(1024)} %get-tuple-element.43.ka_ref, f32[256,64]{1,0:T(8,128)} %constant_dynamic-slice_fusion.ca_ref, f32[128,64,256]{2,1,0:T(8,128)} %copy.88.t_ref), custom_call_target="tpu_custom_call" | custom-call | tf_op jit(solution)/shard_map/pallas_call | solution.py:139
  132.1 5.6 %copy.89 = f32[4096,256]{0,1:T(8,128)} copy(f32[4096,256]{1,0:T(8,128)} %shard_map.155) | data formatting | bytes 8388608 | tf_op jit(solution)/shard_map/pallas_call | solution.py:139
  137.8 2.8 %multiply_reduce_fusion = f32[4096,8]{0,1:T(8,128)S(1)} fusion(f32[4096,32]{0,1:T(8,128)S(1)} %fusion, f32[4096,256]{0,1:T(8,128)} %copy.89), kind=kLoop, calls=%fused_computation.2 | loop fusion | flops 2064384 | bytes 4849664 | tf_op jit(solution)/shard_map/reduce_sum | solution.py:213
  140.7 1.3 collective-permute-done.2
  142.1 2.7 %collective-permute-start.3 = (f32[8,4096]{1,0:T(8,128)S(1)}, f32[8,4096]{1,0:T(8,128)S(1)}, u32[]{:S(2)}, u32[]{:S(2)}) collective-permute-start(f32[8,4096]{1,0:T(8,128)S(1)} %bitcast_add_fusion), channel_id=1, source_target_pairs={{0,4},{4,0},{8,12},{12,8},{1,5},{5,1},{9,13},{13,9},{2,6},{6,2},{1... | collective-permute-start | bytes 393224 | tf_op jit(solution)/shard_map/ppermute | solution.py:231
  144.8 3.8 %collective-permute-done.3 = f32[8,4096]{1,0:T(8,128)S(1)} collective-permute-done((f32[8,4096]{1,0:T(8,128)S(1)}, f32[8,4096]{1,0:T(8,128)S(1)}, u32[]{:S(2)}, u32[]{:S(2)}) %collective-permute-start.3) | collective-permute-done | bytes 131104 | tf_op jit(solution)/shard_map/ppermute | solution.py:231
  148.6 2.8 %collective-permute-start.4 = (f32[8,4096]{1,0:T(8,128)S(1)}, f32[8,4096]{1,0:T(8,128)S(1)}, u32[]{:S(2)}, u32[]{:S(2)}) collective-permute-start(f32[8,4096]{1,0:T(8,128)S(1)} %add.68), channel_id=1, source_target_pairs={{0,8},{4,12},{8,0},{12,4},{1,9},{5,13},{9,1},{13,5},{2,10},{6,14},... | collective-permute-start | bytes 393224 | tf_op jit(solution)/shard_map/ppermute | solution.py:231
  151.4 6.0 %collective-permute-done.4 = f32[8,4096]{1,0:T(8,128)S(1)} collective-permute-done((f32[8,4096]{1,0:T(8,128)S(1)}, f32[8,4096]{1,0:T(8,128)S(1)}, u32[]{:S(2)}, u32[]{:S(2)}) %collective-permute-start.4) | collective-permute-done | bytes 131104 | tf_op jit(solution)/shard_map/ppermute | solution.py:231
  158.0 2.8 %gather_fusion = f32[1024,8]{1,0:T(8,128)S(1)} fusion(f32[8,4096]{0,1:T(8,128)S(1)} %copy.90, s32[1024]{0:T(1024)S(1)} %broadcast_clamp_fusion.2), kind=kCustom, calls=%fused_computation | custom fusion | bytes 69632 | tf_op jit(solution)/shard_map/jit(_take)/gather | solution.py:222
  (47 shorter events, 5.7 us)
Async XLA Ops:
  0.0 15.4 %copy-start = (f32[64,64]{1,0:T(8,128)S(1)}, f32[64,64]{1,0:T(8,128)}, u32[]{:S(2)}) copy-start(f32[64,64]{1,0:T(8,128)} %param.27) | copy-start | bytes 49156
  0.0 15.5 %copy-start.4 = (f32[64,64]{1,0:T(8,128)S(1)}, f32[64,64]{1,0:T(8,128)}, u32[]{:S(2)}) copy-start(f32[64,64]{1,0:T(8,128)} %constant.115.clone) | copy-start | bytes 49156
  0.0 17.3 %copy-start.3 = (f32[256,256]{1,0:T(8,128)S(1)}, f32[256,256]{1,0:T(8,128)}, u32[]{:S(2)}) copy-start(f32[256,256]{1,0:T(8,128)} %constant.114.clone) | copy-start | bytes 786436
  0.0 13.0 %copy-start.6 = (s32[4096]{0:T(1024)S(1)}, s32[4096]{0:T(1024)}, u32[]{:S(2)}) copy-start(s32[4096]{0:T(1024)} %param.28) | copy-start | bytes 49156
  0.0 13.0 %copy-start.5 = (s32[4096]{0:T(1024)S(1)}, s32[4096]{0:T(1024)}, u32[]{:S(2)}) copy-start(s32[4096]{0:T(1024)} %param.29) | copy-start | bytes 49156
  0.0 18.1 %copy-start.7 = (s32[4096]{0:T(1024)S(1)}, s32[4096]{0:T(1024)}, u32[]{:S(2)}) copy-start(s32[4096]{0:T(1024)} %param.30) | copy-start | bytes 49156
  4.0 11.7 %collective-permute-start = (bf16[8,32,512]{2,1,0:T(8,128)(2,1)S(1)}, bf16[8,32,512]{2,1,0:T(8,128)(2,1)S(1)}, u32[]{:S(2)}, u32[]{:S(2)}) collective-permute-start(bf16[8,32,512]{2,1,0:T(8,128)(2,1)S(1)} %get-tuple-element.32), channel_id=1, source_target_pairs={{0,4},{4,8},{8,12},{1,5},{5,9},{9,13},{2,6},{6,10},{10,14},{3,7},{... | collective-permute-start | bytes 786440 | tf_op jit(solution)/shard_map/ppermute | solution.py:162
  15.9 55.6 %collective-permute-start.1 = (bf16[8,32,512]{2,1,0:T(8,128)(2,1)S(1)}, bf16[8,32,512]{2,1,0:T(8,128)(2,1)S(1)}, u32[]{:S(2)}, u32[]{:S(2)}) collective-permute-start(bf16[8,32,512]{2,1,0:T(8,128)(2,1)S(1)} %get-tuple-element.30), channel_id=1, source_target_pairs={{4,0},{8,4},{12,8},{5,1},{9,5},{13,9},{6,2},{10,6},{14,10},{7,3},{... | collective-permute-start | bytes 786440 | tf_op jit(solution)/shard_map/ppermute | solution.py:163
  20.4 51.1 %copy-start.2 = (f32[128,512,1,1]{1,0,3,2:T(8,128)S(1)}, f32[128,512,1,1]{1,0,3,2:T(8,128)}, u32[]{:S(2)}) copy-start(f32[128,512,1,1]{1,0,3,2:T(8,128)} %constant.116) | copy-start | bytes 786436
  132.1 29.8 %copy-start.1 = (f32[64,64]{1,0:T(8,128)S(1)}, f32[64,64]{1,0:T(8,128)}, u32[]{:S(2)}) copy-start(f32[64,64]{1,0:T(8,128)} %param.27) | copy-start | bytes 49156
  140.6 1.4 collective-permute-start.2
  142.1 6.5 %collective-permute-start.3 = (f32[8,4096]{1,0:T(8,128)S(1)}, f32[8,4096]{1,0:T(8,128)S(1)}, u32[]{:S(2)}, u32[]{:S(2)}) collective-permute-start(f32[8,4096]{1,0:T(8,128)S(1)} %bitcast_add_fusion), channel_id=1, source_target_pairs={{0,4},{4,0},{8,12},{12,8},{1,5},{5,1},{9,13},{13,9},{2,6},{6,2},{1... | collective-permute-start | bytes 393224 | tf_op jit(solution)/shard_map/ppermute | solution.py:231
  148.6 8.8 %collective-permute-start.4 = (f32[8,4096]{1,0:T(8,128)S(1)}, f32[8,4096]{1,0:T(8,128)S(1)}, u32[]{:S(2)}, u32[]{:S(2)}) collective-permute-start(f32[8,4096]{1,0:T(8,128)S(1)} %add.68), channel_id=1, source_target_pairs={{0,8},{4,12},{8,0},{12,4},{1,9},{5,13},{9,1},{13,5},{2,10},{6,14},... | collective-permute-start | bytes 393224 | tf_op jit(solution)/shard_map/ppermute | solution.py:231

commit v9 on v8

--- a/solution.py
+++ b/solution.py
@@ -112,12 +112,15 @@
     )(load, vals, lower, upper, rl, ri, pf, ml, mi, tb)
 
 
-def illiquid_kernel(kb_ref, ka_ref, ca_ref, t_ref, out_ref, spectrum):
+def illiquid_kernel(kb_ref, ka_ref, ca_ref, t_ref, rim_ref, out_ref, spectrum):
     j = pl.program_id(0)
-    block = t_ref.shape[0]
+    block, na_loc, lanes = t_ref.shape
     ch, cl = split_bf16(ca_ref[...])
+    row = lax.broadcasted_iota(jnp.int32, (na_loc, lanes), 0)
     for k in range(block):
-        th, tl = split_bf16(t_ref[k])
+        rim = rim_ref[k]
+        t = t_ref[k] + jnp.where(row == 0, rim[0:1], 0.0)
+        th, tl = split_bf16(t + jnp.where(row == na_loc - 1, rim[1:2], 0.0))
         acc = jnp.dot(cl, th, preferred_element_type=jnp.float32)
         acc = acc + jnp.dot(ch, tl, preferred_element_type=jnp.float32)
         spectrum[j * block + k] = acc + jnp.dot(ch, th, preferred_element_type=jnp.float32)
@@ -131,7 +134,7 @@
         lax.fori_loop(0, out_ref.shape[0], pick, 0, unroll=8)
 
 
-def illiquid_pick(ca, t, kb_index, ka_index):
+def illiquid_pick(ca, t, rim, kb_index, ka_index):
     kb, na_loc, lanes = t.shape
     na = ca.shape[0]
     count = kb_index.shape[0]
@@ -144,13 +147,14 @@
             in_specs=[
                 pl.BlockSpec((na, na_loc), lambda j, *_: (0, 0)),
                 pl.BlockSpec((block, na_loc, lanes), lambda j, *_: (j, 0, 0)),
+                pl.BlockSpec((block, 2, lanes), lambda j, *_: (j, 0, 0)),
             ],
             out_specs=pl.BlockSpec((count, lanes), lambda j, *_: (0, 0)),
             scratch_shapes=[pltpu.VMEM((kb, na, lanes), jnp.float32)],
         ),
         out_shape=jax.ShapeDtypeStruct((count, lanes), jnp.float32),
         compiler_params=pltpu.CompilerParams(vmem_limit_bytes=60 * 1024 * 1024),
-    )(kb_index, ka_index, ca, t)
+    )(kb_index, ka_index, ca, t, rim)
 
 
 def edges(values, axis, dim):
@@ -200,11 +204,11 @@
         axis=2,
     )
     rim = jnp.einsum("kb,czeb->czek", jnp.asarray(table_b), rim, precision=high)
-    liquid_part = liquid_part.at[:, :, 0, :].add(rim[:, :, 0]).at[:, :, na_loc - 1, :].add(rim[:, :, 1])
+    rim = jnp.transpose(rim, (3, 2, 0, 1)).reshape(KBLOW, 2, columns * nz_loc)
     liquid_part = jnp.transpose(liquid_part, (3, 2, 0, 1)).reshape(KBLOW, na_loc, columns * nz_loc)
     table_a = lax.dynamic_slice_in_dim(jnp.asarray(cosine_constant(NA)), wide_pos * na_loc, na_loc, axis=1)
     picked = illiquid_pick(
-        table_a, liquid_part, jnp.clip(coef_liquid, 0, KBLOW - 1), jnp.clip(coef_illiquid, 0, NA - 1)
+        table_a, liquid_part, rim, jnp.clip(coef_liquid, 0, KBLOW - 1), jnp.clip(coef_illiquid, 0, NA - 1)
     )
     folded = jnp.dot(jnp.asarray(cosine_constant(NZ)), jump_inverse, precision=lax.Precision.HIGHEST)
     folded = lax.dynamic_slice_in_dim(folded, inc_pos * nz_loc, nz_loc, axis=1)

time: 163 us -> 152 us (0.933)
  local copies, waits for them, and re-layouts: 34.9 us -> 26.7 us
  other arithmetic: 11.5 us -> 8.78 us
    scatter-add x2 -> x0, local copies, waits for them, and re-layouts: 9.03 us -> none  [body(): liquid_part.at[:, :, 0, :].add(rim[:, :, 0]).at[:, :, na_loc - 1, :]]
    add x2 -> x0, other arithmetic: 2.74 us -> none  [body(): liquid_part.at[:, :, 0, :].add(rim[:, :, 0]).at[:, :, na_loc - 1, :]]
  transfers between devices with their start and end apart: 5 -> 5, of which waited for: 3 -> 3; matrix products, arithmetic and copies ran while one was open for 6% -> 13% of each run, Pallas kernels for 31% -> 34%
where the time goes in v9:
time: 152 us; the launch traced here: 151 us
  Pallas kernels  89.9 us (59%)
  local copies, waits for them, and re-layouts  26.7 us (18%)
  starting transfers between devices  11.8 us (8%)
  waiting for transfers between devices  11.1 us (7%)
  other arithmetic  8.78 us (6%)
  matrix products  2.26 us (1%)
    pallas_call x1, Pallas kernels, liquid_step(): pl.pallas_call(step_kernel, grid=(nz // zb,), in_specs=[pl.BlockSpec(memo...  50.9 us
    pallas_call x1, Pallas kernels, illiquid_pick(): pl.pallas_call(illiquid_kernel, grid_spec=pltpu.PrefetchScalarGridSpec(nu...  39 us
    ppermute x3, waiting for transfers between devices, all_sum(): x = x + lax.ppermute(x, axis, [(i, i ^ step) for i in range(count)])  11.1 us
    reshape x1, local copies, waits for them, and re-layouts, body(): jnp.transpose(liquid_part, (3, 2, 0, 1))  9.32 us
    pallas_call x1, local copies, waits for them, and re-layouts, illiquid_pick(): pl.pallas_call(illiquid_kernel, grid_spec=pltpu.PrefetchScalarGridSpec(nu...  5.64 us
    ppermute x3, starting transfers between devices, all_sum(): x = x + lax.ppermute(x, axis, [(i, i ^ step) for i in range(count)])  5.59 us
    ppermute x1, starting transfers between devices, edges(): lax.ppermute(tail, axis, [(i, (i + 1) % count) for i in range(ends)])  4.95 us
    slice x1, local copies, waits for them, and re-layouts, body(): head = values_in[:, :, 0, :].astype(jnp.float32)  3.1 us
  transfers between devices with their start and end apart: 5, of which 3 were waited for; matrix products, arithmetic and copies ran while one was open for 13% of the time, Pallas kernels for 34%

profile of v9, /device:TPU:0, one launch (start us, length us, event | category | flops | bytes accessed | tf_op | source)
XLA Modules:
  0.0 150.9 jit_solution(1656856644460600601)
XLA Ops:
  0.0 3.1 %fusion.8 = (bf16[8,32,1,512]{3,2,1,0:T(2,128)(2,1)S(1)}, bf16[8,32,1,512]{3,2,1,0:T(2,128)(2,1)S(1)}) fusion(bf16[8,32,64,512]{3,2,1,0:T(8,128)(2,1)} %vals_ref.1), kind=kLoop, calls=%fused_computation.37 | loop fusion | bytes 1048576 | tf_op jit(solution)/shard_map/slice | solution.py:191
  3.1 0.9 fusion.7
  4.0 4.9 %collective-permute-start = (bf16[8,32,512]{2,1,0:T(8,128)(2,1)S(1)}, bf16[8,32,512]{2,1,0:T(8,128)(2,1)S(1)}, u32[]{:S(2)}, u32[]{:S(2)}) collective-permute-start(bf16[8,32,512]{2,1,0:T(8,128)(2,1)S(1)} %get-tuple-element.8), channel_id=1, source_target_pairs={{0,4},{4,8},{8,12},{1,5},{5,9},{9,13},{2,6},{6,10},{10,14},{3,7},{... | collective-permute-start | bytes 786440 | tf_op jit(solution)/shard_map/ppermute | solution.py:166
  9.0 1.3 fusion.10
  10.3 1.3 fusion.9
  11.7 0.7 convert_bitcast_fusion
  13.6 1.8 %convert_reduce_fusion = s32[1024]{0:T(1024)S(1)} fusion(s32[4096]{0:T(1024)S(1)} %add_bitcast_fusion, s32[1024]{0:T(1024)S(1)} %iota_add_fusion), kind=kLoop, calls=%fused_computation.1 | loop fusion | flops 12581888 | bytes 24576 | tf_op jit(solution)/shard_map/reduce_sum | solution.py:225
  15.9 1.3 collective-permute-start.1
  17.2 0.8 constant_dynamic-slice_fusion.ca_ref
  17.9 1.4 fusion
  19.4 0.9 convert_element_type.18.lo_ref
  20.2 50.9 %shard_map.154 = f32[8,32,64,128]{3,2,1,0:T(8,128)} custom-call(f32[8]{0:T(128)} %load_ref.1, bf16[8,32,64,512]{3,2,1,0:T(8,128)(2,1)} %vals_ref.1, f32[8,32,512]{2,1,0:T(8,128)} %convert_element_type.18.lo_ref, f32[8,32,512]{2,1,0:T(8,128)} %get-tuple-element.7.up_ref, f32[32,64,512]{2,1,0:T(8,128)} %rl_ref.1, f32[32,64,512]{2,1,0:T(8,128)} %ri_ref.1, ...), custom_call_target="tpu_custom_call" | custom-call | tf_op jit(solution)/shard_map/pallas_call | solution.py:94
  71.2 9.3 %copy.86.t_ref = f32[128,64,256]{2,1,0:T(8,128)} copy(f32[128,64,256]{0,1,2:T(8,128)} %bitcast.44) | data formatting | bytes 16777216 | tf_op jit(solution)/shard_map/reshape | solution.py:208
  81.2 0.8 copy.87.rim_ref
  82.1 39.0 %shard_map.155 = f32[4096,256]{1,0:T(8,128)} custom-call(s32[4096]{0:T(1024)} %get-tuple-element.18.kb_ref, s32[4096]{0:T(1024)} %get-tuple-element.17.ka_ref, f32[256,64]{1,0:T(8,128)} %constant_dynamic-slice_fusion.ca_ref, f32[128,64,256]{2,1,0:T(8,128)} %copy.86.t_ref, f32[128,2,256]{2,1,0:T(2,128)} %copy.87.rim_ref), custom_call_target="tpu_custom_call" | custom-call | tf_op jit(solution)/shard_map/pallas_call | solution.py:142
  121.0 5.6 %copy.88 = f32[4096,256]{0,1:T(8,128)} copy(f32[4096,256]{1,0:T(8,128)} %shard_map.155) | data formatting | bytes 8388608 | tf_op jit(solution)/shard_map/pallas_call | solution.py:142
  126.7 2.8 %multiply_reduce_fusion = f32[4096,8]{0,1:T(8,128)S(1)} fusion(f32[4096,32]{0,1:T(8,128)S(1)} %fusion, f32[4096,256]{0,1:T(8,128)} %copy.88), kind=kLoop, calls=%fused_computation.2 | loop fusion | flops 2064384 | bytes 4849664 | tf_op jit(solution)/shard_map/reduce_sum | solution.py:217
  129.6 1.3 collective-permute-done.2
  131.0 2.7 %collective-permute-start.3 = (f32[8,4096]{1,0:T(8,128)S(1)}, f32[8,4096]{1,0:T(8,128)S(1)}, u32[]{:S(2)}, u32[]{:S(2)}) collective-permute-start(f32[8,4096]{1,0:T(8,128)S(1)} %bitcast_add_fusion), channel_id=1, source_target_pairs={{0,4},{4,0},{8,12},{12,8},{1,5},{5,1},{9,13},{13,9},{2,6},{6,2},{1... | collective-permute-start | bytes 393224 | tf_op jit(solution)/shard_map/ppermute | solution.py:235
  133.7 3.8 %collective-permute-done.3 = f32[8,4096]{1,0:T(8,128)S(1)} collective-permute-done((f32[8,4096]{1,0:T(8,128)S(1)}, f32[8,4096]{1,0:T(8,128)S(1)}, u32[]{:S(2)}, u32[]{:S(2)}) %collective-permute-start.3) | collective-permute-done | bytes 131104 | tf_op jit(solution)/shard_map/ppermute | solution.py:235
  137.5 2.8 %collective-permute-start.4 = (f32[8,4096]{1,0:T(8,128)S(1)}, f32[8,4096]{1,0:T(8,128)S(1)}, u32[]{:S(2)}, u32[]{:S(2)}) collective-permute-start(f32[8,4096]{1,0:T(8,128)S(1)} %add.52), channel_id=1, source_target_pairs={{0,8},{4,12},{8,0},{12,4},{1,9},{5,13},{9,1},{13,5},{2,10},{6,14},... | collective-permute-start | bytes 393224 | tf_op jit(solution)/shard_map/ppermute | solution.py:235
  140.3 6.0 %collective-permute-done.4 = f32[8,4096]{1,0:T(8,128)S(1)} collective-permute-done((f32[8,4096]{1,0:T(8,128)S(1)}, f32[8,4096]{1,0:T(8,128)S(1)}, u32[]{:S(2)}, u32[]{:S(2)}) %collective-permute-start.4) | collective-permute-done | bytes 131104 | tf_op jit(solution)/shard_map/ppermute | solution.py:235
  146.9 2.8 %gather_fusion = f32[1024,8]{1,0:T(8,128)S(1)} fusion(f32[8,4096]{0,1:T(8,128)S(1)} %copy.89, s32[1024]{0:T(1024)S(1)} %broadcast_clamp_fusion.2), kind=kCustom, calls=%fused_computation | custom fusion | bytes 69632 | tf_op jit(solution)/shard_map/jit(_take)/gather | solution.py:226
  150.1 0.8 copy.90
  (44 shorter events, 3.5 us)
Async XLA Ops:
  0.0 15.4 %copy-start = (f32[64,64]{1,0:T(8,128)S(1)}, f32[64,64]{1,0:T(8,128)}, u32[]{:S(2)}) copy-start(f32[64,64]{1,0:T(8,128)} %param.23) | copy-start | bytes 49156
  0.0 15.4 %copy-start.4 = (f32[64,64]{1,0:T(8,128)S(1)}, f32[64,64]{1,0:T(8,128)}, u32[]{:S(2)}) copy-start(f32[64,64]{1,0:T(8,128)} %constant.61.clone) | copy-start | bytes 49156
  0.0 17.2 %copy-start.3 = (f32[256,256]{1,0:T(8,128)S(1)}, f32[256,256]{1,0:T(8,128)}, u32[]{:S(2)}) copy-start(f32[256,256]{1,0:T(8,128)} %constant.60.clone) | copy-start | bytes 786436
  0.0 13.0 %copy-start.6 = (s32[4096]{0:T(1024)S(1)}, s32[4096]{0:T(1024)}, u32[]{:S(2)}) copy-start(s32[4096]{0:T(1024)} %param.24) | copy-start | bytes 49156
  0.0 13.0 %copy-start.5 = (s32[4096]{0:T(1024)S(1)}, s32[4096]{0:T(1024)}, u32[]{:S(2)}) copy-start(s32[4096]{0:T(1024)} %param.25) | copy-start | bytes 49156
  0.0 17.9 %copy-start.7 = (s32[4096]{0:T(1024)S(1)}, s32[4096]{0:T(1024)}, u32[]{:S(2)}) copy-start(s32[4096]{0:T(1024)} %param.26) | copy-start | bytes 49156
  4.0 11.7 %collective-permute-start = (bf16[8,32,512]{2,1,0:T(8,128)(2,1)S(1)}, bf16[8,32,512]{2,1,0:T(8,128)(2,1)S(1)}, u32[]{:S(2)}, u32[]{:S(2)}) collective-permute-start(bf16[8,32,512]{2,1,0:T(8,128)(2,1)S(1)} %get-tuple-element.8), channel_id=1, source_target_pairs={{0,4},{4,8},{8,12},{1,5},{5,9},{9,13},{2,6},{6,10},{10,14},{3,7},{... | collective-permute-start | bytes 786440 | tf_op jit(solution)/shard_map/ppermute | solution.py:166
  15.9 64.6 %collective-permute-start.1 = (bf16[8,32,512]{2,1,0:T(8,128)(2,1)S(1)}, bf16[8,32,512]{2,1,0:T(8,128)(2,1)S(1)}, u32[]{:S(2)}, u32[]{:S(2)}) collective-permute-start(bf16[8,32,512]{2,1,0:T(8,128)(2,1)S(1)} %get-tuple-element.6), channel_id=1, source_target_pairs={{4,0},{8,4},{12,8},{5,1},{9,5},{13,9},{6,2},{10,6},{14,10},{7,3},{... | collective-permute-start | bytes 786440 | tf_op jit(solution)/shard_map/ppermute | solution.py:167
  71.2 9.4 %copy-start.2 = (f32[128,512,1,1]{1,0,3,2:T(8,128)S(1)}, f32[128,512,1,1]{1,0,3,2:T(8,128)}, u32[]{:S(2)}) copy-start(f32[128,512,1,1]{1,0,3,2:T(8,128)} %constant.62) | copy-start | bytes 786436
  121.0 29.8 %copy-start.1 = (f32[64,64]{1,0:T(8,128)S(1)}, f32[64,64]{1,0:T(8,128)}, u32[]{:S(2)}) copy-start(f32[64,64]{1,0:T(8,128)} %param.23) | copy-start | bytes 49156
  129.5 1.4 collective-permute-start.2
  131.0 6.5 %collective-permute-start.3 = (f32[8,4096]{1,0:T(8,128)S(1)}, f32[8,4096]{1,0:T(8,128)S(1)}, u32[]{:S(2)}, u32[]{:S(2)}) collective-permute-start(f32[8,4096]{1,0:T(8,128)S(1)} %bitcast_add_fusion), channel_id=1, source_target_pairs={{0,4},{4,0},{8,12},{12,8},{1,5},{5,1},{9,13},{13,9},{2,6},{6,2},{1... | collective-permute-start | bytes 393224 | tf_op jit(solution)/shard_map/ppermute | solution.py:235
  137.5 8.8 %collective-permute-start.4 = (f32[8,4096]{1,0:T(8,128)S(1)}, f32[8,4096]{1,0:T(8,128)S(1)}, u32[]{:S(2)}, u32[]{:S(2)}) collective-permute-start(f32[8,4096]{1,0:T(8,128)S(1)} %add.52), channel_id=1, source_target_pairs={{0,8},{4,12},{8,0},{12,4},{1,9},{5,13},{9,1},{13,5},{2,10},{6,14},... | collective-permute-start | bytes 393224 | tf_op jit(solution)/shard_map/ppermute | solution.py:235

commit v10 on v9

--- a/solution.py
+++ b/solution.py
@@ -112,7 +112,7 @@
     )(load, vals, lower, upper, rl, ri, pf, ml, mi, tb)
 
 
-def illiquid_kernel(kb_ref, ka_ref, ca_ref, t_ref, rim_ref, out_ref, spectrum):
+def illiquid_kernel(kb_ref, ka_ref, ca_ref, t_ref, rim_ref, w_ref, group_ref, out_ref, spectrum, picked):
     j = pl.program_id(0)
     block, na_loc, lanes = t_ref.shape
     ch, cl = split_bf16(ca_ref[...])
@@ -128,13 +128,22 @@
     @pl.when(j == pl.num_programs(0) - 1)
     def _():
         def pick(i, carry):
-            out_ref[pl.ds(i, 1), :] = spectrum[kb_ref[i], pl.ds(ka_ref[i], 1), :]
+            picked[pl.ds(i, 1), :] = spectrum[kb_ref[i], pl.ds(ka_ref[i], 1), :]
             return carry
 
-        lax.fori_loop(0, out_ref.shape[0], pick, 0, unroll=8)
-
-
-def illiquid_pick(ca, t, rim, kb_index, ka_index):
+        lax.fori_loop(0, picked.shape[0], pick, 0, unroll=8)
+        rest = picked[...] * w_ref[...]
+        group = group_ref[...]
+        total = None
+        for _ in range(3):
+            part = rest.astype(jnp.bfloat16)
+            rest = rest - part.astype(jnp.float32)
+            term = lax.dot_general(group, part, (((1,), (1,)), ((), ())), preferred_element_type=jnp.float32)
+            total = term if total is None else total + term
+        out_ref[...] = total
+
+
+def illiquid_pick(ca, t, rim, weight, group, kb_index, ka_index):
     kb, na_loc, lanes = t.shape
     na = ca.shape[0]
     count = kb_index.shape[0]
@@ -148,13 +157,15 @@
                 pl.BlockSpec((na, na_loc), lambda j, *_: (0, 0)),
                 pl.BlockSpec((block, na_loc, lanes), lambda j, *_: (j, 0, 0)),
                 pl.BlockSpec((block, 2, lanes), lambda j, *_: (j, 0, 0)),
+                pl.BlockSpec((count, lanes), lambda j, *_: (0, 0)),
+                pl.BlockSpec(group.shape, lambda j, *_: (0, 0)),
             ],
-            out_specs=pl.BlockSpec((count, lanes), lambda j, *_: (0, 0)),
-            scratch_shapes=[pltpu.VMEM((kb, na, lanes), jnp.float32)],
+            out_specs=pl.BlockSpec((group.shape[0], count), lambda j, *_: (0, 0)),
+            scratch_shapes=[pltpu.VMEM((kb, na, lanes), jnp.float32), pltpu.VMEM((count, lanes), jnp.float32)],
         ),
-        out_shape=jax.ShapeDtypeStruct((count, lanes), jnp.float32),
+        out_shape=jax.ShapeDtypeStruct((group.shape[0], count), jnp.float32),
         compiler_params=pltpu.CompilerParams(vmem_limit_bytes=60 * 1024 * 1024),
-    )(kb_index, ka_index, ca, t, rim)
+    )(kb_index, ka_index, ca, t, rim, weight, group)
 
 
 def edges(values, axis, dim):
@@ -207,15 +218,17 @@
     rim = jnp.transpose(rim, (3, 2, 0, 1)).reshape(KBLOW, 2, columns * nz_loc)
     liquid_part = jnp.transpose(liquid_part, (3, 2, 0, 1)).reshape(KBLOW, na_loc, columns * nz_loc)
     table_a = lax.dynamic_slice_in_dim(jnp.asarray(cosine_constant(NA)), wide_pos * na_loc, na_loc, axis=1)
-    picked = illiquid_pick(
-        table_a, liquid_part, rim, jnp.clip(coef_liquid, 0, KBLOW - 1), jnp.clip(coef_illiquid, 0, NA - 1)
-    )
     folded = jnp.dot(jnp.asarray(cosine_constant(NZ)), jump_inverse, precision=lax.Precision.HIGHEST)
     folded = lax.dynamic_slice_in_dim(folded, inc_pos * nz_loc, nz_loc, axis=1)
     pick_z = (coef_income[:, None] == jnp.arange(NZ, dtype=jnp.int32)[None, :]).astype(jnp.float32)
-    weight = jnp.dot(pick_z, folded, precision=lax.Precision.HIGHEST)
-    partial = jnp.sum(picked.reshape(-1, columns, nz_loc) * weight[:, None, :], axis=2)
-    kept = all_sum(partial.T, ("inc", "wide"))
+    weight = jnp.dot(pick_z, jnp.tile(folded, (1, columns)), precision=lax.Precision.HIGHEST)
+    lanes = columns * nz_loc
+    group = (jnp.arange(lanes)[None, :] // nz_loc == jnp.arange(columns)[:, None]).astype(jnp.bfloat16)
+    partial = illiquid_pick(
+        table_a, liquid_part, rim, weight, group,
+        jnp.clip(coef_liquid, 0, KBLOW - 1), jnp.clip(coef_illiquid, 0, NA - 1),
+    )
+    kept = all_sum(partial, ("inc", "wide"))
     owners = lax.axis_size(("wide", "inc"))
     count = owner.shape[0]
     capacity = 2 * count // owners

time: 152 us -> 150 us (0.987)
  local copies, waits for them, and re-layouts: 26.7 us -> 21.1 us
  matrix products: 2.26 us -> 5.27 us
  Pallas kernels: 89.9 us -> 91.9 us
    pallas_call x1 -> x0, local copies, waits for them, and re-layouts: 5.64 us -> none  [illiquid_pick(): pl.pallas_call(illiquid_kernel, grid_spec=pltpu.PrefetchScalarGridSpec(nu...]
    dot_general x1, matrix products: 1.45 us -> 4.46 us  [body(): jnp.dot(pick_z, jnp.tile(folded, (1, columns)), precision=lax.Precision.H...]
    reduce_sum x1 -> x0, other arithmetic: 2.84 us -> none  [body(): jnp.sum(picked.reshape(-1, columns, nz_loc) * weight[:, None, :], axis=2)]
    pallas_call x1, Pallas kernels: 39 us -> 40.9 us  [illiquid_pick(): pl.pallas_call(illiquid_kernel, grid_spec=pltpu.PrefetchScalarGridSpec(nu...]
  transfers between devices with their start and end apart: 5 -> 5, of which waited for: 3 -> 3; matrix products, arithmetic and copies ran while one was open for 13% -> 15% of each run, Pallas kernels for 34% -> 34%
where the time goes in v10:
time: 150 us; the launch traced here: 149 us
  Pallas kernels  91.9 us (61%)
  local copies, waits for them, and re-layouts  21.1 us (14%)
  starting transfers between devices  11.9 us (8%)
  waiting for transfers between devices  11.4 us (8%)
  other arithmetic  7.47 us (5%)
  matrix products  5.27 us (4%)
    pallas_call x1, Pallas kernels, liquid_step(): pl.pallas_call(step_kernel, grid=(nz // zb,), in_specs=[pl.BlockSpec(memo...  51 us
    pallas_call x1, Pallas kernels, illiquid_pick(): pl.pallas_call(illiquid_kernel, grid_spec=pltpu.PrefetchScalarGridSpec(nu...  40.9 us
    ppermute x3, waiting for transfers between devices, all_sum(): x = x + lax.ppermute(x, axis, [(i, i ^ step) for i in range(count)])  11.3 us
    reshape x1, local copies, waits for them, and re-layouts, body(): jnp.transpose(liquid_part, (3, 2, 0, 1))  9.32 us
    ppermute x3, starting transfers between devices, all_sum(): x = x + lax.ppermute(x, axis, [(i, i ^ step) for i in range(count)])  5.52 us
    ppermute x1, starting transfers between devices, edges(): lax.ppermute(tail, axis, [(i, (i + 1) % count) for i in range(ends)])  4.95 us
    dot_general x1, matrix products, body(): jnp.dot(pick_z, jnp.tile(folded, (1, columns)), precision=lax.Precision.H...  4.46 us
    slice x1, local copies, waits for them, and re-layouts, body(): head = values_in[:, :, 0, :].astype(jnp.float32)  3.06 us
  transfers between devices with their start and end apart: 5, of which 3 were waited for; matrix products, arithmetic and copies ran while one was open for 15% of the time, Pallas kernels for 34%

profile of v10, /device:TPU:0, one launch (start us, length us, event | category | flops | bytes accessed | tf_op | source)
XLA Modules:
  0.0 149.3 jit_solution(15141445044029739391)
XLA Ops:
  0.0 3.1 %fusion.7 = (bf16[8,32,1,512]{3,2,1,0:T(2,128)(2,1)S(1)}, bf16[8,32,1,512]{3,2,1,0:T(2,128)(2,1)S(1)}) fusion(bf16[8,32,64,512]{3,2,1,0:T(8,128)(2,1)} %vals_ref.1), kind=kLoop, calls=%fused_computation.40 | loop fusion | bytes 1048576 | tf_op jit(solution)/shard_map/slice | solution.py:202
  3.1 0.9 fusion.6
  4.0 4.9 %collective-permute-start = (bf16[8,32,512]{2,1,0:T(8,128)(2,1)S(1)}, bf16[8,32,512]{2,1,0:T(8,128)(2,1)S(1)}, u32[]{:S(2)}, u32[]{:S(2)}) collective-permute-start(bf16[8,32,512]{2,1,0:T(8,128)(2,1)S(1)} %get-tuple-element.8), channel_id=1, source_target_pairs={{0,4},{4,8},{8,12},{1,5},{5,9},{9,13},{2,6},{6,10},{10,14},{3,7},{... | collective-permute-start | bytes 786440 | tf_op jit(solution)/shard_map/ppermute | solution.py:177
  9.0 1.3 fusion.9
  10.3 1.3 fusion.8
  11.6 0.7 convert_bitcast_fusion
  13.0 1.8 %convert_reduce_fusion = s32[1024]{0:T(1024)S(1)} fusion(s32[4096]{0:T(1024)S(1)} %add_bitcast_fusion, s32[1024]{0:T(1024)S(1)} %iota_add_fusion), kind=kLoop, calls=%fused_computation.1 | loop fusion | flops 12581888 | bytes 24576 | tf_op jit(solution)/shard_map/reduce_sum | solution.py:238
  15.1 4.5 %fusion.w_ref = f32[4096,256]{1,0:T(8,128)} fusion(f32[64,256]{0,1:T(8,128)S(1)} %bitcast.44, s32[4096]{0:T(1024)S(1)} %copy-done.3), kind=kOutput, calls=%fused_computation.3 | convolution fusion | flops 805568512 | bytes 4276224 | tf_op jit(solution)/shard_map/dot_general | solution.py:224
  19.5 0.6 broadcast_clamp_fusion
  20.9 1.5 collective-permute-start.1
  22.4 0.8 constant_dynamic-slice_fusion.1.ca_ref
  23.2 0.9 convert_element_type.21.lo_ref
  24.0 51.0 %shard_map.154 = f32[8,32,64,128]{3,2,1,0:T(8,128)} custom-call(f32[8]{0:T(128)} %load_ref.1, bf16[8,32,64,512]{3,2,1,0:T(8,128)(2,1)} %vals_ref.1, f32[8,32,512]{2,1,0:T(8,128)} %convert_element_type.21.lo_ref, f32[8,32,512]{2,1,0:T(8,128)} %get-tuple-element.7.up_ref, f32[32,64,512]{2,1,0:T(8,128)} %rl_ref.1, f32[32,64,512]{2,1,0:T(8,128)} %ri_ref.1, ...), custom_call_target="tpu_custom_call" | custom-call | tf_op jit(solution)/shard_map/pallas_call | solution.py:94
  75.0 9.3 %copy.47.t_ref = f32[128,64,256]{2,1,0:T(8,128)} copy(f32[128,64,256]{0,1,2:T(8,128)} %bitcast.42) | data formatting | bytes 16777216 | tf_op jit(solution)/shard_map/reshape | solution.py:219
  85.1 0.9 copy.48.rim_ref
  85.9 40.9 %shard_map.155 = f32[8,4096]{1,0:T(8,128)} custom-call(s32[4096]{0:T(1024)} %get-tuple-element.18.kb_ref, s32[4096]{0:T(1024)} %get-tuple-element.17.ka_ref, f32[256,64]{1,0:T(8,128)} %constant_dynamic-slice_fusion.1.ca_ref, f32[128,64,256]{2,1,0:T(8,128)} %copy.47.t_ref, f32[128,2,256]{2,1,0:T(2,128)} %copy.48.rim_ref, f32[4096,256]{1,0:T(8,128)} %fusion.w_ref, ...), custom_call_target="tpu_custom_call" | custom-call | tf_op jit(solution)/shard_map/pallas_call | solution.py:151
  126.9 1.5 %collective-permute-done.2 = f32[8,4096]{1,0:T(8,128)S(1)} collective-permute-done((f32[8,4096]{1,0:T(8,128)}, f32[8,4096]{1,0:T(8,128)S(1)}, u32[]{:S(2)}, u32[]{:S(2)}) %collective-permute-start.2) | collective-permute-done | bytes 131104 | tf_op jit(solution)/shard_map/ppermute | solution.py:248
  128.4 0.9 add.57
  129.4 2.7 %collective-permute-start.3 = (f32[8,4096]{1,0:T(8,128)S(1)}, f32[8,4096]{1,0:T(8,128)S(1)}, u32[]{:S(2)}, u32[]{:S(2)}) collective-permute-start(f32[8,4096]{1,0:T(8,128)S(1)} %add.57), channel_id=1, source_target_pairs={{0,4},{4,0},{8,12},{12,8},{1,5},{5,1},{9,13},{13,9},{2,6},{6,2},{1... | collective-permute-start | bytes 393224 | tf_op jit(solution)/shard_map/ppermute | solution.py:248
  132.1 3.8 %collective-permute-done.3 = f32[8,4096]{1,0:T(8,128)S(1)} collective-permute-done((f32[8,4096]{1,0:T(8,128)S(1)}, f32[8,4096]{1,0:T(8,128)S(1)}, u32[]{:S(2)}, u32[]{:S(2)}) %collective-permute-start.3) | collective-permute-done | bytes 131104 | tf_op jit(solution)/shard_map/ppermute | solution.py:248
  135.9 2.8 %collective-permute-start.4 = (f32[8,4096]{1,0:T(8,128)S(1)}, f32[8,4096]{1,0:T(8,128)S(1)}, u32[]{:S(2)}, u32[]{:S(2)}) collective-permute-start(f32[8,4096]{1,0:T(8,128)S(1)} %add.58), channel_id=1, source_target_pairs={{0,8},{4,12},{8,0},{12,4},{1,9},{5,13},{9,1},{13,5},{2,10},{6,14},... | collective-permute-start | bytes 393224 | tf_op jit(solution)/shard_map/ppermute | solution.py:248
  138.7 6.0 %collective-permute-done.4 = f32[8,4096]{1,0:T(8,128)S(1)} collective-permute-done((f32[8,4096]{1,0:T(8,128)S(1)}, f32[8,4096]{1,0:T(8,128)S(1)}, u32[]{:S(2)}, u32[]{:S(2)}) %collective-permute-start.4) | collective-permute-done | bytes 131104 | tf_op jit(solution)/shard_map/ppermute | solution.py:248
  145.3 2.8 %gather_fusion = f32[1024,8]{1,0:T(8,128)S(1)} fusion(f32[8,4096]{0,1:T(8,128)S(1)} %copy.49, s32[1024]{0:T(1024)S(1)} %broadcast_clamp_fusion.2), kind=kCustom, calls=%fused_computation | custom fusion | bytes 69632 | tf_op jit(solution)/shard_map/jit(_take)/gather | solution.py:239
  148.5 0.8 copy.50
  (46 shorter events, 3.4 us)
Async XLA Ops:
  0.0 14.8 %copy-start = (f32[64,64]{1,0:T(8,128)S(1)}, f32[64,64]{1,0:T(8,128)}, u32[]{:S(2)}) copy-start(f32[64,64]{1,0:T(8,128)} %param.23) | copy-start | bytes 49156
  0.0 14.8 %copy-start.5 = (f32[64,64]{1,0:T(8,128)S(1)}, f32[64,64]{1,0:T(8,128)}, u32[]{:S(2)}) copy-start(f32[64,64]{1,0:T(8,128)} %constant.76.clone) | copy-start | bytes 49156
  0.0 15.1 %copy-start.3 = (s32[4096]{0:T(1024)S(1)}, s32[4096]{0:T(1024)}, u32[]{:S(2)}) copy-start(s32[4096]{0:T(1024)} %param.26) | copy-start | bytes 49156
  4.0 16.8 %collective-permute-start = (bf16[8,32,512]{2,1,0:T(8,128)(2,1)S(1)}, bf16[8,32,512]{2,1,0:T(8,128)(2,1)S(1)}, u32[]{:S(2)}, u32[]{:S(2)}) collective-permute-start(bf16[8,32,512]{2,1,0:T(8,128)(2,1)S(1)} %get-tuple-element.8), channel_id=1, source_target_pairs={{0,4},{4,8},{8,12},{1,5},{5,9},{9,13},{2,6},{6,10},{10,14},{3,7},{... | collective-permute-start | bytes 786440 | tf_op jit(solution)/shard_map/ppermute | solution.py:177
  10.3 9.3 %copy-start.6 = (s32[4096]{0:T(1024)S(1)}, s32[4096]{0:T(1024)}, u32[]{:S(2)}) copy-start(s32[4096]{0:T(1024)} %param.25) | copy-start | bytes 49156
  10.3 9.3 %copy-start.7 = (s32[4096]{0:T(1024)S(1)}, s32[4096]{0:T(1024)}, u32[]{:S(2)}) copy-start(s32[4096]{0:T(1024)} %param.24) | copy-start | bytes 49156
  15.1 7.3 %copy-start.4 = (f32[256,256]{1,0:T(8,128)S(1)}, f32[256,256]{1,0:T(8,128)}, u32[]{:S(2)}) copy-start(f32[256,256]{1,0:T(8,128)} %constant.75.clone) | copy-start | bytes 786436
  20.9 63.4 %collective-permute-start.1 = (bf16[8,32,512]{2,1,0:T(8,128)(2,1)S(1)}, bf16[8,32,512]{2,1,0:T(8,128)(2,1)S(1)}, u32[]{:S(2)}, u32[]{:S(2)}) collective-permute-start(bf16[8,32,512]{2,1,0:T(8,128)(2,1)S(1)} %get-tuple-element.6), channel_id=1, source_target_pairs={{4,0},{8,4},{12,8},{5,1},{9,5},{13,9},{6,2},{10,6},{14,10},{7,3},{... | collective-permute-start | bytes 786440 | tf_op jit(solution)/shard_map/ppermute | solution.py:178
  75.0 9.4 %copy-start.2 = (f32[128,512,1,1]{1,0,3,2:T(8,128)S(1)}, f32[128,512,1,1]{1,0,3,2:T(8,128)}, u32[]{:S(2)}) copy-start(f32[128,512,1,1]{1,0,3,2:T(8,128)} %constant.77) | copy-start | bytes 786436
  85.9 63.4 %copy-start.1 = (f32[64,64]{1,0:T(8,128)S(1)}, f32[64,64]{1,0:T(8,128)}, u32[]{:S(2)}) copy-start(f32[64,64]{1,0:T(8,128)} %param.23) | copy-start | bytes 49156
  126.9 1.6 %collective-permute-start.2 = (f32[8,4096]{1,0:T(8,128)}, f32[8,4096]{1,0:T(8,128)S(1)}, u32[]{:S(2)}, u32[]{:S(2)}) collective-permute-start(f32[8,4096]{1,0:T(8,128)} %shard_map.155), channel_id=1, source_target_pairs={{0,1},{1,0},{2,3},{3,2},{4,5},{5,4},{6,7},{7,6},{8,9},{9,8},{10,11... | collective-permute-start | bytes 393224 | tf_op jit(solution)/shard_map/ppermute | solution.py:248
  129.4 6.5 %collective-permute-start.3 = (f32[8,4096]{1,0:T(8,128)S(1)}, f32[8,4096]{1,0:T(8,128)S(1)}, u32[]{:S(2)}, u32[]{:S(2)}) collective-permute-start(f32[8,4096]{1,0:T(8,128)S(1)} %add.57), channel_id=1, source_target_pairs={{0,4},{4,0},{8,12},{12,8},{1,5},{5,1},{9,13},{13,9},{2,6},{6,2},{1... | collective-permute-start | bytes 393224 | tf_op jit(solution)/shard_map/ppermute | solution.py:248
  135.9 8.8 %collective-permute-start.4 = (f32[8,4096]{1,0:T(8,128)S(1)}, f32[8,4096]{1,0:T(8,128)S(1)}, u32[]{:S(2)}, u32[]{:S(2)}) collective-permute-start(f32[8,4096]{1,0:T(8,128)S(1)} %add.58), channel_id=1, source_target_pairs={{0,8},{4,12},{8,0},{12,4},{1,9},{5,13},{9,1},{13,5},{2,10},{6,14},... | collective-permute-start | bytes 393224 | tf_op jit(solution)/shard_map/ppermute | solution.py:248

commit v11 on v10

--- a/solution.py
+++ b/solution.py
@@ -1,4 +1,5 @@
 import functools
+import ml_dtypes
 import numpy as np
 import jax
 import jax.numpy as jnp
@@ -29,6 +30,13 @@
     table = np.cos(np.pi * ((2 * cell + 1) * freq % (4 * count)) / (2.0 * count)) * np.sqrt(2.0 / count)
     table[0] *= np.sqrt(0.5)
     return table.astype(np.float32)
+
+
+def stacked_constant(count):
+    table = cosine_constant(count)
+    high = table.astype(ml_dtypes.bfloat16)
+    low = (table - high.astype(np.float32)).astype(ml_dtypes.bfloat16)
+    return np.stack([low, high, high], axis=1)
 
 
 def slot_targets(owner, owners, capacity):
@@ -115,15 +123,14 @@
 def illiquid_kernel(kb_ref, ka_ref, ca_ref, t_ref, rim_ref, w_ref, group_ref, out_ref, spectrum, picked):
     j = pl.program_id(0)
     block, na_loc, lanes = t_ref.shape
-    ch, cl = split_bf16(ca_ref[...])
+    stacked = ca_ref[...]
     row = lax.broadcasted_iota(jnp.int32, (na_loc, lanes), 0)
     for k in range(block):
         rim = rim_ref[k]
         t = t_ref[k] + jnp.where(row == 0, rim[0:1], 0.0)
         th, tl = split_bf16(t + jnp.where(row == na_loc - 1, rim[1:2], 0.0))
-        acc = jnp.dot(cl, th, preferred_element_type=jnp.float32)
-        acc = acc + jnp.dot(ch, tl, preferred_element_type=jnp.float32)
-        spectrum[j * block + k] = acc + jnp.dot(ch, th, preferred_element_type=jnp.float32)
+        rhs = jnp.concatenate([th, th, tl], axis=0)
+        spectrum[j * block + k] = jnp.dot(stacked, rhs, preferred_element_type=jnp.float32)
 
     @pl.when(j == pl.num_programs(0) - 1)
     def _():
@@ -145,7 +152,7 @@
 
 def illiquid_pick(ca, t, rim, weight, group, kb_index, ka_index):
     kb, na_loc, lanes = t.shape
-    na = ca.shape[0]
+    na, depth = ca.shape
     count = kb_index.shape[0]
     block = 8
     return pl.pallas_call(
@@ -154,7 +161,7 @@
             num_scalar_prefetch=2,
             grid=(kb // block,),
             in_specs=[
-                pl.BlockSpec((na, na_loc), lambda j, *_: (0, 0)),
+                pl.BlockSpec((na, depth), lambda j, *_: (0, 0)),
                 pl.BlockSpec((block, na_loc, lanes), lambda j, *_: (j, 0, 0)),
                 pl.BlockSpec((block, 2, lanes), lambda j, *_: (j, 0, 0)),
                 pl.BlockSpec((count, lanes), lambda j, *_: (0, 0)),
@@ -217,7 +224,8 @@
     rim = jnp.einsum("kb,czeb->czek", jnp.asarray(table_b), rim, precision=high)
     rim = jnp.transpose(rim, (3, 2, 0, 1)).reshape(KBLOW, 2, columns * nz_loc)
     liquid_part = jnp.transpose(liquid_part, (3, 2, 0, 1)).reshape(KBLOW, na_loc, columns * nz_loc)
-    table_a = lax.dynamic_slice_in_dim(jnp.asarray(cosine_constant(NA)), wide_pos * na_loc, na_loc, axis=1)
+    table_a = lax.dynamic_slice_in_dim(jnp.asarray(stacked_constant(NA)), wide_pos * na_loc, na_loc, axis=2)
+    table_a = table_a.reshape(NA, 3 * na_loc)
     folded = jnp.dot(jnp.asarray(cosine_constant(NZ)), jump_inverse, precision=lax.Precision.HIGHEST)
     folded = lax.dynamic_slice_in_dim(folded, inc_pos * nz_loc, nz_loc, axis=1)
     pick_z = (coef_income[:, None] == jnp.arange(NZ, dtype=jnp.int32)[None, :]).astype(jnp.float32)

time: 150 us -> 146 us (0.973)
  Pallas kernels: 91.9 us -> 87.3 us
    pallas_call x1, Pallas kernels: 40.9 us -> 36.3 us  [illiquid_pick(): pl.pallas_call(illiquid_kernel, grid_spec=pltpu.PrefetchScalarGridSpec(nu...]
  transfers between devices with their start and end apart: 5 -> 5, of which waited for: 3 -> 3; matrix products, arithmetic and copies ran while one was open for 15% -> 16% of each run, Pallas kernels for 34% -> 35%
where the time goes in v11:
time: 146 us; the launch traced here: 145 us
  Pallas kernels  87.3 us (60%)
  local copies, waits for them, and re-layouts  22 us (15%)
  starting transfers between devices  11.8 us (8%)
  waiting for transfers between devices  11.4 us (8%)
  other arithmetic  7.45 us (5%)
  matrix products  5.28 us (4%)
    pallas_call x1, Pallas kernels, liquid_step(): pl.pallas_call(step_kernel, grid=(nz // zb,), in_specs=[pl.BlockSpec(memo...  51 us
    pallas_call x1, Pallas kernels, illiquid_pick(): pl.pallas_call(illiquid_kernel, grid_spec=pltpu.PrefetchScalarGridSpec(nu...  36.3 us
    ppermute x3, waiting for transfers between devices, all_sum(): x = x + lax.ppermute(x, axis, [(i, i ^ step) for i in range(count)])  11.4 us
    reshape x1, local copies, waits for them, and re-layouts, body(): jnp.transpose(liquid_part, (3, 2, 0, 1))  9.3 us
    ppermute x3, starting transfers between devices, all_sum(): x = x + lax.ppermute(x, axis, [(i, i ^ step) for i in range(count)])  5.52 us
    ppermute x1, starting transfers between devices, edges(): lax.ppermute(tail, axis, [(i, (i + 1) % count) for i in range(ends)])  4.95 us
    dot_general x1, matrix products, body(): jnp.dot(pick_z, jnp.tile(folded, (1, columns)), precision=lax.Precision.H...  4.46 us
    slice x1, local copies, waits for them, and re-layouts, body(): head = values_in[:, :, 0, :].astype(jnp.float32)  3.06 us
  transfers between devices with their start and end apart: 5, of which 3 were waited for; matrix products, arithmetic and copies ran while one was open for 16% of the time, Pallas kernels for 35%

profile of v11, /device:TPU:0, one launch (start us, length us, event | category | flops | bytes accessed | tf_op | source)
XLA Modules:
  0.0 145.3 jit_solution(7669993309857160331)
XLA Ops:
  0.0 3.1 %fusion.7 = (bf16[8,32,1,512]{3,2,1,0:T(2,128)(2,1)S(1)}, bf16[8,32,1,512]{3,2,1,0:T(2,128)(2,1)S(1)}) fusion(bf16[8,32,64,512]{3,2,1,0:T(8,128)(2,1)} %vals_ref.1), kind=kLoop, calls=%fused_computation.40 | loop fusion | bytes 1048576 | tf_op jit(solution)/shard_map/slice | solution.py:209
  3.1 0.9 fusion.6
  4.0 4.9 %collective-permute-start = (bf16[8,32,512]{2,1,0:T(8,128)(2,1)S(1)}, bf16[8,32,512]{2,1,0:T(8,128)(2,1)S(1)}, u32[]{:S(2)}, u32[]{:S(2)}) collective-permute-start(bf16[8,32,512]{2,1,0:T(8,128)(2,1)S(1)} %get-tuple-element.8), channel_id=1, source_target_pairs={{0,4},{4,8},{8,12},{1,5},{5,9},{9,13},{2,6},{6,10},{10,14},{3,7},{... | collective-permute-start | bytes 786440 | tf_op jit(solution)/shard_map/ppermute | solution.py:184
  8.9 1.3 fusion.9
  10.3 1.3 fusion.8
  11.6 0.7 convert_bitcast_fusion
  12.9 1.8 %convert_reduce_fusion = s32[1024]{0:T(1024)S(1)} fusion(s32[4096]{0:T(1024)S(1)} %add_bitcast_fusion, s32[1024]{0:T(1024)S(1)} %iota_add_fusion), kind=kLoop, calls=%fused_computation.1 | loop fusion | flops 12581888 | bytes 24576 | tf_op jit(solution)/shard_map/reduce_sum | solution.py:246
  15.1 4.5 %fusion.w_ref = f32[4096,256]{1,0:T(8,128)} fusion(f32[64,256]{0,1:T(8,128)S(1)} %bitcast.45, s32[4096]{0:T(1024)S(1)} %copy-done.3), kind=kOutput, calls=%fused_computation.3 | convolution fusion | flops 805568512 | bytes 4276224 | tf_op jit(solution)/shard_map/dot_general | solution.py:232
  20.9 1.3 collective-permute-start.1
  22.2 0.9 constant_dynamic-slice_fusion.1
  23.1 0.7 copy.48.ca_ref
  23.9 0.9 convert_element_type.21.lo_ref
  24.7 51.0 %shard_map.154 = f32[8,32,64,128]{3,2,1,0:T(8,128)} custom-call(f32[8]{0:T(128)} %load_ref.1, bf16[8,32,64,512]{3,2,1,0:T(8,128)(2,1)} %vals_ref.1, f32[8,32,512]{2,1,0:T(8,128)} %convert_element_type.21.lo_ref, f32[8,32,512]{2,1,0:T(8,128)} %get-tuple-element.7.up_ref, f32[32,64,512]{2,1,0:T(8,128)} %rl_ref.1, f32[32,64,512]{2,1,0:T(8,128)} %ri_ref.1, ...), custom_call_target="tpu_custom_call" | custom-call | tf_op jit(solution)/shard_map/pallas_call | solution.py:102
  75.7 9.3 %copy.49.t_ref = f32[128,64,256]{2,1,0:T(8,128)} copy(f32[128,64,256]{0,1,2:T(8,128)} %bitcast.43) | data formatting | bytes 16777216 | tf_op jit(solution)/shard_map/reshape | solution.py:226
  85.7 0.9 copy.50.rim_ref
  86.6 36.3 %shard_map.155 = f32[8,4096]{1,0:T(8,128)} custom-call(s32[4096]{0:T(1024)} %get-tuple-element.18.kb_ref, s32[4096]{0:T(1024)} %get-tuple-element.17.ka_ref, bf16[256,192]{1,0:T(8,128)(2,1)} %copy.48.ca_ref, f32[128,64,256]{2,1,0:T(8,128)} %copy.49.t_ref, f32[128,2,256]{2,1,0:T(2,128)} %copy.50.rim_ref, f32[4096,256]{1,0:T(8,128)} %fusion.w_ref, ...), custom_call_target="tpu_custom_call" | custom-call | tf_op jit(solution)/shard_map/pallas_call | solution.py:158
  122.9 1.5 %collective-permute-done.2 = f32[8,4096]{1,0:T(8,128)S(1)} collective-permute-done((f32[8,4096]{1,0:T(8,128)}, f32[8,4096]{1,0:T(8,128)S(1)}, u32[]{:S(2)}, u32[]{:S(2)}) %collective-permute-start.2) | collective-permute-done | bytes 131104 | tf_op jit(solution)/shard_map/ppermute | solution.py:256
  124.5 0.9 add.57
  125.4 2.7 %collective-permute-start.3 = (f32[8,4096]{1,0:T(8,128)S(1)}, f32[8,4096]{1,0:T(8,128)S(1)}, u32[]{:S(2)}, u32[]{:S(2)}) collective-permute-start(f32[8,4096]{1,0:T(8,128)S(1)} %add.57), channel_id=1, source_target_pairs={{0,4},{4,0},{8,12},{12,8},{1,5},{5,1},{9,13},{13,9},{2,6},{6,2},{1... | collective-permute-start | bytes 393224 | tf_op jit(solution)/shard_map/ppermute | solution.py:256
  128.1 3.8 %collective-permute-done.3 = f32[8,4096]{1,0:T(8,128)S(1)} collective-permute-done((f32[8,4096]{1,0:T(8,128)S(1)}, f32[8,4096]{1,0:T(8,128)S(1)}, u32[]{:S(2)}, u32[]{:S(2)}) %collective-permute-start.3) | collective-permute-done | bytes 131104 | tf_op jit(solution)/shard_map/ppermute | solution.py:256
  131.9 2.8 %collective-permute-start.4 = (f32[8,4096]{1,0:T(8,128)S(1)}, f32[8,4096]{1,0:T(8,128)S(1)}, u32[]{:S(2)}, u32[]{:S(2)}) collective-permute-start(f32[8,4096]{1,0:T(8,128)S(1)} %add.58), channel_id=1, source_target_pairs={{0,8},{4,12},{8,0},{12,4},{1,9},{5,13},{9,1},{13,5},{2,10},{6,14},... | collective-permute-start | bytes 393224 | tf_op jit(solution)/shard_map/ppermute | solution.py:256
  134.7 6.0 %collective-permute-done.4 = f32[8,4096]{1,0:T(8,128)S(1)} collective-permute-done((f32[8,4096]{1,0:T(8,128)S(1)}, f32[8,4096]{1,0:T(8,128)S(1)}, u32[]{:S(2)}, u32[]{:S(2)}) %collective-permute-start.4) | collective-permute-done | bytes 131104 | tf_op jit(solution)/shard_map/ppermute | solution.py:256
  141.4 2.8 %gather_fusion = f32[1024,8]{1,0:T(8,128)S(1)} fusion(f32[8,4096]{0,1:T(8,128)S(1)} %copy.51, s32[1024]{0:T(1024)S(1)} %broadcast_clamp_fusion.2), kind=kCustom, calls=%fused_computation | custom fusion | bytes 69632 | tf_op jit(solution)/shard_map/jit(_take)/gather | solution.py:247
  144.5 0.8 copy.52
  (45 shorter events, 4.0 us)
Async XLA Ops:
  0.0 14.7 %copy-start = (f32[64,64]{1,0:T(8,128)S(1)}, f32[64,64]{1,0:T(8,128)}, u32[]{:S(2)}) copy-start(f32[64,64]{1,0:T(8,128)} %param.23) | copy-start | bytes 49156
  0.0 14.7 %copy-start.4 = (f32[64,64]{1,0:T(8,128)S(1)}, f32[64,64]{1,0:T(8,128)}, u32[]{:S(2)}) copy-start(f32[64,64]{1,0:T(8,128)} %constant.76.clone) | copy-start | bytes 49156
  0.0 15.0 %copy-start.3 = (s32[4096]{0:T(1024)S(1)}, s32[4096]{0:T(1024)}, u32[]{:S(2)}) copy-start(s32[4096]{0:T(1024)} %param.26) | copy-start | bytes 49156
  4.0 16.8 %collective-permute-start = (bf16[8,32,512]{2,1,0:T(8,128)(2,1)S(1)}, bf16[8,32,512]{2,1,0:T(8,128)(2,1)S(1)}, u32[]{:S(2)}, u32[]{:S(2)}) collective-permute-start(bf16[8,32,512]{2,1,0:T(8,128)(2,1)S(1)} %get-tuple-element.8), channel_id=1, source_target_pairs={{0,4},{4,8},{8,12},{1,5},{5,9},{9,13},{2,6},{6,10},{10,14},{3,7},{... | collective-permute-start | bytes 786440 | tf_op jit(solution)/shard_map/ppermute | solution.py:184
  10.3 9.3 %copy-start.5 = (s32[4096]{0:T(1024)S(1)}, s32[4096]{0:T(1024)}, u32[]{:S(2)}) copy-start(s32[4096]{0:T(1024)} %param.25) | copy-start | bytes 49156
  10.3 9.2 %copy-start.6 = (s32[4096]{0:T(1024)S(1)}, s32[4096]{0:T(1024)}, u32[]{:S(2)}) copy-start(s32[4096]{0:T(1024)} %param.24) | copy-start | bytes 49156
  20.9 64.1 %collective-permute-start.1 = (bf16[8,32,512]{2,1,0:T(8,128)(2,1)S(1)}, bf16[8,32,512]{2,1,0:T(8,128)(2,1)S(1)}, u32[]{:S(2)}, u32[]{:S(2)}) collective-permute-start(bf16[8,32,512]{2,1,0:T(8,128)(2,1)S(1)} %get-tuple-element.6), channel_id=1, source_target_pairs={{4,0},{8,4},{12,8},{5,1},{9,5},{13,9},{6,2},{10,6},{14,10},{7,3},{... | collective-permute-start | bytes 786440 | tf_op jit(solution)/shard_map/ppermute | solution.py:185
  75.7 9.4 %copy-start.2 = (f32[128,512,1,1]{1,0,3,2:T(8,128)S(1)}, f32[128,512,1,1]{1,0,3,2:T(8,128)}, u32[]{:S(2)}) copy-start(f32[128,512,1,1]{1,0,3,2:T(8,128)} %constant.77) | copy-start | bytes 786436
  86.6 58.7 %copy-start.1 = (f32[64,64]{1,0:T(8,128)S(1)}, f32[64,64]{1,0:T(8,128)}, u32[]{:S(2)}) copy-start(f32[64,64]{1,0:T(8,128)} %param.23) | copy-start | bytes 49156
  122.9 1.6 %collective-permute-start.2 = (f32[8,4096]{1,0:T(8,128)}, f32[8,4096]{1,0:T(8,128)S(1)}, u32[]{:S(2)}, u32[]{:S(2)}) collective-permute-start(f32[8,4096]{1,0:T(8,128)} %shard_map.155), channel_id=1, source_target_pairs={{0,1},{1,0},{2,3},{3,2},{4,5},{5,4},{6,7},{7,6},{8,9},{9,8},{10,11... | collective-permute-start | bytes 393224 | tf_op jit(solution)/shard_map/ppermute | solution.py:256
  125.4 6.5 %collective-permute-start.3 = (f32[8,4096]{1,0:T(8,128)S(1)}, f32[8,4096]{1,0:T(8,128)S(1)}, u32[]{:S(2)}, u32[]{:S(2)}) collective-permute-start(f32[8,4096]{1,0:T(8,128)S(1)} %add.57), channel_id=1, source_target_pairs={{0,4},{4,0},{8,12},{12,8},{1,5},{5,1},{9,13},{13,9},{2,6},{6,2},{1... | collective-permute-start | bytes 393224 | tf_op jit(solution)/shard_map/ppermute | solution.py:256
  131.9 8.8 %collective-permute-start.4 = (f32[8,4096]{1,0:T(8,128)S(1)}, f32[8,4096]{1,0:T(8,128)S(1)}, u32[]{:S(2)}, u32[]{:S(2)}) collective-permute-start(f32[8,4096]{1,0:T(8,128)S(1)} %add.58), channel_id=1, source_target_pairs={{0,8},{4,12},{8,0},{12,4},{1,9},{5,13},{9,1},{13,5},{2,10},{6,14},... | collective-permute-start | bytes 393224 | tf_op jit(solution)/shard_map/ppermute | solution.py:256

commit v12 on v11

--- a/solution.py
+++ b/solution.py
@@ -68,10 +68,14 @@
     top = arow == na - 1
     bottom = arow == 0
     th, tl = split_bf16(tb_ref[...])
-    pf_hi, pf_lo = split_bf16(pf)
-    price = jnp.dot(pf_lo, th, preferred_element_type=jnp.float32)
-    price = price + jnp.dot(pf_hi, tl, preferred_element_type=jnp.float32)
-    price = price + jnp.dot(pf_hi, th, preferred_element_type=jnp.float32)
+    both = jnp.concatenate([th, tl], axis=1)
+
+    def transform(x):
+        hi, low = split_bf16(x)
+        pair = jnp.dot(hi, both, preferred_element_type=jnp.float32)
+        return jnp.dot(low, th, preferred_element_type=jnp.float32) + pair[:, kb:] + pair[:, :kb]
+
+    price = transform(pf)
 
     def per_column(c, carry):
         v = vals_ref[c].reshape(rows, nb).astype(jnp.float32)
@@ -82,11 +86,7 @@
         below = jnp.where(bottom, lo, pltpu.roll(v, 1, 0))
         side_a = jnp.where(ma, above, below)
         explicit = v + rl * (side_b - v) + ri * (side_a - v)
-        hi, low = split_bf16(explicit)
-        acc = jnp.dot(low, th, preferred_element_type=jnp.float32)
-        acc = acc + jnp.dot(hi, tl, preferred_element_type=jnp.float32)
-        acc = acc + jnp.dot(hi, th, preferred_element_type=jnp.float32)
-        out_ref[c] = (acc + load_ref[c] * price).reshape(zb, na, kb)
+        out_ref[c] = (transform(explicit) + load_ref[c] * price).reshape(zb, na, kb)
         return carry
 
     lax.fori_loop(0, columns, per_column, 0)

time: 146 us -> 140 us (0.959)
  Pallas kernels: 87.3 us -> 81.5 us
    pallas_call x1, Pallas kernels: 51 us -> 45.2 us  [liquid_step(): pl.pallas_call(step_kernel, grid=(nz // zb,), in_specs=[pl.BlockSpec(memo...]
  transfers between devices with their start and end apart: 5 -> 5, of which waited for: 3 -> 3; matrix products, arithmetic and copies ran while one was open for 16% -> 17% of each run, Pallas kernels for 35% -> 32%
where the time goes in v12:
time: 140 us
  Pallas kernels  81.5 us (58%)
  local copies, waits for them, and re-layouts  22 us (16%)
  starting transfers between devices  11.8 us (8%)
  waiting for transfers between devices  11.4 us (8%)
  other arithmetic  7.45 us (5%)
  matrix products  5.28 us (4%)
    pallas_call x1, Pallas kernels, liquid_step(): pl.pallas_call(step_kernel, grid=(nz // zb,), in_specs=[pl.BlockSpec(memo...  45.2 us
    pallas_call x1, Pallas kernels, illiquid_pick(): pl.pallas_call(illiquid_kernel, grid_spec=pltpu.PrefetchScalarGridSpec(nu...  36.3 us
    ppermute x3, waiting for transfers between devices, all_sum(): x = x + lax.ppermute(x, axis, [(i, i ^ step) for i in range(count)])  11.4 us
    reshape x1, local copies, waits for them, and re-layouts, body(): jnp.transpose(liquid_part, (3, 2, 0, 1))  9.3 us
    ppermute x3, starting transfers between devices, all_sum(): x = x + lax.ppermute(x, axis, [(i, i ^ step) for i in range(count)])  5.52 us
    ppermute x1, starting transfers between devices, edges(): lax.ppermute(tail, axis, [(i, (i + 1) % count) for i in range(ends)])  4.95 us
    dot_general x1, matrix products, body(): jnp.dot(pick_z, jnp.tile(folded, (1, columns)), precision=lax.Precision.H...  4.46 us
    slice x1, local copies, waits for them, and re-layouts, body(): head = values_in[:, :, 0, :].astype(jnp.float32)  3.06 us
  transfers between devices with their start and end apart: 5, of which 3 were waited for; matrix products, arithmetic and copies ran while one was open for 17% of the time, Pallas kernels for 32%

profile of v12, /device:TPU:0, one launch (start us, length us, event | category | flops | bytes accessed | tf_op | source)
XLA Modules:
  0.0 139.6 jit_solution(6533950811334613317)
XLA Ops:
  0.0 3.1 %fusion.7 = (bf16[8,32,1,512]{3,2,1,0:T(2,128)(2,1)S(1)}, bf16[8,32,1,512]{3,2,1,0:T(2,128)(2,1)S(1)}) fusion(bf16[8,32,64,512]{3,2,1,0:T(8,128)(2,1)} %vals_ref.1), kind=kLoop, calls=%fused_computation.40 | loop fusion | bytes 1048576 | tf_op jit(solution)/shard_map/slice | solution.py:209
  3.1 0.9 fusion.6
  4.0 4.9 %collective-permute-start = (bf16[8,32,512]{2,1,0:T(8,128)(2,1)S(1)}, bf16[8,32,512]{2,1,0:T(8,128)(2,1)S(1)}, u32[]{:S(2)}, u32[]{:S(2)}) collective-permute-start(bf16[8,32,512]{2,1,0:T(8,128)(2,1)S(1)} %get-tuple-element.8), channel_id=1, source_target_pairs={{0,4},{4,8},{8,12},{1,5},{5,9},{9,13},{2,6},{6,10},{10,14},{3,7},{... | collective-permute-start | bytes 786440 | tf_op jit(solution)/shard_map/ppermute | solution.py:184
  8.9 1.3 fusion.9
  10.3 1.3 fusion.8
  11.6 0.7 convert_bitcast_fusion
  12.9 1.8 %convert_reduce_fusion = s32[1024]{0:T(1024)S(1)} fusion(s32[4096]{0:T(1024)S(1)} %add_bitcast_fusion, s32[1024]{0:T(1024)S(1)} %iota_add_fusion), kind=kLoop, calls=%fused_computation.1 | loop fusion | flops 12581888 | bytes 24576 | tf_op jit(solution)/shard_map/reduce_sum | solution.py:246
  15.1 4.5 %fusion.w_ref = f32[4096,256]{1,0:T(8,128)} fusion(f32[64,256]{0,1:T(8,128)S(1)} %bitcast.45, s32[4096]{0:T(1024)S(1)} %copy-done.3), kind=kOutput, calls=%fused_computation.3 | convolution fusion | flops 805568512 | bytes 4276224 | tf_op jit(solution)/shard_map/dot_general | solution.py:232
  20.9 1.3 collective-permute-start.1
  22.2 0.9 constant_dynamic-slice_fusion.1
  23.1 0.7 copy.48.ca_ref
  23.9 0.9 convert_element_type.21.lo_ref
  24.7 45.2 %shard_map.154 = f32[8,32,64,128]{3,2,1,0:T(8,128)} custom-call(f32[8]{0:T(128)} %load_ref.1, bf16[8,32,64,512]{3,2,1,0:T(8,128)(2,1)} %vals_ref.1, f32[8,32,512]{2,1,0:T(8,128)} %convert_element_type.21.lo_ref, f32[8,32,512]{2,1,0:T(8,128)} %get-tuple-element.7.up_ref, f32[32,64,512]{2,1,0:T(8,128)} %rl_ref.1, f32[32,64,512]{2,1,0:T(8,128)} %ri_ref.1, ...), custom_call_target="tpu_custom_call" | custom-call | tf_op jit(solution)/shard_map/pallas_call | solution.py:102
  70.0 9.3 %copy.49.t_ref = f32[128,64,256]{2,1,0:T(8,128)} copy(f32[128,64,256]{0,1,2:T(8,128)} %bitcast.43) | data formatting | bytes 16777216 | tf_op jit(solution)/shard_map/reshape | solution.py:226
  80.0 0.9 copy.50.rim_ref
  80.9 36.3 %shard_map.155 = f32[8,4096]{1,0:T(8,128)} custom-call(s32[4096]{0:T(1024)} %get-tuple-element.18.kb_ref, s32[4096]{0:T(1024)} %get-tuple-element.17.ka_ref, bf16[256,192]{1,0:T(8,128)(2,1)} %copy.48.ca_ref, f32[128,64,256]{2,1,0:T(8,128)} %copy.49.t_ref, f32[128,2,256]{2,1,0:T(2,128)} %copy.50.rim_ref, f32[4096,256]{1,0:T(8,128)} %fusion.w_ref, ...), custom_call_target="tpu_custom_call" | custom-call | tf_op jit(solution)/shard_map/pallas_call | solution.py:158
  117.2 1.5 %collective-permute-done.2 = f32[8,4096]{1,0:T(8,128)S(1)} collective-permute-done((f32[8,4096]{1,0:T(8,128)}, f32[8,4096]{1,0:T(8,128)S(1)}, u32[]{:S(2)}, u32[]{:S(2)}) %collective-permute-start.2) | collective-permute-done | bytes 131104 | tf_op jit(solution)/shard_map/ppermute | solution.py:256
  118.7 0.9 add.57
  119.7 2.7 %collective-permute-start.3 = (f32[8,4096]{1,0:T(8,128)S(1)}, f32[8,4096]{1,0:T(8,128)S(1)}, u32[]{:S(2)}, u32[]{:S(2)}) collective-permute-start(f32[8,4096]{1,0:T(8,128)S(1)} %add.57), channel_id=1, source_target_pairs={{0,4},{4,0},{8,12},{12,8},{1,5},{5,1},{9,13},{13,9},{2,6},{6,2},{1... | collective-permute-start | bytes 393224 | tf_op jit(solution)/shard_map/ppermute | solution.py:256
  122.4 3.8 %collective-permute-done.3 = f32[8,4096]{1,0:T(8,128)S(1)} collective-permute-done((f32[8,4096]{1,0:T(8,128)S(1)}, f32[8,4096]{1,0:T(8,128)S(1)}, u32[]{:S(2)}, u32[]{:S(2)}) %collective-permute-start.3) | collective-permute-done | bytes 131104 | tf_op jit(solution)/shard_map/ppermute | solution.py:256
  126.2 2.8 %collective-permute-start.4 = (f32[8,4096]{1,0:T(8,128)S(1)}, f32[8,4096]{1,0:T(8,128)S(1)}, u32[]{:S(2)}, u32[]{:S(2)}) collective-permute-start(f32[8,4096]{1,0:T(8,128)S(1)} %add.58), channel_id=1, source_target_pairs={{0,8},{4,12},{8,0},{12,4},{1,9},{5,13},{9,1},{13,5},{2,10},{6,14},... | collective-permute-start | bytes 393224 | tf_op jit(solution)/shard_map/ppermute | solution.py:256
  129.0 6.0 %collective-permute-done.4 = f32[8,4096]{1,0:T(8,128)S(1)} collective-permute-done((f32[8,4096]{1,0:T(8,128)S(1)}, f32[8,4096]{1,0:T(8,128)S(1)}, u32[]{:S(2)}, u32[]{:S(2)}) %collective-permute-start.4) | collective-permute-done | bytes 131104 | tf_op jit(solution)/shard_map/ppermute | solution.py:256
  135.6 2.8 %gather_fusion = f32[1024,8]{1,0:T(8,128)S(1)} fusion(f32[8,4096]{0,1:T(8,128)S(1)} %copy.51, s32[1024]{0:T(1024)S(1)} %broadcast_clamp_fusion.2), kind=kCustom, calls=%fused_computation | custom fusion | bytes 69632 | tf_op jit(solution)/shard_map/jit(_take)/gather | solution.py:247
  138.8 0.8 copy.52
  (45 shorter events, 4.0 us)
Async XLA Ops:
  0.0 14.7 %copy-start = (f32[64,64]{1,0:T(8,128)S(1)}, f32[64,64]{1,0:T(8,128)}, u32[]{:S(2)}) copy-start(f32[64,64]{1,0:T(8,128)} %param.23) | copy-start | bytes 49156
  0.0 14.7 %copy-start.4 = (f32[64,64]{1,0:T(8,128)S(1)}, f32[64,64]{1,0:T(8,128)}, u32[]{:S(2)}) copy-start(f32[64,64]{1,0:T(8,128)} %constant.76.clone) | copy-start | bytes 49156
  0.0 15.0 %copy-start.3 = (s32[4096]{0:T(1024)S(1)}, s32[4096]{0:T(1024)}, u32[]{:S(2)}) copy-start(s32[4096]{0:T(1024)} %param.26) | copy-start | bytes 49156
  4.0 16.8 %collective-permute-start = (bf16[8,32,512]{2,1,0:T(8,128)(2,1)S(1)}, bf16[8,32,512]{2,1,0:T(8,128)(2,1)S(1)}, u32[]{:S(2)}, u32[]{:S(2)}) collective-permute-start(bf16[8,32,512]{2,1,0:T(8,128)(2,1)S(1)} %get-tuple-element.8), channel_id=1, source_target_pairs={{0,4},{4,8},{8,12},{1,5},{5,9},{9,13},{2,6},{6,10},{10,14},{3,7},{... | collective-permute-start | bytes 786440 | tf_op jit(solution)/shard_map/ppermute | solution.py:184
  10.3 9.3 %copy-start.5 = (s32[4096]{0:T(1024)S(1)}, s32[4096]{0:T(1024)}, u32[]{:S(2)}) copy-start(s32[4096]{0:T(1024)} %param.25) | copy-start | bytes 49156
  10.3 9.2 %copy-start.6 = (s32[4096]{0:T(1024)S(1)}, s32[4096]{0:T(1024)}, u32[]{:S(2)}) copy-start(s32[4096]{0:T(1024)} %param.24) | copy-start | bytes 49156
  20.9 58.4 %collective-permute-start.1 = (bf16[8,32,512]{2,1,0:T(8,128)(2,1)S(1)}, bf16[8,32,512]{2,1,0:T(8,128)(2,1)S(1)}, u32[]{:S(2)}, u32[]{:S(2)}) collective-permute-start(bf16[8,32,512]{2,1,0:T(8,128)(2,1)S(1)} %get-tuple-element.6), channel_id=1, source_target_pairs={{4,0},{8,4},{12,8},{5,1},{9,5},{13,9},{6,2},{10,6},{14,10},{7,3},{... | collective-permute-start | bytes 786440 | tf_op jit(solution)/shard_map/ppermute | solution.py:185
  69.9 9.4 %copy-start.2 = (f32[128,512,1,1]{1,0,3,2:T(8,128)S(1)}, f32[128,512,1,1]{1,0,3,2:T(8,128)}, u32[]{:S(2)}) copy-start(f32[128,512,1,1]{1,0,3,2:T(8,128)} %constant.77) | copy-start | bytes 786436
  80.9 58.7 %copy-start.1 = (f32[64,64]{1,0:T(8,128)S(1)}, f32[64,64]{1,0:T(8,128)}, u32[]{:S(2)}) copy-start(f32[64,64]{1,0:T(8,128)} %param.23) | copy-start | bytes 49156
  117.2 1.6 %collective-permute-start.2 = (f32[8,4096]{1,0:T(8,128)}, f32[8,4096]{1,0:T(8,128)S(1)}, u32[]{:S(2)}, u32[]{:S(2)}) collective-permute-start(f32[8,4096]{1,0:T(8,128)} %shard_map.155), channel_id=1, source_target_pairs={{0,1},{1,0},{2,3},{3,2},{4,5},{5,4},{6,7},{7,6},{8,9},{9,8},{10,11... | collective-permute-start | bytes 393224 | tf_op jit(solution)/shard_map/ppermute | solution.py:256
  119.7 6.5 %collective-permute-start.3 = (f32[8,4096]{1,0:T(8,128)S(1)}, f32[8,4096]{1,0:T(8,128)S(1)}, u32[]{:S(2)}, u32[]{:S(2)}) collective-permute-start(f32[8,4096]{1,0:T(8,128)S(1)} %add.57), channel_id=1, source_target_pairs={{0,4},{4,0},{8,12},{12,8},{1,5},{5,1},{9,13},{13,9},{2,6},{6,2},{1... | collective-permute-start | bytes 393224 | tf_op jit(solution)/shard_map/ppermute | solution.py:256
  126.2 8.8 %collective-permute-start.4 = (f32[8,4096]{1,0:T(8,128)S(1)}, f32[8,4096]{1,0:T(8,128)S(1)}, u32[]{:S(2)}, u32[]{:S(2)}) collective-permute-start(f32[8,4096]{1,0:T(8,128)S(1)} %add.58), channel_id=1, source_target_pairs={{0,8},{4,12},{8,0},{12,4},{1,9},{5,13},{9,1},{13,5},{2,10},{6,14},... | collective-permute-start | bytes 393224 | tf_op jit(solution)/shard_map/ppermute | solution.py:256

commit v13 on v12

--- a/solution.py
+++ b/solution.py
@@ -120,7 +120,7 @@
     )(load, vals, lower, upper, rl, ri, pf, ml, mi, tb)
 
 
-def illiquid_kernel(kb_ref, ka_ref, ca_ref, t_ref, rim_ref, w_ref, group_ref, out_ref, spectrum, picked):
+def illiquid_kernel(row_ref, ca_ref, t_ref, rim_ref, w_ref, group_ref, out_ref, spectrum, picked):
     j = pl.program_id(0)
     block, na_loc, lanes = t_ref.shape
     stacked = ca_ref[...]
@@ -130,12 +130,13 @@
         t = t_ref[k] + jnp.where(row == 0, rim[0:1], 0.0)
         th, tl = split_bf16(t + jnp.where(row == na_loc - 1, rim[1:2], 0.0))
         rhs = jnp.concatenate([th, th, tl], axis=0)
-        spectrum[j * block + k] = jnp.dot(stacked, rhs, preferred_element_type=jnp.float32)
+        start = pl.multiple_of((j * block + k) * stacked.shape[0], stacked.shape[0])
+        spectrum[pl.ds(start, stacked.shape[0]), :] = jnp.dot(stacked, rhs, preferred_element_type=jnp.float32)
 
     @pl.when(j == pl.num_programs(0) - 1)
     def _():
         def pick(i, carry):
-            picked[pl.ds(i, 1), :] = spectrum[kb_ref[i], pl.ds(ka_ref[i], 1), :]
+            picked[pl.ds(i, 1), :] = spectrum[pl.ds(row_ref[i], 1), :]
             return carry
 
         lax.fori_loop(0, picked.shape[0], pick, 0, unroll=8)
@@ -150,15 +151,15 @@
         out_ref[...] = total
 
 
-def illiquid_pick(ca, t, rim, weight, group, kb_index, ka_index):
+def illiquid_pick(ca, t, rim, weight, group, row_index):
     kb, na_loc, lanes = t.shape
     na, depth = ca.shape
-    count = kb_index.shape[0]
+    count = row_index.shape[0]
     block = 8
     return pl.pallas_call(
         illiquid_kernel,
         grid_spec=pltpu.PrefetchScalarGridSpec(
-            num_scalar_prefetch=2,
+            num_scalar_prefetch=1,
             grid=(kb // block,),
             in_specs=[
                 pl.BlockSpec((na, depth), lambda j, *_: (0, 0)),
@@ -168,11 +169,11 @@
                 pl.BlockSpec(group.shape, lambda j, *_: (0, 0)),
             ],
             out_specs=pl.BlockSpec((group.shape[0], count), lambda j, *_: (0, 0)),
-            scratch_shapes=[pltpu.VMEM((kb, na, lanes), jnp.float32), pltpu.VMEM((count, lanes), jnp.float32)],
+            scratch_shapes=[pltpu.VMEM((kb * na, lanes), jnp.float32), pltpu.VMEM((count, lanes), jnp.float32)],
         ),
         out_shape=jax.ShapeDtypeStruct((group.shape[0], count), jnp.float32),
         compiler_params=pltpu.CompilerParams(vmem_limit_bytes=60 * 1024 * 1024),
-    )(kb_index, ka_index, ca, t, rim, weight, group)
+    )(row_index, ca, t, rim, weight, group)
 
 
 def edges(values, axis, dim):
@@ -234,7 +235,7 @@
     group = (jnp.arange(lanes)[None, :] // nz_loc == jnp.arange(columns)[:, None]).astype(jnp.bfloat16)
     partial = illiquid_pick(
         table_a, liquid_part, rim, weight, group,
-        jnp.clip(coef_liquid, 0, KBLOW - 1), jnp.clip(coef_illiquid, 0, NA - 1),
+        jnp.clip(coef_liquid, 0, KBLOW - 1) * NA + jnp.clip(coef_illiquid, 0, NA - 1),
     )
     kept = all_sum(partial, ("inc", "wide"))
     owners = lax.axis_size(("wide", "inc"))

time: 140 us -> 137 us (0.979)
  Pallas kernels: 81.5 us -> 78.3 us
    pallas_call x1, Pallas kernels: 36.3 us -> 33.1 us  [illiquid_pick(): pl.pallas_call(illiquid_kernel, grid_spec=pltpu.PrefetchScalarGridSpec(nu...]
  transfers between devices with their start and end apart: 5 -> 5, of which waited for: 3 -> 3; matrix products, arithmetic and copies ran while one was open for 17% -> 17% of each run, Pallas kernels for 32% -> 33%
where the time goes in v13:
time: 137 us; the launch traced here: 136 us
  Pallas kernels  78.3 us (57%)
  local copies, waits for them, and re-layouts  22 us (16%)
  starting transfers between devices  11.8 us (9%)
  waiting for transfers between devices  11.4 us (8%)
  other arithmetic  7.46 us (5%)
  matrix products  5.28 us (4%)
    pallas_call x1, Pallas kernels, liquid_step(): pl.pallas_call(step_kernel, grid=(nz // zb,), in_specs=[pl.BlockSpec(memo...  45.2 us
    pallas_call x1, Pallas kernels, illiquid_pick(): pl.pallas_call(illiquid_kernel, grid_spec=pltpu.PrefetchScalarGridSpec(nu...  33.1 us
    ppermute x3, waiting for transfers between devices, all_sum(): x = x + lax.ppermute(x, axis, [(i, i ^ step) for i in range(count)])  11.3 us
    reshape x1, local copies, waits for them, and re-layouts, body(): jnp.transpose(liquid_part, (3, 2, 0, 1))  9.3 us
    ppermute x3, starting transfers between devices, all_sum(): x = x + lax.ppermute(x, axis, [(i, i ^ step) for i in range(count)])  5.52 us
    ppermute x1, starting transfers between devices, edges(): lax.ppermute(tail, axis, [(i, (i + 1) % count) for i in range(ends)])  4.95 us
    dot_general x1, matrix products, body(): jnp.dot(pick_z, jnp.tile(folded, (1, columns)), precision=lax.Precision.H...  4.47 us
    slice x1, local copies, waits for them, and re-layouts, body(): head = values_in[:, :, 0, :].astype(jnp.float32)  3.06 us
  transfers between devices with their start and end apart: 5, of which 3 were waited for; matrix products, arithmetic and copies ran while one was open for 17% of the time, Pallas kernels for 33%

profile of v13, /device:TPU:0, one launch (start us, length us, event | category | flops | bytes accessed | tf_op | source)
XLA Modules:
  0.0 136.4 jit_solution(15523560218468007948)
XLA Ops:
  0.0 3.1 %fusion.7 = (bf16[8,32,1,512]{3,2,1,0:T(2,128)(2,1)S(1)}, bf16[8,32,1,512]{3,2,1,0:T(2,128)(2,1)S(1)}) fusion(bf16[8,32,64,512]{3,2,1,0:T(8,128)(2,1)} %vals_ref.1), kind=kLoop, calls=%fused_computation.39 | loop fusion | bytes 1048576 | tf_op jit(solution)/shard_map/slice | solution.py:210
  3.1 0.9 fusion.6
  4.0 4.9 %collective-permute-start = (bf16[8,32,512]{2,1,0:T(8,128)(2,1)S(1)}, bf16[8,32,512]{2,1,0:T(8,128)(2,1)S(1)}, u32[]{:S(2)}, u32[]{:S(2)}) collective-permute-start(bf16[8,32,512]{2,1,0:T(8,128)(2,1)S(1)} %get-tuple-element.8), channel_id=1, source_target_pairs={{0,4},{4,8},{8,12},{1,5},{5,9},{9,13},{2,6},{6,10},{10,14},{3,7},{... | collective-permute-start | bytes 786440 | tf_op jit(solution)/shard_map/ppermute | solution.py:185
  8.9 1.3 fusion.9
  10.3 1.3 fusion.8
  11.6 0.7 convert_bitcast_fusion
  12.9 1.8 %convert_reduce_fusion = s32[1024]{0:T(1024)S(1)} fusion(s32[4096]{0:T(1024)S(1)} %add_bitcast_fusion, s32[1024]{0:T(1024)S(1)} %iota_add_fusion), kind=kLoop, calls=%fused_computation.1 | loop fusion | flops 12581888 | bytes 24576 | tf_op jit(solution)/shard_map/reduce_sum | solution.py:247
  15.1 4.5 %fusion.w_ref = f32[4096,256]{1,0:T(8,128)} fusion(f32[64,256]{0,1:T(8,128)S(1)} %bitcast.45, s32[4096]{0:T(1024)S(1)} %copy-done.3), kind=kOutput, calls=%fused_computation.3 | convolution fusion | flops 805568512 | bytes 4276224 | tf_op jit(solution)/shard_map/dot_general | solution.py:233
  20.9 1.3 collective-permute-start.1
  22.2 0.9 constant_dynamic-slice_fusion.1
  23.1 0.7 copy.48.ca_ref
  23.9 0.9 convert_element_type.21.lo_ref
  24.7 45.2 %shard_map.154 = f32[8,32,64,128]{3,2,1,0:T(8,128)} custom-call(f32[8]{0:T(128)} %load_ref.1, bf16[8,32,64,512]{3,2,1,0:T(8,128)(2,1)} %vals_ref.1, f32[8,32,512]{2,1,0:T(8,128)} %convert_element_type.21.lo_ref, f32[8,32,512]{2,1,0:T(8,128)} %get-tuple-element.7.up_ref, f32[32,64,512]{2,1,0:T(8,128)} %rl_ref.1, f32[32,64,512]{2,1,0:T(8,128)} %ri_ref.1, ...), custom_call_target="tpu_custom_call" | custom-call | tf_op jit(solution)/shard_map/pallas_call | solution.py:102
  70.0 9.3 %copy.49.t_ref = f32[128,64,256]{2,1,0:T(8,128)} copy(f32[128,64,256]{0,1,2:T(8,128)} %bitcast.43) | data formatting | bytes 16777216 | tf_op jit(solution)/shard_map/reshape | solution.py:227
  80.0 0.9 copy.50.rim_ref
  80.9 33.1 %shard_map.155 = f32[8,4096]{1,0:T(8,128)} custom-call(s32[4096]{0:T(1024)} %clamp_add_fusion.row_ref, bf16[256,192]{1,0:T(8,128)(2,1)} %copy.48.ca_ref, f32[128,64,256]{2,1,0:T(8,128)} %copy.49.t_ref, f32[128,2,256]{2,1,0:T(2,128)} %copy.50.rim_ref, f32[4096,256]{1,0:T(8,128)} %fusion.w_ref, bf16[8,256]{1,0:T(8,128)(2,1)} %fusion.5.group_ref), custom_call_target="tpu_custom_call" | custom-call | tf_op jit(solution)/shard_map/pallas_call | solution.py:159
  114.0 1.5 %collective-permute-done.2 = f32[8,4096]{1,0:T(8,128)S(1)} collective-permute-done((f32[8,4096]{1,0:T(8,128)}, f32[8,4096]{1,0:T(8,128)S(1)}, u32[]{:S(2)}, u32[]{:S(2)}) %collective-permute-start.2) | collective-permute-done | bytes 131104 | tf_op jit(solution)/shard_map/ppermute | solution.py:257
  115.5 0.9 add.61
  116.5 2.7 %collective-permute-start.3 = (f32[8,4096]{1,0:T(8,128)S(1)}, f32[8,4096]{1,0:T(8,128)S(1)}, u32[]{:S(2)}, u32[]{:S(2)}) collective-permute-start(f32[8,4096]{1,0:T(8,128)S(1)} %add.61), channel_id=1, source_target_pairs={{0,4},{4,0},{8,12},{12,8},{1,5},{5,1},{9,13},{13,9},{2,6},{6,2},{1... | collective-permute-start | bytes 393224 | tf_op jit(solution)/shard_map/ppermute | solution.py:257
  119.2 3.8 %collective-permute-done.3 = f32[8,4096]{1,0:T(8,128)S(1)} collective-permute-done((f32[8,4096]{1,0:T(8,128)S(1)}, f32[8,4096]{1,0:T(8,128)S(1)}, u32[]{:S(2)}, u32[]{:S(2)}) %collective-permute-start.3) | collective-permute-done | bytes 131104 | tf_op jit(solution)/shard_map/ppermute | solution.py:257
  123.0 2.8 %collective-permute-start.4 = (f32[8,4096]{1,0:T(8,128)S(1)}, f32[8,4096]{1,0:T(8,128)S(1)}, u32[]{:S(2)}, u32[]{:S(2)}) collective-permute-start(f32[8,4096]{1,0:T(8,128)S(1)} %add.62), channel_id=1, source_target_pairs={{0,8},{4,12},{8,0},{12,4},{1,9},{5,13},{9,1},{13,5},{2,10},{6,14},... | collective-permute-start | bytes 393224 | tf_op jit(solution)/shard_map/ppermute | solution.py:257
  125.8 6.0 %collective-permute-done.4 = f32[8,4096]{1,0:T(8,128)S(1)} collective-permute-done((f32[8,4096]{1,0:T(8,128)S(1)}, f32[8,4096]{1,0:T(8,128)S(1)}, u32[]{:S(2)}, u32[]{:S(2)}) %collective-permute-start.4) | collective-permute-done | bytes 131104 | tf_op jit(solution)/shard_map/ppermute | solution.py:257
  132.4 2.8 %gather_fusion = f32[1024,8]{1,0:T(8,128)S(1)} fusion(f32[8,4096]{0,1:T(8,128)S(1)} %copy.51, s32[1024]{0:T(1024)S(1)} %broadcast_clamp_fusion), kind=kCustom, calls=%fused_computation | custom fusion | bytes 69632 | tf_op jit(solution)/shard_map/jit(_take)/gather | solution.py:248
  135.6 0.8 copy.52
  (45 shorter events, 4.0 us)
Async XLA Ops:
  0.0 14.7 %copy-start = (f32[64,64]{1,0:T(8,128)S(1)}, f32[64,64]{1,0:T(8,128)}, u32[]{:S(2)}) copy-start(f32[64,64]{1,0:T(8,128)} %param.23) | copy-start | bytes 49156
  0.0 14.7 %copy-start.4 = (f32[64,64]{1,0:T(8,128)S(1)}, f32[64,64]{1,0:T(8,128)}, u32[]{:S(2)}) copy-start(f32[64,64]{1,0:T(8,128)} %constant.77.clone) | copy-start | bytes 49156
  0.0 15.0 %copy-start.3 = (s32[4096]{0:T(1024)S(1)}, s32[4096]{0:T(1024)}, u32[]{:S(2)}) copy-start(s32[4096]{0:T(1024)} %param.26) | copy-start | bytes 49156
  4.0 16.8 %collective-permute-start = (bf16[8,32,512]{2,1,0:T(8,128)(2,1)S(1)}, bf16[8,32,512]{2,1,0:T(8,128)(2,1)S(1)}, u32[]{:S(2)}, u32[]{:S(2)}) collective-permute-start(bf16[8,32,512]{2,1,0:T(8,128)(2,1)S(1)} %get-tuple-element.8), channel_id=1, source_target_pairs={{0,4},{4,8},{8,12},{1,5},{5,9},{9,13},{2,6},{6,10},{10,14},{3,7},{... | collective-permute-start | bytes 786440 | tf_op jit(solution)/shard_map/ppermute | solution.py:185
  10.3 9.3 %copy-start.5 = (s32[4096]{0:T(1024)S(1)}, s32[4096]{0:T(1024)}, u32[]{:S(2)}) copy-start(s32[4096]{0:T(1024)} %param.25) | copy-start | bytes 49156
  10.3 9.3 %copy-start.6 = (s32[4096]{0:T(1024)S(1)}, s32[4096]{0:T(1024)}, u32[]{:S(2)}) copy-start(s32[4096]{0:T(1024)} %param.24) | copy-start | bytes 49156
  20.9 58.4 %collective-permute-start.1 = (bf16[8,32,512]{2,1,0:T(8,128)(2,1)S(1)}, bf16[8,32,512]{2,1,0:T(8,128)(2,1)S(1)}, u32[]{:S(2)}, u32[]{:S(2)}) collective-permute-start(bf16[8,32,512]{2,1,0:T(8,128)(2,1)S(1)} %get-tuple-element.6), channel_id=1, source_target_pairs={{4,0},{8,4},{12,8},{5,1},{9,5},{13,9},{6,2},{10,6},{14,10},{7,3},{... | collective-permute-start | bytes 786440 | tf_op jit(solution)/shard_map/ppermute | solution.py:186
  70.0 9.4 %copy-start.2 = (f32[128,512,1,1]{1,0,3,2:T(8,128)S(1)}, f32[128,512,1,1]{1,0,3,2:T(8,128)}, u32[]{:S(2)}) copy-start(f32[128,512,1,1]{1,0,3,2:T(8,128)} %constant.78) | copy-start | bytes 786436
  80.9 55.5 %copy-start.1 = (f32[64,64]{1,0:T(8,128)S(1)}, f32[64,64]{1,0:T(8,128)}, u32[]{:S(2)}) copy-start(f32[64,64]{1,0:T(8,128)} %param.23) | copy-start | bytes 49156
  114.0 1.6 %collective-permute-start.2 = (f32[8,4096]{1,0:T(8,128)}, f32[8,4096]{1,0:T(8,128)S(1)}, u32[]{:S(2)}, u32[]{:S(2)}) collective-permute-start(f32[8,4096]{1,0:T(8,128)} %shard_map.155), channel_id=1, source_target_pairs={{0,1},{1,0},{2,3},{3,2},{4,5},{5,4},{6,7},{7,6},{8,9},{9,8},{10,11... | collective-permute-start | bytes 393224 | tf_op jit(solution)/shard_map/ppermute | solution.py:257
  116.5 6.5 %collective-permute-start.3 = (f32[8,4096]{1,0:T(8,128)S(1)}, f32[8,4096]{1,0:T(8,128)S(1)}, u32[]{:S(2)}, u32[]{:S(2)}) collective-permute-start(f32[8,4096]{1,0:T(8,128)S(1)} %add.61), channel_id=1, source_target_pairs={{0,4},{4,0},{8,12},{12,8},{1,5},{5,1},{9,13},{13,9},{2,6},{6,2},{1... | collective-permute-start | bytes 393224 | tf_op jit(solution)/shard_map/ppermute | solution.py:257
  123.0 8.8 %collective-permute-start.4 = (f32[8,4096]{1,0:T(8,128)S(1)}, f32[8,4096]{1,0:T(8,128)S(1)}, u32[]{:S(2)}, u32[]{:S(2)}) collective-permute-start(f32[8,4096]{1,0:T(8,128)S(1)} %add.62), channel_id=1, source_target_pairs={{0,8},{4,12},{8,0},{12,4},{1,9},{5,13},{9,1},{13,5},{2,10},{6,14},... | collective-permute-start | bytes 393224 | tf_op jit(solution)/shard_map/ppermute | solution.py:257

commit v14 on v13

--- a/solution.py
+++ b/solution.py
@@ -51,7 +51,7 @@
     return hi, (x - hi.astype(jnp.float32)).astype(jnp.bfloat16)
 
 
-def step_kernel(load_ref, vals_ref, lo_ref, up_ref, rl_ref, ri_ref, pf_ref, ml_ref, mi_ref, tb_ref, out_ref):
+def step_kernel(load_ref, vals_ref, rl_ref, ri_ref, pf_ref, ml_ref, mi_ref, tb_ref, out_ref):
     columns = vals_ref.shape[0]
     zb, na, nb = rl_ref.shape
     kb = tb_ref.shape[1]
@@ -65,8 +65,8 @@
     arow = lax.broadcasted_iota(jnp.int32, (zb, na, nb), 1).reshape(rows, nb)
     next_b = mb & (col != nb - 1)
     prev_b = jnp.logical_not(mb) & (col != 0)
-    top = arow == na - 1
-    bottom = arow == 0
+    next_a = ma & (arow != na - 1)
+    prev_a = jnp.logical_not(ma) & (arow != 0)
     th, tl = split_bf16(tb_ref[...])
     both = jnp.concatenate([th, tl], axis=1)
 
@@ -79,12 +79,8 @@
 
     def per_column(c, carry):
         v = vals_ref[c].reshape(rows, nb).astype(jnp.float32)
-        lo = jnp.broadcast_to(lo_ref[c][:, None, :], (zb, na, nb)).reshape(rows, nb)
-        up = jnp.broadcast_to(up_ref[c][:, None, :], (zb, na, nb)).reshape(rows, nb)
         side_b = jnp.where(next_b, pltpu.roll(v, nb - 1, 1), jnp.where(prev_b, pltpu.roll(v, 1, 1), v))
-        above = jnp.where(top, up, pltpu.roll(v, rows - 1, 0))
-        below = jnp.where(bottom, lo, pltpu.roll(v, 1, 0))
-        side_a = jnp.where(ma, above, below)
+        side_a = jnp.where(next_a, pltpu.roll(v, rows - 1, 0), jnp.where(prev_a, pltpu.roll(v, 1, 0), v))
         explicit = v + rl * (side_b - v) + ri * (side_a - v)
         out_ref[c] = (transform(explicit) + load_ref[c] * price).reshape(zb, na, kb)
         return carry
@@ -92,12 +88,11 @@
     lax.fori_loop(0, columns, per_column, 0)
 
 
-def liquid_step(load, vals, lower, upper, rl, ri, pf, ml, mi, tb):
+def liquid_step(load, vals, rl, ri, pf, ml, mi, tb):
     columns, nz, na, nb = vals.shape
     kb = tb.shape[1]
     zb = min(Z_BLOCK, nz)
     field = pl.BlockSpec((zb, na, nb), lambda j: (j, 0, 0))
-    edge = pl.BlockSpec((columns, zb, nb), lambda j: (0, j, 0))
     table = pl.BlockSpec((nb, kb), lambda j: (0, 0))
     return pl.pallas_call(
         step_kernel,
@@ -105,8 +100,6 @@
         in_specs=[
             pl.BlockSpec(memory_space=pltpu.SMEM),
             pl.BlockSpec((columns, zb, na, nb), lambda j: (0, j, 0, 0)),
-            edge,
-            edge,
             field,
             field,
             field,
@@ -117,7 +110,7 @@
         out_specs=pl.BlockSpec((columns, zb, na, kb), lambda j: (0, j, 0, 0)),
         out_shape=jax.ShapeDtypeStruct((columns, nz, na, kb), jnp.float32),
         compiler_params=pltpu.CompilerParams(vmem_limit_bytes=56 * 1024 * 1024),
-    )(load, vals, lower, upper, rl, ri, pf, ml, mi, tb)
+    )(load, vals, rl, ri, pf, ml, mi, tb)
 
 
 def illiquid_kernel(row_ref, ca_ref, t_ref, rim_ref, w_ref, group_ref, out_ref, spectrum, picked):
@@ -212,7 +205,7 @@
     lower, upper = edges(values_in, "wide", 2)
     table_b = cosine_constant(NB)[:KBLOW]
     liquid_part = liquid_step(
-        shock_load, values_in, head, tail, rate_liquid, rate_illiquid, price_field,
+        shock_load, values_in, rate_liquid, rate_illiquid, price_field,
         mask_liquid, mask_illiquid, jnp.asarray(table_b.T),
     )
     rim = jnp.stack(

time: 137 us -> 140 us (1.022)
  Pallas kernels: 78.3 us -> 80.4 us
    pallas_call x1, Pallas kernels: 45.2 us -> 47.3 us  [liquid_step(): pl.pallas_call(step_kernel, grid=(nz // zb,), in_specs=[pl.BlockSpec(memo...]
    convert_element_type x2 -> x0, other arithmetic: 1.74 us -> none  [the longest x1 0.88 us: body(): tail = values_in[:, :, na_loc - 1, :].astype(jnp.float32)]
  transfers between devices with their start and end apart: 5 -> 5, of which waited for: 3 -> 3; matrix products, arithmetic and copies ran while one was open for 17% -> 18% of each run, Pallas kernels for 33% -> 34%
where the time goes in v14:
time: 140 us; the launch traced here: 139 us
  Pallas kernels  80.4 us (57%)
  local copies, waits for them, and re-layouts  22.2 us (16%)
  starting transfers between devices  11.8 us (8%)
  waiting for transfers between devices  11.4 us (8%)
  matrix products  6.49 us (5%)
  other arithmetic  6.45 us (5%)
    pallas_call x1, Pallas kernels, liquid_step(): pl.pallas_call(step_kernel, grid=(nz // zb,), in_specs=[pl.BlockSpec(memo...  47.3 us
    pallas_call x1, Pallas kernels, illiquid_pick(): pl.pallas_call(illiquid_kernel, grid_spec=pltpu.PrefetchScalarGridSpec(nu...  33.1 us
    ppermute x3, waiting for transfers between devices, all_sum(): x = x + lax.ppermute(x, axis, [(i, i ^ step) for i in range(count)])  11.4 us
    reshape x1, local copies, waits for them, and re-layouts, body(): jnp.transpose(liquid_part, (3, 2, 0, 1))  9.31 us
    ppermute x3, starting transfers between devices, all_sum(): x = x + lax.ppermute(x, axis, [(i, i ^ step) for i in range(count)])  5.52 us
    ppermute x1, starting transfers between devices, edges(): lax.ppermute(tail, axis, [(i, (i + 1) % count) for i in range(ends)])  4.94 us
    dot_general x1, matrix products, body(): jnp.dot(pick_z, jnp.tile(folded, (1, columns)), precision=lax.Precision.H...  4.92 us
    slice x1, local copies, waits for them, and re-layouts, edges(): head = lax.index_in_dim(values, 0, axis=dim, keepdims=False)  3.27 us
  transfers between devices with their start and end apart: 5, of which 3 were waited for; matrix products, arithmetic and copies ran while one was open for 18% of the time, Pallas kernels for 34%

profile of v14, /device:TPU:0, one launch (start us, length us, event | category | flops | bytes accessed | tf_op | source)
XLA Modules:
  0.0 138.9 jit_solution(5753474190794403986)
XLA Ops:
  0.0 3.3 %fusion.9 = (bf16[8,32,1,512]{3,2,1,0:T(2,128)(2,1)S(1)}, bf16[8,32,1,512]{3,2,1,0:T(2,128)(2,1)S(1)}) fusion(bf16[8,32,64,512]{3,2,1,0:T(8,128)(2,1)} %vals_ref.1), kind=kLoop, calls=%fused_computation.40 | loop fusion | bytes 1048576 | tf_op jit(solution)/shard_map/slice | solution.py:176
  3.3 4.9 %collective-permute-start = (bf16[8,32,512]{2,1,0:T(8,128)(2,1)S(1)}, bf16[8,32,512]{2,1,0:T(8,128)(2,1)S(1)}, u32[]{:S(2)}, u32[]{:S(2)}) collective-permute-start(bf16[8,32,512]{2,1,0:T(8,128)(2,1)S(1)} %bitcast.51), channel_id=1, source_target_pairs={{0,4},{4,8},{8,12},{1,5},{5,9},{9,13},{2,6},{6,10},{10,14},{3,7},{... | collective-permute-start | bytes 786440 | tf_op jit(solution)/shard_map/ppermute | solution.py:178
  8.3 1.3 fusion.11
  9.6 1.3 fusion.10
  11.0 0.7 convert_bitcast_fusion
  12.3 1.8 %convert_reduce_fusion = s32[1024]{0:T(1024)S(1)} fusion(s32[4096]{0:T(1024)S(1)} %add_bitcast_fusion, s32[1024]{0:T(1024)S(1)} %iota_add_fusion), kind=kLoop, calls=%fused_computation.1 | loop fusion | flops 12581888 | bytes 24576 | tf_op jit(solution)/shard_map/reduce_sum | solution.py:240
  14.1 1.4 clamp_add_fusion.row_ref
  15.4 1.0 fusion.12
  16.5 4.9 %fusion.w_ref = f32[4096,256]{1,0:T(8,128)} fusion(f32[64,256]{0,1:T(8,128)S(1)} %bitcast.49, s32[4096]{0:T(1024)} %param.26), kind=kOutput, calls=%fused_computation.3 | convolution fusion | flops 805568512 | bytes 4276224 | tf_op jit(solution)/shard_map/dot_general | solution.py:226
  22.1 1.3 collective-permute-start.1
  23.4 0.9 constant_dynamic-slice_fusion.1
  24.4 0.7 copy.48.ca_ref
  25.1 47.3 %shard_map.154 = f32[8,32,64,128]{3,2,1,0:T(8,128)} custom-call(f32[8]{0:T(128)} %load_ref.1, bf16[8,32,64,512]{3,2,1,0:T(8,128)(2,1)} %vals_ref.1, f32[32,64,512]{2,1,0:T(8,128)} %rl_ref.1, f32[32,64,512]{2,1,0:T(8,128)} %ri_ref.1, f32[32,64,512]{2,1,0:T(8,128)} %pf_ref.1, s32[32,64,512]{2,1,0:T(8,128)} %ml_ref.1, s32[32,64,512]{2,1,0:T(8,128)} %mi_ref.1, ...), custom_call_target="tpu_custom_call" | custom-call | tf_op jit(solution)/shard_map/pallas_call | solution.py:97
  72.4 9.3 %copy.49.t_ref = f32[128,64,256]{2,1,0:T(8,128)} copy(f32[128,64,256]{0,1,2:T(8,128)} %bitcast.47) | data formatting | bytes 16777216 | tf_op jit(solution)/shard_map/reshape | solution.py:220
  82.5 0.9 copy.50.rim_ref
  83.4 33.1 %shard_map.155 = f32[8,4096]{1,0:T(8,128)} custom-call(s32[4096]{0:T(1024)} %clamp_add_fusion.row_ref, bf16[256,192]{1,0:T(8,128)(2,1)} %copy.48.ca_ref, f32[128,64,256]{2,1,0:T(8,128)} %copy.49.t_ref, f32[128,2,256]{2,1,0:T(2,128)} %copy.50.rim_ref, f32[4096,256]{1,0:T(8,128)} %fusion.w_ref, bf16[8,256]{1,0:T(8,128)(2,1)} %fusion.7.group_ref), custom_call_target="tpu_custom_call" | custom-call | tf_op jit(solution)/shard_map/pallas_call | solution.py:152
  116.5 1.5 %collective-permute-done.2 = f32[8,4096]{1,0:T(8,128)S(1)} collective-permute-done((f32[8,4096]{1,0:T(8,128)}, f32[8,4096]{1,0:T(8,128)S(1)}, u32[]{:S(2)}, u32[]{:S(2)}) %collective-permute-start.2) | collective-permute-done | bytes 131104 | tf_op jit(solution)/shard_map/ppermute | solution.py:250
  118.0 0.9 add.61
  118.9 2.7 %collective-permute-start.3 = (f32[8,4096]{1,0:T(8,128)S(1)}, f32[8,4096]{1,0:T(8,128)S(1)}, u32[]{:S(2)}, u32[]{:S(2)}) collective-permute-start(f32[8,4096]{1,0:T(8,128)S(1)} %add.61), channel_id=1, source_target_pairs={{0,4},{4,0},{8,12},{12,8},{1,5},{5,1},{9,13},{13,9},{2,6},{6,2},{1... | collective-permute-start | bytes 393224 | tf_op jit(solution)/shard_map/ppermute | solution.py:250
  121.7 3.8 %collective-permute-done.3 = f32[8,4096]{1,0:T(8,128)S(1)} collective-permute-done((f32[8,4096]{1,0:T(8,128)S(1)}, f32[8,4096]{1,0:T(8,128)S(1)}, u32[]{:S(2)}, u32[]{:S(2)}) %collective-permute-start.3) | collective-permute-done | bytes 131104 | tf_op jit(solution)/shard_map/ppermute | solution.py:250
  125.5 2.8 %collective-permute-start.4 = (f32[8,4096]{1,0:T(8,128)S(1)}, f32[8,4096]{1,0:T(8,128)S(1)}, u32[]{:S(2)}, u32[]{:S(2)}) collective-permute-start(f32[8,4096]{1,0:T(8,128)S(1)} %add.62), channel_id=1, source_target_pairs={{0,8},{4,12},{8,0},{12,4},{1,9},{5,13},{9,1},{13,5},{2,10},{6,14},... | collective-permute-start | bytes 393224 | tf_op jit(solution)/shard_map/ppermute | solution.py:250
  128.3 6.0 %collective-permute-done.4 = f32[8,4096]{1,0:T(8,128)S(1)} collective-permute-done((f32[8,4096]{1,0:T(8,128)S(1)}, f32[8,4096]{1,0:T(8,128)S(1)}, u32[]{:S(2)}, u32[]{:S(2)}) %collective-permute-start.4) | collective-permute-done | bytes 131104 | tf_op jit(solution)/shard_map/ppermute | solution.py:250
  134.9 2.8 %gather_fusion = f32[1024,8]{1,0:T(8,128)S(1)} fusion(f32[8,4096]{0,1:T(8,128)S(1)} %copy.51, s32[1024]{0:T(1024)S(1)} %broadcast_clamp_fusion), kind=kCustom, calls=%fused_computation | custom fusion | bytes 69632 | tf_op jit(solution)/shard_map/jit(_take)/gather | solution.py:241
  138.1 0.8 copy.52
  (36 shorter events, 3.1 us)
Async XLA Ops:
  0.0 15.4 %copy-start = (f32[64,64]{1,0:T(8,128)S(1)}, f32[64,64]{1,0:T(8,128)}, u32[]{:S(2)}) copy-start(f32[64,64]{1,0:T(8,128)} %param.23) | copy-start | bytes 49156
  3.3 18.7 %collective-permute-start = (bf16[8,32,512]{2,1,0:T(8,128)(2,1)S(1)}, bf16[8,32,512]{2,1,0:T(8,128)(2,1)S(1)}, u32[]{:S(2)}, u32[]{:S(2)}) collective-permute-start(bf16[8,32,512]{2,1,0:T(8,128)(2,1)S(1)} %bitcast.51), channel_id=1, source_target_pairs={{0,4},{4,8},{8,12},{1,5},{5,9},{9,13},{2,6},{6,10},{10,14},{3,7},{... | collective-permute-start | bytes 786440 | tf_op jit(solution)/shard_map/ppermute | solution.py:178
  22.1 59.6 %collective-permute-start.1 = (bf16[8,32,512]{2,1,0:T(8,128)(2,1)S(1)}, bf16[8,32,512]{2,1,0:T(8,128)(2,1)S(1)}, u32[]{:S(2)}, u32[]{:S(2)}) collective-permute-start(bf16[8,32,512]{2,1,0:T(8,128)(2,1)S(1)} %get-tuple-element.6), channel_id=1, source_target_pairs={{4,0},{8,4},{12,8},{5,1},{9,5},{13,9},{6,2},{10,6},{14,10},{7,3},{... | collective-permute-start | bytes 786440 | tf_op jit(solution)/shard_map/ppermute | solution.py:179
  72.4 9.5 %copy-start.2 = (f32[128,512,1,1]{1,0,3,2:T(8,128)S(1)}, f32[128,512,1,1]{1,0,3,2:T(8,128)}, u32[]{:S(2)}) copy-start(f32[128,512,1,1]{1,0,3,2:T(8,128)} %constant.78) | copy-start | bytes 786436
  83.4 55.5 %copy-start.1 = (f32[64,64]{1,0:T(8,128)S(1)}, f32[64,64]{1,0:T(8,128)}, u32[]{:S(2)}) copy-start(f32[64,64]{1,0:T(8,128)} %param.23) | copy-start | bytes 49156
  116.5 1.6 %collective-permute-start.2 = (f32[8,4096]{1,0:T(8,128)}, f32[8,4096]{1,0:T(8,128)S(1)}, u32[]{:S(2)}, u32[]{:S(2)}) collective-permute-start(f32[8,4096]{1,0:T(8,128)} %shard_map.155), channel_id=1, source_target_pairs={{0,1},{1,0},{2,3},{3,2},{4,5},{5,4},{6,7},{7,6},{8,9},{9,8},{10,11... | collective-permute-start | bytes 393224 | tf_op jit(solution)/shard_map/ppermute | solution.py:250
  118.9 6.5 %collective-permute-start.3 = (f32[8,4096]{1,0:T(8,128)S(1)}, f32[8,4096]{1,0:T(8,128)S(1)}, u32[]{:S(2)}, u32[]{:S(2)}) collective-permute-start(f32[8,4096]{1,0:T(8,128)S(1)} %add.61), channel_id=1, source_target_pairs={{0,4},{4,0},{8,12},{12,8},{1,5},{5,1},{9,13},{13,9},{2,6},{6,2},{1... | collective-permute-start | bytes 393224 | tf_op jit(solution)/shard_map/ppermute | solution.py:250
  125.5 8.8 %collective-permute-start.4 = (f32[8,4096]{1,0:T(8,128)S(1)}, f32[8,4096]{1,0:T(8,128)S(1)}, u32[]{:S(2)}, u32[]{:S(2)}) collective-permute-start(f32[8,4096]{1,0:T(8,128)S(1)} %add.62), channel_id=1, source_target_pairs={{0,8},{4,12},{8,0},{12,4},{1,9},{5,13},{9,1},{13,5},{2,10},{6,14},... | collective-permute-start | bytes 393224 | tf_op jit(solution)/shard_map/ppermute | solution.py:250

commit v15 on v13

--- a/solution.py
+++ b/solution.py
@@ -139,7 +139,7 @@
             picked[pl.ds(i, 1), :] = spectrum[pl.ds(row_ref[i], 1), :]
             return carry
 
-        lax.fori_loop(0, picked.shape[0], pick, 0, unroll=8)
+        lax.fori_loop(0, picked.shape[0], pick, 0, unroll=32)
         rest = picked[...] * w_ref[...]
         group = group_ref[...]
         total = None

time: 137 us -> 136 us (level)
  Pallas kernels: 78.3 us -> 76.7 us
    pallas_call x1, Pallas kernels: 33.1 us -> 31.5 us  [illiquid_pick(): pl.pallas_call(illiquid_kernel, grid_spec=pltpu.PrefetchScalarGridSpec(nu...]
  transfers between devices with their start and end apart: 5 -> 5, of which waited for: 3 -> 3; matrix products, arithmetic and copies ran while one was open for 17% -> 17% of each run, Pallas kernels for 33% -> 34%
where the time goes in v15:
time: 136 us; the launch traced here: 135 us
  Pallas kernels  76.7 us (56%)
  local copies, waits for them, and re-layouts  22 us (16%)
  starting transfers between devices  11.8 us (9%)
  waiting for transfers between devices  11.4 us (8%)
  other arithmetic  7.46 us (5%)
  matrix products  5.28 us (4%)
    pallas_call x1, Pallas kernels, liquid_step(): pl.pallas_call(step_kernel, grid=(nz // zb,), in_specs=[pl.BlockSpec(memo...  45.2 us
    pallas_call x1, Pallas kernels, illiquid_pick(): pl.pallas_call(illiquid_kernel, grid_spec=pltpu.PrefetchScalarGridSpec(nu...  31.5 us
    ppermute x3, waiting for transfers between devices, all_sum(): x = x + lax.ppermute(x, axis, [(i, i ^ step) for i in range(count)])  11.3 us
    reshape x1, local copies, waits for them, and re-layouts, body(): jnp.transpose(liquid_part, (3, 2, 0, 1))  9.3 us
    ppermute x3, starting transfers between devices, all_sum(): x = x + lax.ppermute(x, axis, [(i, i ^ step) for i in range(count)])  5.52 us
    ppermute x1, starting transfers between devices, edges(): lax.ppermute(tail, axis, [(i, (i + 1) % count) for i in range(ends)])  4.95 us
    dot_general x1, matrix products, body(): jnp.dot(pick_z, jnp.tile(folded, (1, columns)), precision=lax.Precision.H...  4.47 us
    slice x1, local copies, waits for them, and re-layouts, body(): head = values_in[:, :, 0, :].astype(jnp.float32)  3.06 us
  transfers between devices with their start and end apart: 5, of which 3 were waited for; matrix products, arithmetic and copies ran while one was open for 17% of the time, Pallas kernels for 34%

profile of v15, /device:TPU:0, one launch (start us, length us, event | category | flops | bytes accessed | tf_op | source)
XLA Modules:
  0.0 134.8 jit_solution(9171781243782600728)
XLA Ops:
  0.0 3.1 %fusion.7 = (bf16[8,32,1,512]{3,2,1,0:T(2,128)(2,1)S(1)}, bf16[8,32,1,512]{3,2,1,0:T(2,128)(2,1)S(1)}) fusion(bf16[8,32,64,512]{3,2,1,0:T(8,128)(2,1)} %vals_ref.1), kind=kLoop, calls=%fused_computation.39 | loop fusion | bytes 1048576 | tf_op jit(solution)/shard_map/slice | solution.py:210
  3.1 0.9 fusion.6
  4.0 4.9 %collective-permute-start = (bf16[8,32,512]{2,1,0:T(8,128)(2,1)S(1)}, bf16[8,32,512]{2,1,0:T(8,128)(2,1)S(1)}, u32[]{:S(2)}, u32[]{:S(2)}) collective-permute-start(bf16[8,32,512]{2,1,0:T(8,128)(2,1)S(1)} %get-tuple-element.8), channel_id=1, source_target_pairs={{0,4},{4,8},{8,12},{1,5},{5,9},{9,13},{2,6},{6,10},{10,14},{3,7},{... | collective-permute-start | bytes 786440 | tf_op jit(solution)/shard_map/ppermute | solution.py:185
  8.9 1.3 fusion.9
  10.3 1.3 fusion.8
  11.6 0.7 convert_bitcast_fusion
  12.9 1.8 %convert_reduce_fusion = s32[1024]{0:T(1024)S(1)} fusion(s32[4096]{0:T(1024)S(1)} %add_bitcast_fusion, s32[1024]{0:T(1024)S(1)} %iota_add_fusion), kind=kLoop, calls=%fused_computation.1 | loop fusion | flops 12581888 | bytes 24576 | tf_op jit(solution)/shard_map/reduce_sum | solution.py:247
  15.1 4.5 %fusion.w_ref = f32[4096,256]{1,0:T(8,128)} fusion(f32[64,256]{0,1:T(8,128)S(1)} %bitcast.45, s32[4096]{0:T(1024)S(1)} %copy-done.3), kind=kOutput, calls=%fused_computation.3 | convolution fusion | flops 805568512 | bytes 4276224 | tf_op jit(solution)/shard_map/dot_general | solution.py:233
  20.9 1.3 collective-permute-start.1
  22.2 0.9 constant_dynamic-slice_fusion.1
  23.1 0.7 copy.48.ca_ref
  23.9 0.9 convert_element_type.21.lo_ref
  24.7 45.2 %shard_map.154 = f32[8,32,64,128]{3,2,1,0:T(8,128)} custom-call(f32[8]{0:T(128)} %load_ref.1, bf16[8,32,64,512]{3,2,1,0:T(8,128)(2,1)} %vals_ref.1, f32[8,32,512]{2,1,0:T(8,128)} %convert_element_type.21.lo_ref, f32[8,32,512]{2,1,0:T(8,128)} %get-tuple-element.7.up_ref, f32[32,64,512]{2,1,0:T(8,128)} %rl_ref.1, f32[32,64,512]{2,1,0:T(8,128)} %ri_ref.1, ...), custom_call_target="tpu_custom_call" | custom-call | tf_op jit(solution)/shard_map/pallas_call | solution.py:102
  70.0 9.3 %copy.49.t_ref = f32[128,64,256]{2,1,0:T(8,128)} copy(f32[128,64,256]{0,1,2:T(8,128)} %bitcast.43) | data formatting | bytes 16777216 | tf_op jit(solution)/shard_map/reshape | solution.py:227
  80.0 0.9 copy.50.rim_ref
  80.9 31.5 %shard_map.155 = f32[8,4096]{1,0:T(8,128)} custom-call(s32[4096]{0:T(1024)} %clamp_add_fusion.row_ref, bf16[256,192]{1,0:T(8,128)(2,1)} %copy.48.ca_ref, f32[128,64,256]{2,1,0:T(8,128)} %copy.49.t_ref, f32[128,2,256]{2,1,0:T(2,128)} %copy.50.rim_ref, f32[4096,256]{1,0:T(8,128)} %fusion.w_ref, bf16[8,256]{1,0:T(8,128)(2,1)} %fusion.5.group_ref), custom_call_target="tpu_custom_call" | custom-call | tf_op jit(solution)/shard_map/pallas_call | solution.py:159
  112.4 1.5 %collective-permute-done.2 = f32[8,4096]{1,0:T(8,128)S(1)} collective-permute-done((f32[8,4096]{1,0:T(8,128)}, f32[8,4096]{1,0:T(8,128)S(1)}, u32[]{:S(2)}, u32[]{:S(2)}) %collective-permute-start.2) | collective-permute-done | bytes 131104 | tf_op jit(solution)/shard_map/ppermute | solution.py:257
  113.9 0.9 add.61
  114.8 2.7 %collective-permute-start.3 = (f32[8,4096]{1,0:T(8,128)S(1)}, f32[8,4096]{1,0:T(8,128)S(1)}, u32[]{:S(2)}, u32[]{:S(2)}) collective-permute-start(f32[8,4096]{1,0:T(8,128)S(1)} %add.61), channel_id=1, source_target_pairs={{0,4},{4,0},{8,12},{12,8},{1,5},{5,1},{9,13},{13,9},{2,6},{6,2},{1... | collective-permute-start | bytes 393224 | tf_op jit(solution)/shard_map/ppermute | solution.py:257
  117.6 3.8 %collective-permute-done.3 = f32[8,4096]{1,0:T(8,128)S(1)} collective-permute-done((f32[8,4096]{1,0:T(8,128)S(1)}, f32[8,4096]{1,0:T(8,128)S(1)}, u32[]{:S(2)}, u32[]{:S(2)}) %collective-permute-start.3) | collective-permute-done | bytes 131104 | tf_op jit(solution)/shard_map/ppermute | solution.py:257
  121.4 2.8 %collective-permute-start.4 = (f32[8,4096]{1,0:T(8,128)S(1)}, f32[8,4096]{1,0:T(8,128)S(1)}, u32[]{:S(2)}, u32[]{:S(2)}) collective-permute-start(f32[8,4096]{1,0:T(8,128)S(1)} %add.62), channel_id=1, source_target_pairs={{0,8},{4,12},{8,0},{12,4},{1,9},{5,13},{9,1},{13,5},{2,10},{6,14},... | collective-permute-start | bytes 393224 | tf_op jit(solution)/shard_map/ppermute | solution.py:257
  124.2 6.0 %collective-permute-done.4 = f32[8,4096]{1,0:T(8,128)S(1)} collective-permute-done((f32[8,4096]{1,0:T(8,128)S(1)}, f32[8,4096]{1,0:T(8,128)S(1)}, u32[]{:S(2)}, u32[]{:S(2)}) %collective-permute-start.4) | collective-permute-done | bytes 131104 | tf_op jit(solution)/shard_map/ppermute | solution.py:257
  130.8 2.8 %gather_fusion = f32[1024,8]{1,0:T(8,128)S(1)} fusion(f32[8,4096]{0,1:T(8,128)S(1)} %copy.51, s32[1024]{0:T(1024)S(1)} %broadcast_clamp_fusion), kind=kCustom, calls=%fused_computation | custom fusion | bytes 69632 | tf_op jit(solution)/shard_map/jit(_take)/gather | solution.py:248
  134.0 0.8 copy.52
  (45 shorter events, 4.0 us)
Async XLA Ops:
  0.0 14.7 %copy-start = (f32[64,64]{1,0:T(8,128)S(1)}, f32[64,64]{1,0:T(8,128)}, u32[]{:S(2)}) copy-start(f32[64,64]{1,0:T(8,128)} %param.23) | copy-start | bytes 49156
  0.0 14.7 %copy-start.4 = (f32[64,64]{1,0:T(8,128)S(1)}, f32[64,64]{1,0:T(8,128)}, u32[]{:S(2)}) copy-start(f32[64,64]{1,0:T(8,128)} %constant.77.clone) | copy-start | bytes 49156
  0.0 15.0 %copy-start.3 = (s32[4096]{0:T(1024)S(1)}, s32[4096]{0:T(1024)}, u32[]{:S(2)}) copy-start(s32[4096]{0:T(1024)} %param.26) | copy-start | bytes 49156
  4.0 16.8 %collective-permute-start = (bf16[8,32,512]{2,1,0:T(8,128)(2,1)S(1)}, bf16[8,32,512]{2,1,0:T(8,128)(2,1)S(1)}, u32[]{:S(2)}, u32[]{:S(2)}) collective-permute-start(bf16[8,32,512]{2,1,0:T(8,128)(2,1)S(1)} %get-tuple-element.8), channel_id=1, source_target_pairs={{0,4},{4,8},{8,12},{1,5},{5,9},{9,13},{2,6},{6,10},{10,14},{3,7},{... | collective-permute-start | bytes 786440 | tf_op jit(solution)/shard_map/ppermute | solution.py:185
  10.3 9.3 %copy-start.5 = (s32[4096]{0:T(1024)S(1)}, s32[4096]{0:T(1024)}, u32[]{:S(2)}) copy-start(s32[4096]{0:T(1024)} %param.25) | copy-start | bytes 49156
  10.3 9.3 %copy-start.6 = (s32[4096]{0:T(1024)S(1)}, s32[4096]{0:T(1024)}, u32[]{:S(2)}) copy-start(s32[4096]{0:T(1024)} %param.24) | copy-start | bytes 49156
  20.9 58.4 %collective-permute-start.1 = (bf16[8,32,512]{2,1,0:T(8,128)(2,1)S(1)}, bf16[8,32,512]{2,1,0:T(8,128)(2,1)S(1)}, u32[]{:S(2)}, u32[]{:S(2)}) collective-permute-start(bf16[8,32,512]{2,1,0:T(8,128)(2,1)S(1)} %get-tuple-element.6), channel_id=1, source_target_pairs={{4,0},{8,4},{12,8},{5,1},{9,5},{13,9},{6,2},{10,6},{14,10},{7,3},{... | collective-permute-start | bytes 786440 | tf_op jit(solution)/shard_map/ppermute | solution.py:186
  70.0 9.4 %copy-start.2 = (f32[128,512,1,1]{1,0,3,2:T(8,128)S(1)}, f32[128,512,1,1]{1,0,3,2:T(8,128)}, u32[]{:S(2)}) copy-start(f32[128,512,1,1]{1,0,3,2:T(8,128)} %constant.78) | copy-start | bytes 786436
  80.9 53.9 %copy-start.1 = (f32[64,64]{1,0:T(8,128)S(1)}, f32[64,64]{1,0:T(8,128)}, u32[]{:S(2)}) copy-start(f32[64,64]{1,0:T(8,128)} %param.23) | copy-start | bytes 49156
  112.4 1.6 %collective-permute-start.2 = (f32[8,4096]{1,0:T(8,128)}, f32[8,4096]{1,0:T(8,128)S(1)}, u32[]{:S(2)}, u32[]{:S(2)}) collective-permute-start(f32[8,4096]{1,0:T(8,128)} %shard_map.155), channel_id=1, source_target_pairs={{0,1},{1,0},{2,3},{3,2},{4,5},{5,4},{6,7},{7,6},{8,9},{9,8},{10,11... | collective-permute-start | bytes 393224 | tf_op jit(solution)/shard_map/ppermute | solution.py:257
  114.8 6.5 %collective-permute-start.3 = (f32[8,4096]{1,0:T(8,128)S(1)}, f32[8,4096]{1,0:T(8,128)S(1)}, u32[]{:S(2)}, u32[]{:S(2)}) collective-permute-start(f32[8,4096]{1,0:T(8,128)S(1)} %add.61), channel_id=1, source_target_pairs={{0,4},{4,0},{8,12},{12,8},{1,5},{5,1},{9,13},{13,9},{2,6},{6,2},{1... | collective-permute-start | bytes 393224 | tf_op jit(solution)/shard_map/ppermute | solution.py:257
  121.4 8.8 %collective-permute-start.4 = (f32[8,4096]{1,0:T(8,128)S(1)}, f32[8,4096]{1,0:T(8,128)S(1)}, u32[]{:S(2)}, u32[]{:S(2)}) collective-permute-start(f32[8,4096]{1,0:T(8,128)S(1)} %add.62), channel_id=1, source_target_pairs={{0,8},{4,12},{8,0},{12,4},{1,9},{5,13},{9,1},{13,5},{2,10},{6,14},... | collective-permute-start | bytes 393224 | tf_op jit(solution)/shard_map/ppermute | solution.py:257

commit v16 on v15

--- a/solution.py
+++ b/solution.py
@@ -68,12 +68,14 @@
     top = arow == na - 1
     bottom = arow == 0
     th, tl = split_bf16(tb_ref[...])
-    both = jnp.concatenate([th, tl], axis=1)
+    both = jnp.concatenate(
+        [jnp.concatenate([th, tl], axis=1), jnp.concatenate([th, jnp.zeros_like(tl)], axis=1)], axis=0
+    )
 
     def transform(x):
         hi, low = split_bf16(x)
-        pair = jnp.dot(hi, both, preferred_element_type=jnp.float32)
-        return jnp.dot(low, th, preferred_element_type=jnp.float32) + pair[:, kb:] + pair[:, :kb]
+        pair = jnp.dot(jnp.concatenate([hi, low], axis=1), both, preferred_element_type=jnp.float32)
+        return pair[:, kb:] + pair[:, :kb]
 
     price = transform(pf)
 

time: 136 us -> 136 us (level)
  no operation moved by 1% of the time
where the time goes in v16:
time: 136 us; the launch traced here: 135 us
  Pallas kernels  76.8 us (56%)
  local copies, waits for them, and re-layouts  22 us (16%)
  starting transfers between devices  11.8 us (9%)
  waiting for transfers between devices  11.4 us (8%)
  other arithmetic  7.46 us (5%)
  matrix products  5.28 us (4%)
    pallas_call x1, Pallas kernels, liquid_step(): pl.pallas_call(step_kernel, grid=(nz // zb,), in_specs=[pl.BlockSpec(memo...  45.4 us
    pallas_call x1, Pallas kernels, illiquid_pick(): pl.pallas_call(illiquid_kernel, grid_spec=pltpu.PrefetchScalarGridSpec(nu...  31.5 us
    ppermute x3, waiting for transfers between devices, all_sum(): x = x + lax.ppermute(x, axis, [(i, i ^ step) for i in range(count)])  11.3 us
    reshape x1, local copies, waits for them, and re-layouts, body(): jnp.transpose(liquid_part, (3, 2, 0, 1))  9.3 us
    ppermute x3, starting transfers between devices, all_sum(): x = x + lax.ppermute(x, axis, [(i, i ^ step) for i in range(count)])  5.52 us
    ppermute x1, starting transfers between devices, edges(): lax.ppermute(tail, axis, [(i, (i + 1) % count) for i in range(ends)])  4.95 us
    dot_general x1, matrix products, body(): jnp.dot(pick_z, jnp.tile(folded, (1, columns)), precision=lax.Precision.H...  4.47 us
    slice x1, local copies, waits for them, and re-layouts, body(): head = values_in[:, :, 0, :].astype(jnp.float32)  3.06 us
  transfers between devices with their start and end apart: 5, of which 3 were waited for; matrix products, arithmetic and copies ran while one was open for 17% of the time, Pallas kernels for 34%

profile of v16, /device:TPU:0, one launch (start us, length us, event | category | flops | bytes accessed | tf_op | source)
XLA Modules:
  0.0 134.9 jit_solution(4106078795476553556)
XLA Ops:
  0.0 3.1 %fusion.7 = (bf16[8,32,1,512]{3,2,1,0:T(2,128)(2,1)S(1)}, bf16[8,32,1,512]{3,2,1,0:T(2,128)(2,1)S(1)}) fusion(bf16[8,32,64,512]{3,2,1,0:T(8,128)(2,1)} %vals_ref.1), kind=kLoop, calls=%fused_computation.39 | loop fusion | bytes 1048576 | tf_op jit(solution)/shard_map/slice | solution.py:212
  3.1 0.9 fusion.6
  4.0 4.9 %collective-permute-start = (bf16[8,32,512]{2,1,0:T(8,128)(2,1)S(1)}, bf16[8,32,512]{2,1,0:T(8,128)(2,1)S(1)}, u32[]{:S(2)}, u32[]{:S(2)}) collective-permute-start(bf16[8,32,512]{2,1,0:T(8,128)(2,1)S(1)} %get-tuple-element.8), channel_id=1, source_target_pairs={{0,4},{4,8},{8,12},{1,5},{5,9},{9,13},{2,6},{6,10},{10,14},{3,7},{... | collective-permute-start | bytes 786440 | tf_op jit(solution)/shard_map/ppermute | solution.py:187
  8.9 1.3 fusion.9
  10.3 1.3 fusion.8
  11.6 0.7 convert_bitcast_fusion
  12.9 1.8 %convert_reduce_fusion = s32[1024]{0:T(1024)S(1)} fusion(s32[4096]{0:T(1024)S(1)} %add_bitcast_fusion, s32[1024]{0:T(1024)S(1)} %iota_add_fusion), kind=kLoop, calls=%fused_computation.1 | loop fusion | flops 12581888 | bytes 24576 | tf_op jit(solution)/shard_map/reduce_sum | solution.py:249
  15.1 4.5 %fusion.w_ref = f32[4096,256]{1,0:T(8,128)} fusion(f32[64,256]{0,1:T(8,128)S(1)} %bitcast.45, s32[4096]{0:T(1024)S(1)} %copy-done.3), kind=kOutput, calls=%fused_computation.3 | convolution fusion | flops 805568512 | bytes 4276224 | tf_op jit(solution)/shard_map/dot_general | solution.py:235
  20.9 1.3 collective-permute-start.1
  22.2 0.9 constant_dynamic-slice_fusion.1
  23.1 0.7 copy.48.ca_ref
  23.9 0.9 convert_element_type.21.lo_ref
  24.7 45.4 %shard_map.154 = f32[8,32,64,128]{3,2,1,0:T(8,128)} custom-call(f32[8]{0:T(128)} %load_ref.1, bf16[8,32,64,512]{3,2,1,0:T(8,128)(2,1)} %vals_ref.1, f32[8,32,512]{2,1,0:T(8,128)} %convert_element_type.21.lo_ref, f32[8,32,512]{2,1,0:T(8,128)} %get-tuple-element.7.up_ref, f32[32,64,512]{2,1,0:T(8,128)} %rl_ref.1, f32[32,64,512]{2,1,0:T(8,128)} %ri_ref.1, ...), custom_call_target="tpu_custom_call" | custom-call | tf_op jit(solution)/shard_map/pallas_call | solution.py:104
  70.1 9.3 %copy.49.t_ref = f32[128,64,256]{2,1,0:T(8,128)} copy(f32[128,64,256]{0,1,2:T(8,128)} %bitcast.43) | data formatting | bytes 16777216 | tf_op jit(solution)/shard_map/reshape | solution.py:229
  80.2 0.9 copy.50.rim_ref
  81.0 31.5 %shard_map.155 = f32[8,4096]{1,0:T(8,128)} custom-call(s32[4096]{0:T(1024)} %clamp_add_fusion.row_ref, bf16[256,192]{1,0:T(8,128)(2,1)} %copy.48.ca_ref, f32[128,64,256]{2,1,0:T(8,128)} %copy.49.t_ref, f32[128,2,256]{2,1,0:T(2,128)} %copy.50.rim_ref, f32[4096,256]{1,0:T(8,128)} %fusion.w_ref, bf16[8,256]{1,0:T(8,128)(2,1)} %fusion.5.group_ref), custom_call_target="tpu_custom_call" | custom-call | tf_op jit(solution)/shard_map/pallas_call | solution.py:161
  112.5 1.5 %collective-permute-done.2 = f32[8,4096]{1,0:T(8,128)S(1)} collective-permute-done((f32[8,4096]{1,0:T(8,128)}, f32[8,4096]{1,0:T(8,128)S(1)}, u32[]{:S(2)}, u32[]{:S(2)}) %collective-permute-start.2) | collective-permute-done | bytes 131104 | tf_op jit(solution)/shard_map/ppermute | solution.py:259
  114.1 0.9 add.61
  115.0 2.7 %collective-permute-start.3 = (f32[8,4096]{1,0:T(8,128)S(1)}, f32[8,4096]{1,0:T(8,128)S(1)}, u32[]{:S(2)}, u32[]{:S(2)}) collective-permute-start(f32[8,4096]{1,0:T(8,128)S(1)} %add.61), channel_id=1, source_target_pairs={{0,4},{4,0},{8,12},{12,8},{1,5},{5,1},{9,13},{13,9},{2,6},{6,2},{1... | collective-permute-start | bytes 393224 | tf_op jit(solution)/shard_map/ppermute | solution.py:259
  117.7 3.8 %collective-permute-done.3 = f32[8,4096]{1,0:T(8,128)S(1)} collective-permute-done((f32[8,4096]{1,0:T(8,128)S(1)}, f32[8,4096]{1,0:T(8,128)S(1)}, u32[]{:S(2)}, u32[]{:S(2)}) %collective-permute-start.3) | collective-permute-done | bytes 131104 | tf_op jit(solution)/shard_map/ppermute | solution.py:259
  121.5 2.8 %collective-permute-start.4 = (f32[8,4096]{1,0:T(8,128)S(1)}, f32[8,4096]{1,0:T(8,128)S(1)}, u32[]{:S(2)}, u32[]{:S(2)}) collective-permute-start(f32[8,4096]{1,0:T(8,128)S(1)} %add.62), channel_id=1, source_target_pairs={{0,8},{4,12},{8,0},{12,4},{1,9},{5,13},{9,1},{13,5},{2,10},{6,14},... | collective-permute-start | bytes 393224 | tf_op jit(solution)/shard_map/ppermute | solution.py:259
  124.4 6.0 %collective-permute-done.4 = f32[8,4096]{1,0:T(8,128)S(1)} collective-permute-done((f32[8,4096]{1,0:T(8,128)S(1)}, f32[8,4096]{1,0:T(8,128)S(1)}, u32[]{:S(2)}, u32[]{:S(2)}) %collective-permute-start.4) | collective-permute-done | bytes 131104 | tf_op jit(solution)/shard_map/ppermute | solution.py:259
  131.0 2.8 %gather_fusion = f32[1024,8]{1,0:T(8,128)S(1)} fusion(f32[8,4096]{0,1:T(8,128)S(1)} %copy.51, s32[1024]{0:T(1024)S(1)} %broadcast_clamp_fusion), kind=kCustom, calls=%fused_computation | custom fusion | bytes 69632 | tf_op jit(solution)/shard_map/jit(_take)/gather | solution.py:250
  134.1 0.8 copy.52
  (45 shorter events, 4.0 us)
Async XLA Ops:
  0.0 14.7 %copy-start = (f32[64,64]{1,0:T(8,128)S(1)}, f32[64,64]{1,0:T(8,128)}, u32[]{:S(2)}) copy-start(f32[64,64]{1,0:T(8,128)} %param.23) | copy-start | bytes 49156
  0.0 14.7 %copy-start.4 = (f32[64,64]{1,0:T(8,128)S(1)}, f32[64,64]{1,0:T(8,128)}, u32[]{:S(2)}) copy-start(f32[64,64]{1,0:T(8,128)} %constant.77.clone) | copy-start | bytes 49156
  0.0 15.0 %copy-start.3 = (s32[4096]{0:T(1024)S(1)}, s32[4096]{0:T(1024)}, u32[]{:S(2)}) copy-start(s32[4096]{0:T(1024)} %param.26) | copy-start | bytes 49156
  4.0 16.8 %collective-permute-start = (bf16[8,32,512]{2,1,0:T(8,128)(2,1)S(1)}, bf16[8,32,512]{2,1,0:T(8,128)(2,1)S(1)}, u32[]{:S(2)}, u32[]{:S(2)}) collective-permute-start(bf16[8,32,512]{2,1,0:T(8,128)(2,1)S(1)} %get-tuple-element.8), channel_id=1, source_target_pairs={{0,4},{4,8},{8,12},{1,5},{5,9},{9,13},{2,6},{6,10},{10,14},{3,7},{... | collective-permute-start | bytes 786440 | tf_op jit(solution)/shard_map/ppermute | solution.py:187
  10.3 9.3 %copy-start.5 = (s32[4096]{0:T(1024)S(1)}, s32[4096]{0:T(1024)}, u32[]{:S(2)}) copy-start(s32[4096]{0:T(1024)} %param.25) | copy-start | bytes 49156
  10.3 9.3 %copy-start.6 = (s32[4096]{0:T(1024)S(1)}, s32[4096]{0:T(1024)}, u32[]{:S(2)}) copy-start(s32[4096]{0:T(1024)} %param.24) | copy-start | bytes 49156
  20.9 58.5 %collective-permute-start.1 = (bf16[8,32,512]{2,1,0:T(8,128)(2,1)S(1)}, bf16[8,32,512]{2,1,0:T(8,128)(2,1)S(1)}, u32[]{:S(2)}, u32[]{:S(2)}) collective-permute-start(bf16[8,32,512]{2,1,0:T(8,128)(2,1)S(1)} %get-tuple-element.6), channel_id=1, source_target_pairs={{4,0},{8,4},{12,8},{5,1},{9,5},{13,9},{6,2},{10,6},{14,10},{7,3},{... | collective-permute-start | bytes 786440 | tf_op jit(solution)/shard_map/ppermute | solution.py:188
  70.1 9.4 %copy-start.2 = (f32[128,512,1,1]{1,0,3,2:T(8,128)S(1)}, f32[128,512,1,1]{1,0,3,2:T(8,128)}, u32[]{:S(2)}) copy-start(f32[128,512,1,1]{1,0,3,2:T(8,128)} %constant.78) | copy-start | bytes 786436
  81.0 53.9 %copy-start.1 = (f32[64,64]{1,0:T(8,128)S(1)}, f32[64,64]{1,0:T(8,128)}, u32[]{:S(2)}) copy-start(f32[64,64]{1,0:T(8,128)} %param.23) | copy-start | bytes 49156
  112.5 1.6 %collective-permute-start.2 = (f32[8,4096]{1,0:T(8,128)}, f32[8,4096]{1,0:T(8,128)S(1)}, u32[]{:S(2)}, u32[]{:S(2)}) collective-permute-start(f32[8,4096]{1,0:T(8,128)} %shard_map.155), channel_id=1, source_target_pairs={{0,1},{1,0},{2,3},{3,2},{4,5},{5,4},{6,7},{7,6},{8,9},{9,8},{10,11... | collective-permute-start | bytes 393224 | tf_op jit(solution)/shard_map/ppermute | solution.py:259
  115.0 6.5 %collective-permute-start.3 = (f32[8,4096]{1,0:T(8,128)S(1)}, f32[8,4096]{1,0:T(8,128)S(1)}, u32[]{:S(2)}, u32[]{:S(2)}) collective-permute-start(f32[8,4096]{1,0:T(8,128)S(1)} %add.61), channel_id=1, source_target_pairs={{0,4},{4,0},{8,12},{12,8},{1,5},{5,1},{9,13},{13,9},{2,6},{6,2},{1... | collective-permute-start | bytes 393224 | tf_op jit(solution)/shard_map/ppermute | solution.py:259
  121.5 8.8 %collective-permute-start.4 = (f32[8,4096]{1,0:T(8,128)S(1)}, f32[8,4096]{1,0:T(8,128)S(1)}, u32[]{:S(2)}, u32[]{:S(2)}) collective-permute-start(f32[8,4096]{1,0:T(8,128)S(1)} %add.62), channel_id=1, source_target_pairs={{0,8},{4,12},{8,0},{12,4},{1,9},{5,13},{9,1},{13,5},{2,10},{6,14},... | collective-permute-start | bytes 393224 | tf_op jit(solution)/shard_map/ppermute | solution.py:259

commit v17 on v15

--- a/solution.py
+++ b/solution.py
@@ -155,7 +155,7 @@
     kb, na_loc, lanes = t.shape
     na, depth = ca.shape
     count = row_index.shape[0]
-    block = 8
+    block = 16
     return pl.pallas_call(
         illiquid_kernel,
         grid_spec=pltpu.PrefetchScalarGridSpec(

time: 136 us -> 132 us (0.971)
  Pallas kernels: 76.7 us -> 72.9 us
    pallas_call x1, Pallas kernels: 31.5 us -> 27.7 us  [illiquid_pick(): pl.pallas_call(illiquid_kernel, grid_spec=pltpu.PrefetchScalarGridSpec(nu...]
  transfers between devices with their start and end apart: 5 -> 5, of which waited for: 3 -> 3; matrix products, arithmetic and copies ran while one was open for 17% -> 18% of each run, Pallas kernels for 34% -> 34%
where the time goes in v17:
time: 132 us; the launch traced here: 131 us
  Pallas kernels  72.9 us (55%)
  local copies, waits for them, and re-layouts  22 us (17%)
  starting transfers between devices  11.9 us (9%)
  waiting for transfers between devices  11.4 us (9%)
  other arithmetic  7.46 us (6%)
  matrix products  5.29 us (4%)
    pallas_call x1, Pallas kernels, liquid_step(): pl.pallas_call(step_kernel, grid=(nz // zb,), in_specs=[pl.BlockSpec(memo...  45.2 us
    pallas_call x1, Pallas kernels, illiquid_pick(): pl.pallas_call(illiquid_kernel, grid_spec=pltpu.PrefetchScalarGridSpec(nu...  27.7 us
    ppermute x3, waiting for transfers between devices, all_sum(): x = x + lax.ppermute(x, axis, [(i, i ^ step) for i in range(count)])  11.4 us
    reshape x1, local copies, waits for them, and re-layouts, body(): jnp.transpose(liquid_part, (3, 2, 0, 1))  9.3 us
    ppermute x3, starting transfers between devices, all_sum(): x = x + lax.ppermute(x, axis, [(i, i ^ step) for i in range(count)])  5.51 us
    ppermute x1, starting transfers between devices, edges(): lax.ppermute(tail, axis, [(i, (i + 1) % count) for i in range(ends)])  4.95 us
    dot_general x1, matrix products, body(): jnp.dot(pick_z, jnp.tile(folded, (1, columns)), precision=lax.Precision.H...  4.47 us
    slice x1, local copies, waits for them, and re-layouts, body(): head = values_in[:, :, 0, :].astype(jnp.float32)  3.06 us
  transfers between devices with their start and end apart: 5, of which 3 were waited for; matrix products, arithmetic and copies ran while one was open for 18% of the time, Pallas kernels for 34%

profile of v17, /device:TPU:0, one launch (start us, length us, event | category | flops | bytes accessed | tf_op | source)
XLA Modules:
  0.0 131.2 jit_solution(10748261623365138873)
XLA Ops:
  0.0 3.1 %fusion.7 = (bf16[8,32,1,512]{3,2,1,0:T(2,128)(2,1)S(1)}, bf16[8,32,1,512]{3,2,1,0:T(2,128)(2,1)S(1)}) fusion(bf16[8,32,64,512]{3,2,1,0:T(8,128)(2,1)} %vals_ref.1), kind=kLoop, calls=%fused_computation.39 | loop fusion | bytes 1048576 | tf_op jit(solution)/shard_map/slice | solution.py:210
  3.1 0.9 fusion.6
  4.0 4.9 %collective-permute-start = (bf16[8,32,512]{2,1,0:T(8,128)(2,1)S(1)}, bf16[8,32,512]{2,1,0:T(8,128)(2,1)S(1)}, u32[]{:S(2)}, u32[]{:S(2)}) collective-permute-start(bf16[8,32,512]{2,1,0:T(8,128)(2,1)S(1)} %get-tuple-element.8), channel_id=1, source_target_pairs={{0,4},{4,8},{8,12},{1,5},{5,9},{9,13},{2,6},{6,10},{10,14},{3,7},{... | collective-permute-start | bytes 786440 | tf_op jit(solution)/shard_map/ppermute | solution.py:185
  8.9 1.3 %fusion.9 = (f32[32,1,512]{2,1,0:T(1,128)S(1)}, f32[32,1,512]{2,1,0:T(1,128)S(1)}) fusion(f32[32,64,512]{2,1,0:T(8,128)} %ri_ref.1), kind=kLoop, calls=%fused_computation.41 | loop fusion | bytes 262144 | tf_op jit(solution)/shard_map/slice | solution.py:221
  10.3 1.3 %fusion.8 = (s32[32,1,512]{2,1,0:T(1,128)S(1)}, s32[32,1,512]{2,1,0:T(1,128)S(1)}) fusion(s32[32,64,512]{2,1,0:T(8,128)} %mi_ref.1), kind=kLoop, calls=%fused_computation.40 | loop fusion | bytes 262144 | tf_op jit(solution)/shard_map/slice | solution.py:221
  11.6 0.7 convert_bitcast_fusion
  12.9 1.8 %convert_reduce_fusion = s32[1024]{0:T(1024)S(1)} fusion(s32[4096]{0:T(1024)S(1)} %add_bitcast_fusion, s32[1024]{0:T(1024)S(1)} %iota_add_fusion), kind=kLoop, calls=%fused_computation.1 | loop fusion | flops 12581888 | bytes 24576 | tf_op jit(solution)/shard_map/reduce_sum | solution.py:247
  15.1 4.5 %fusion.w_ref = f32[4096,256]{1,0:T(8,128)} fusion(f32[64,256]{0,1:T(8,128)S(1)} %bitcast.45, s32[4096]{0:T(1024)S(1)} %copy-done.3), kind=kOutput, calls=%fused_computation.3 | convolution fusion | flops 805568512 | bytes 4276224 | tf_op jit(solution)/shard_map/dot_general | solution.py:233
  20.9 1.5 %collective-permute-start.1 = (bf16[8,32,512]{2,1,0:T(8,128)(2,1)S(1)}, bf16[8,32,512]{2,1,0:T(8,128)(2,1)S(1)}, u32[]{:S(2)}, u32[]{:S(2)}) collective-permute-start(bf16[8,32,512]{2,1,0:T(8,128)(2,1)S(1)} %get-tuple-element.6), channel_id=1, source_target_pairs={{4,0},{8,4},{12,8},{5,1},{9,5},{13,9},{6,2},{10,6},{14,10},{7,3},{... | collective-permute-start | bytes 786440 | tf_op jit(solution)/shard_map/ppermute | solution.py:186
  22.4 0.9 constant_dynamic-slice_fusion.1
  23.3 0.7 copy.48.ca_ref
  24.1 0.9 convert_element_type.21.lo_ref
  24.9 45.2 %shard_map.154 = f32[8,32,64,128]{3,2,1,0:T(8,128)} custom-call(f32[8]{0:T(128)} %load_ref.1, bf16[8,32,64,512]{3,2,1,0:T(8,128)(2,1)} %vals_ref.1, f32[8,32,512]{2,1,0:T(8,128)} %convert_element_type.21.lo_ref, f32[8,32,512]{2,1,0:T(8,128)} %get-tuple-element.7.up_ref, f32[32,64,512]{2,1,0:T(8,128)} %rl_ref.1, f32[32,64,512]{2,1,0:T(8,128)} %ri_ref.1, ...), custom_call_target="tpu_custom_call" | custom-call | tf_op jit(solution)/shard_map/pallas_call | solution.py:102
  70.2 9.3 %copy.49.t_ref = f32[128,64,256]{2,1,0:T(8,128)} copy(f32[128,64,256]{0,1,2:T(8,128)} %bitcast.43) | data formatting | bytes 16777216 | tf_op jit(solution)/shard_map/reshape | solution.py:227
  80.2 0.9 copy.50.rim_ref
  81.1 27.7 %shard_map.155 = f32[8,4096]{1,0:T(8,128)} custom-call(s32[4096]{0:T(1024)} %clamp_add_fusion.row_ref, bf16[256,192]{1,0:T(8,128)(2,1)} %copy.48.ca_ref, f32[128,64,256]{2,1,0:T(8,128)} %copy.49.t_ref, f32[128,2,256]{2,1,0:T(2,128)} %copy.50.rim_ref, f32[4096,256]{1,0:T(8,128)} %fusion.w_ref, bf16[8,256]{1,0:T(8,128)(2,1)} %fusion.5.group_ref), custom_call_target="tpu_custom_call" | custom-call | tf_op jit(solution)/shard_map/pallas_call | solution.py:159
  108.8 1.5 %collective-permute-done.2 = f32[8,4096]{1,0:T(8,128)S(1)} collective-permute-done((f32[8,4096]{1,0:T(8,128)}, f32[8,4096]{1,0:T(8,128)S(1)}, u32[]{:S(2)}, u32[]{:S(2)}) %collective-permute-start.2) | collective-permute-done | bytes 131104 | tf_op jit(solution)/shard_map/ppermute | solution.py:257
  110.3 0.9 add.61
  111.2 2.7 %collective-permute-start.3 = (f32[8,4096]{1,0:T(8,128)S(1)}, f32[8,4096]{1,0:T(8,128)S(1)}, u32[]{:S(2)}, u32[]{:S(2)}) collective-permute-start(f32[8,4096]{1,0:T(8,128)S(1)} %add.61), channel_id=1, source_target_pairs={{0,4},{4,0},{8,12},{12,8},{1,5},{5,1},{9,13},{13,9},{2,6},{6,2},{1... | collective-permute-start | bytes 393224 | tf_op jit(solution)/shard_map/ppermute | solution.py:257
  113.9 3.8 %collective-permute-done.3 = f32[8,4096]{1,0:T(8,128)S(1)} collective-permute-done((f32[8,4096]{1,0:T(8,128)S(1)}, f32[8,4096]{1,0:T(8,128)S(1)}, u32[]{:S(2)}, u32[]{:S(2)}) %collective-permute-start.3) | collective-permute-done | bytes 131104 | tf_op jit(solution)/shard_map/ppermute | solution.py:257
  117.8 2.8 %collective-permute-start.4 = (f32[8,4096]{1,0:T(8,128)S(1)}, f32[8,4096]{1,0:T(8,128)S(1)}, u32[]{:S(2)}, u32[]{:S(2)}) collective-permute-start(f32[8,4096]{1,0:T(8,128)S(1)} %add.62), channel_id=1, source_target_pairs={{0,8},{4,12},{8,0},{12,4},{1,9},{5,13},{9,1},{13,5},{2,10},{6,14},... | collective-permute-start | bytes 393224 | tf_op jit(solution)/shard_map/ppermute | solution.py:257
  120.6 6.0 %collective-permute-done.4 = f32[8,4096]{1,0:T(8,128)S(1)} collective-permute-done((f32[8,4096]{1,0:T(8,128)S(1)}, f32[8,4096]{1,0:T(8,128)S(1)}, u32[]{:S(2)}, u32[]{:S(2)}) %collective-permute-start.4) | collective-permute-done | bytes 131104 | tf_op jit(solution)/shard_map/ppermute | solution.py:257
  127.2 2.8 %gather_fusion = f32[1024,8]{1,0:T(8,128)S(1)} fusion(f32[8,4096]{0,1:T(8,128)S(1)} %copy.51, s32[1024]{0:T(1024)S(1)} %broadcast_clamp_fusion), kind=kCustom, calls=%fused_computation | custom fusion | bytes 69632 | tf_op jit(solution)/shard_map/jit(_take)/gather | solution.py:248
  130.4 0.8 copy.52
  (45 shorter events, 4.0 us)
Async XLA Ops:
  0.0 14.7 %copy-start = (f32[64,64]{1,0:T(8,128)S(1)}, f32[64,64]{1,0:T(8,128)}, u32[]{:S(2)}) copy-start(f32[64,64]{1,0:T(8,128)} %param.23) | copy-start | bytes 49156
  0.0 14.7 %copy-start.4 = (f32[64,64]{1,0:T(8,128)S(1)}, f32[64,64]{1,0:T(8,128)}, u32[]{:S(2)}) copy-start(f32[64,64]{1,0:T(8,128)} %constant.77.clone) | copy-start | bytes 49156
  0.0 15.0 %copy-start.3 = (s32[4096]{0:T(1024)S(1)}, s32[4096]{0:T(1024)}, u32[]{:S(2)}) copy-start(s32[4096]{0:T(1024)} %param.26) | copy-start | bytes 49156
  4.0 16.8 %collective-permute-start = (bf16[8,32,512]{2,1,0:T(8,128)(2,1)S(1)}, bf16[8,32,512]{2,1,0:T(8,128)(2,1)S(1)}, u32[]{:S(2)}, u32[]{:S(2)}) collective-permute-start(bf16[8,32,512]{2,1,0:T(8,128)(2,1)S(1)} %get-tuple-element.8), channel_id=1, source_target_pairs={{0,4},{4,8},{8,12},{1,5},{5,9},{9,13},{2,6},{6,10},{10,14},{3,7},{... | collective-permute-start | bytes 786440 | tf_op jit(solution)/shard_map/ppermute | solution.py:185
  10.3 9.3 %copy-start.5 = (s32[4096]{0:T(1024)S(1)}, s32[4096]{0:T(1024)}, u32[]{:S(2)}) copy-start(s32[4096]{0:T(1024)} %param.25) | copy-start | bytes 49156
  10.3 9.3 %copy-start.6 = (s32[4096]{0:T(1024)S(1)}, s32[4096]{0:T(1024)}, u32[]{:S(2)}) copy-start(s32[4096]{0:T(1024)} %param.24) | copy-start | bytes 49156
  20.9 58.6 %collective-permute-start.1 = (bf16[8,32,512]{2,1,0:T(8,128)(2,1)S(1)}, bf16[8,32,512]{2,1,0:T(8,128)(2,1)S(1)}, u32[]{:S(2)}, u32[]{:S(2)}) collective-permute-start(bf16[8,32,512]{2,1,0:T(8,128)(2,1)S(1)} %get-tuple-element.6), channel_id=1, source_target_pairs={{4,0},{8,4},{12,8},{5,1},{9,5},{13,9},{6,2},{10,6},{14,10},{7,3},{... | collective-permute-start | bytes 786440 | tf_op jit(solution)/shard_map/ppermute | solution.py:186
  70.2 9.4 %copy-start.2 = (f32[128,512,1,1]{1,0,3,2:T(8,128)S(1)}, f32[128,512,1,1]{1,0,3,2:T(8,128)}, u32[]{:S(2)}) copy-start(f32[128,512,1,1]{1,0,3,2:T(8,128)} %constant.78) | copy-start | bytes 786436
  81.1 50.1 %copy-start.1 = (f32[64,64]{1,0:T(8,128)S(1)}, f32[64,64]{1,0:T(8,128)}, u32[]{:S(2)}) copy-start(f32[64,64]{1,0:T(8,128)} %param.23) | copy-start | bytes 49156
  108.7 1.6 %collective-permute-start.2 = (f32[8,4096]{1,0:T(8,128)}, f32[8,4096]{1,0:T(8,128)S(1)}, u32[]{:S(2)}, u32[]{:S(2)}) collective-permute-start(f32[8,4096]{1,0:T(8,128)} %shard_map.155), channel_id=1, source_target_pairs={{0,1},{1,0},{2,3},{3,2},{4,5},{5,4},{6,7},{7,6},{8,9},{9,8},{10,11... | collective-permute-start | bytes 393224 | tf_op jit(solution)/shard_map/ppermute | solution.py:257
  111.2 6.5 %collective-permute-start.3 = (f32[8,4096]{1,0:T(8,128)S(1)}, f32[8,4096]{1,0:T(8,128)S(1)}, u32[]{:S(2)}, u32[]{:S(2)}) collective-permute-start(f32[8,4096]{1,0:T(8,128)S(1)} %add.61), channel_id=1, source_target_pairs={{0,4},{4,0},{8,12},{12,8},{1,5},{5,1},{9,13},{13,9},{2,6},{6,2},{1... | collective-permute-start | bytes 393224 | tf_op jit(solution)/shard_map/ppermute | solution.py:257
  117.8 8.8 %collective-permute-start.4 = (f32[8,4096]{1,0:T(8,128)S(1)}, f32[8,4096]{1,0:T(8,128)S(1)}, u32[]{:S(2)}, u32[]{:S(2)}) collective-permute-start(f32[8,4096]{1,0:T(8,128)S(1)} %add.62), channel_id=1, source_target_pairs={{0,8},{4,12},{8,0},{12,4},{1,9},{5,13},{9,1},{13,5},{2,10},{6,14},... | collective-permute-start | bytes 393224 | tf_op jit(solution)/shard_map/ppermute | solution.py:257

commit v18 on v17

--- a/solution.py
+++ b/solution.py
@@ -155,7 +155,7 @@
     kb, na_loc, lanes = t.shape
     na, depth = ca.shape
     count = row_index.shape[0]
-    block = 16
+    block = 32
     return pl.pallas_call(
         illiquid_kernel,
         grid_spec=pltpu.PrefetchScalarGridSpec(

time: 132 us -> 130 us (0.985)
  Pallas kernels: 72.9 us -> 71.2 us
    pallas_call x1, Pallas kernels: 27.7 us -> 26 us  [illiquid_pick(): pl.pallas_call(illiquid_kernel, grid_spec=pltpu.PrefetchScalarGridSpec(nu...]
  transfers between devices with their start and end apart: 5 -> 5, of which waited for: 3 -> 3; matrix products, arithmetic and copies ran while one was open for 18% -> 18% of each run, Pallas kernels for 34% -> 35%
where the time goes in v18:
time: 130 us
  Pallas kernels  71.2 us (55%)
  local copies, waits for them, and re-layouts  22 us (17%)
  starting transfers between devices  11.9 us (9%)
  waiting for transfers between devices  11.4 us (9%)
  other arithmetic  7.46 us (6%)
  matrix products  5.29 us (4%)
    pallas_call x1, Pallas kernels, liquid_step(): pl.pallas_call(step_kernel, grid=(nz // zb,), in_specs=[pl.BlockSpec(memo...  45.2 us
    pallas_call x1, Pallas kernels, illiquid_pick(): pl.pallas_call(illiquid_kernel, grid_spec=pltpu.PrefetchScalarGridSpec(nu...  26 us
    ppermute x3, waiting for transfers between devices, all_sum(): x = x + lax.ppermute(x, axis, [(i, i ^ step) for i in range(count)])  11.4 us
    reshape x1, local copies, waits for them, and re-layouts, body(): jnp.transpose(liquid_part, (3, 2, 0, 1))  9.3 us
    ppermute x3, starting transfers between devices, all_sum(): x = x + lax.ppermute(x, axis, [(i, i ^ step) for i in range(count)])  5.52 us
    ppermute x1, starting transfers between devices, edges(): lax.ppermute(tail, axis, [(i, (i + 1) % count) for i in range(ends)])  4.95 us
    dot_general x1, matrix products, body(): jnp.dot(pick_z, jnp.tile(folded, (1, columns)), precision=lax.Precision.H...  4.47 us
    slice x1, local copies, waits for them, and re-layouts, body(): head = values_in[:, :, 0, :].astype(jnp.float32)  3.06 us
  transfers between devices with their start and end apart: 5, of which 3 were waited for; matrix products, arithmetic and copies ran while one was open for 18% of the time, Pallas kernels for 35%

profile of v18, /device:TPU:0, one launch (start us, length us, event | category | flops | bytes accessed | tf_op | source)
XLA Modules:
  0.0 129.5 jit_solution(3484747765956730149)
XLA Ops:
  0.0 3.1 %fusion.7 = (bf16[8,32,1,512]{3,2,1,0:T(2,128)(2,1)S(1)}, bf16[8,32,1,512]{3,2,1,0:T(2,128)(2,1)S(1)}) fusion(bf16[8,32,64,512]{3,2,1,0:T(8,128)(2,1)} %vals_ref.1), kind=kLoop, calls=%fused_computation.39 | loop fusion | bytes 1048576 | tf_op jit(solution)/shard_map/slice | solution.py:210
  3.1 0.9 fusion.6
  4.0 4.9 %collective-permute-start = (bf16[8,32,512]{2,1,0:T(8,128)(2,1)S(1)}, bf16[8,32,512]{2,1,0:T(8,128)(2,1)S(1)}, u32[]{:S(2)}, u32[]{:S(2)}) collective-permute-start(bf16[8,32,512]{2,1,0:T(8,128)(2,1)S(1)} %get-tuple-element.8), channel_id=1, source_target_pairs={{0,4},{4,8},{8,12},{1,5},{5,9},{9,13},{2,6},{6,10},{10,14},{3,7},{... | collective-permute-start | bytes 786440 | tf_op jit(solution)/shard_map/ppermute | solution.py:185
  8.9 1.3 %fusion.9 = (f32[32,1,512]{2,1,0:T(1,128)S(1)}, f32[32,1,512]{2,1,0:T(1,128)S(1)}) fusion(f32[32,64,512]{2,1,0:T(8,128)} %ri_ref.1), kind=kLoop, calls=%fused_computation.41 | loop fusion | bytes 262144 | tf_op jit(solution)/shard_map/slice | solution.py:221
  10.3 1.3 %fusion.8 = (s32[32,1,512]{2,1,0:T(1,128)S(1)}, s32[32,1,512]{2,1,0:T(1,128)S(1)}) fusion(s32[32,64,512]{2,1,0:T(8,128)} %mi_ref.1), kind=kLoop, calls=%fused_computation.40 | loop fusion | bytes 262144 | tf_op jit(solution)/shard_map/slice | solution.py:221
  11.6 0.7 convert_bitcast_fusion
  12.9 1.8 %convert_reduce_fusion = s32[1024]{0:T(1024)S(1)} fusion(s32[4096]{0:T(1024)S(1)} %add_bitcast_fusion, s32[1024]{0:T(1024)S(1)} %iota_add_fusion), kind=kLoop, calls=%fused_computation.1 | loop fusion | flops 12581888 | bytes 24576 | tf_op jit(solution)/shard_map/reduce_sum | solution.py:247
  15.1 4.5 %fusion.w_ref = f32[4096,256]{1,0:T(8,128)} fusion(f32[64,256]{0,1:T(8,128)S(1)} %bitcast.45, s32[4096]{0:T(1024)S(1)} %copy-done.3), kind=kOutput, calls=%fused_computation.3 | convolution fusion | flops 805568512 | bytes 4276224 | tf_op jit(solution)/shard_map/dot_general | solution.py:233
  20.9 1.5 %collective-permute-start.1 = (bf16[8,32,512]{2,1,0:T(8,128)(2,1)S(1)}, bf16[8,32,512]{2,1,0:T(8,128)(2,1)S(1)}, u32[]{:S(2)}, u32[]{:S(2)}) collective-permute-start(bf16[8,32,512]{2,1,0:T(8,128)(2,1)S(1)} %get-tuple-element.6), channel_id=1, source_target_pairs={{4,0},{8,4},{12,8},{5,1},{9,5},{13,9},{6,2},{10,6},{14,10},{7,3},{... | collective-permute-start | bytes 786440 | tf_op jit(solution)/shard_map/ppermute | solution.py:186
  22.4 0.9 constant_dynamic-slice_fusion.1
  23.3 0.7 copy.48.ca_ref
  24.1 0.9 convert_element_type.21.lo_ref
  24.9 45.2 %shard_map.154 = f32[8,32,64,128]{3,2,1,0:T(8,128)} custom-call(f32[8]{0:T(128)} %load_ref.1, bf16[8,32,64,512]{3,2,1,0:T(8,128)(2,1)} %vals_ref.1, f32[8,32,512]{2,1,0:T(8,128)} %convert_element_type.21.lo_ref, f32[8,32,512]{2,1,0:T(8,128)} %get-tuple-element.7.up_ref, f32[32,64,512]{2,1,0:T(8,128)} %rl_ref.1, f32[32,64,512]{2,1,0:T(8,128)} %ri_ref.1, ...), custom_call_target="tpu_custom_call" | custom-call | tf_op jit(solution)/shard_map/pallas_call | solution.py:102
  70.2 9.3 %copy.49.t_ref = f32[128,64,256]{2,1,0:T(8,128)} copy(f32[128,64,256]{0,1,2:T(8,128)} %bitcast.43) | data formatting | bytes 16777216 | tf_op jit(solution)/shard_map/reshape | solution.py:227
  80.2 0.9 copy.50.rim_ref
  81.1 26.0 %shard_map.155 = f32[8,4096]{1,0:T(8,128)} custom-call(s32[4096]{0:T(1024)} %clamp_add_fusion.row_ref, bf16[256,192]{1,0:T(8,128)(2,1)} %copy.48.ca_ref, f32[128,64,256]{2,1,0:T(8,128)} %copy.49.t_ref, f32[128,2,256]{2,1,0:T(2,128)} %copy.50.rim_ref, f32[4096,256]{1,0:T(8,128)} %fusion.w_ref, bf16[8,256]{1,0:T(8,128)(2,1)} %fusion.5.group_ref), custom_call_target="tpu_custom_call" | custom-call | tf_op jit(solution)/shard_map/pallas_call | solution.py:159
  107.1 1.5 %collective-permute-done.2 = f32[8,4096]{1,0:T(8,128)S(1)} collective-permute-done((f32[8,4096]{1,0:T(8,128)}, f32[8,4096]{1,0:T(8,128)S(1)}, u32[]{:S(2)}, u32[]{:S(2)}) %collective-permute-start.2) | collective-permute-done | bytes 131104 | tf_op jit(solution)/shard_map/ppermute | solution.py:257
  108.7 0.9 add.61
  109.6 2.7 %collective-permute-start.3 = (f32[8,4096]{1,0:T(8,128)S(1)}, f32[8,4096]{1,0:T(8,128)S(1)}, u32[]{:S(2)}, u32[]{:S(2)}) collective-permute-start(f32[8,4096]{1,0:T(8,128)S(1)} %add.61), channel_id=1, source_target_pairs={{0,4},{4,0},{8,12},{12,8},{1,5},{5,1},{9,13},{13,9},{2,6},{6,2},{1... | collective-permute-start | bytes 393224 | tf_op jit(solution)/shard_map/ppermute | solution.py:257
  112.3 3.8 %collective-permute-done.3 = f32[8,4096]{1,0:T(8,128)S(1)} collective-permute-done((f32[8,4096]{1,0:T(8,128)S(1)}, f32[8,4096]{1,0:T(8,128)S(1)}, u32[]{:S(2)}, u32[]{:S(2)}) %collective-permute-start.3) | collective-permute-done | bytes 131104 | tf_op jit(solution)/shard_map/ppermute | solution.py:257
  116.1 2.8 %collective-permute-start.4 = (f32[8,4096]{1,0:T(8,128)S(1)}, f32[8,4096]{1,0:T(8,128)S(1)}, u32[]{:S(2)}, u32[]{:S(2)}) collective-permute-start(f32[8,4096]{1,0:T(8,128)S(1)} %add.62), channel_id=1, source_target_pairs={{0,8},{4,12},{8,0},{12,4},{1,9},{5,13},{9,1},{13,5},{2,10},{6,14},... | collective-permute-start | bytes 393224 | tf_op jit(solution)/shard_map/ppermute | solution.py:257
  118.9 6.0 %collective-permute-done.4 = f32[8,4096]{1,0:T(8,128)S(1)} collective-permute-done((f32[8,4096]{1,0:T(8,128)S(1)}, f32[8,4096]{1,0:T(8,128)S(1)}, u32[]{:S(2)}, u32[]{:S(2)}) %collective-permute-start.4) | collective-permute-done | bytes 131104 | tf_op jit(solution)/shard_map/ppermute | solution.py:257
  125.6 2.8 %gather_fusion = f32[1024,8]{1,0:T(8,128)S(1)} fusion(f32[8,4096]{0,1:T(8,128)S(1)} %copy.51, s32[1024]{0:T(1024)S(1)} %broadcast_clamp_fusion), kind=kCustom, calls=%fused_computation | custom fusion | bytes 69632 | tf_op jit(solution)/shard_map/jit(_take)/gather | solution.py:248
  128.7 0.8 copy.52
  (45 shorter events, 4.0 us)
Async XLA Ops:
  0.0 14.7 %copy-start = (f32[64,64]{1,0:T(8,128)S(1)}, f32[64,64]{1,0:T(8,128)}, u32[]{:S(2)}) copy-start(f32[64,64]{1,0:T(8,128)} %param.23) | copy-start | bytes 49156
  0.0 14.7 %copy-start.4 = (f32[64,64]{1,0:T(8,128)S(1)}, f32[64,64]{1,0:T(8,128)}, u32[]{:S(2)}) copy-start(f32[64,64]{1,0:T(8,128)} %constant.77.clone) | copy-start | bytes 49156
  0.0 15.0 %copy-start.3 = (s32[4096]{0:T(1024)S(1)}, s32[4096]{0:T(1024)}, u32[]{:S(2)}) copy-start(s32[4096]{0:T(1024)} %param.26) | copy-start | bytes 49156
  4.0 16.8 %collective-permute-start = (bf16[8,32,512]{2,1,0:T(8,128)(2,1)S(1)}, bf16[8,32,512]{2,1,0:T(8,128)(2,1)S(1)}, u32[]{:S(2)}, u32[]{:S(2)}) collective-permute-start(bf16[8,32,512]{2,1,0:T(8,128)(2,1)S(1)} %get-tuple-element.8), channel_id=1, source_target_pairs={{0,4},{4,8},{8,12},{1,5},{5,9},{9,13},{2,6},{6,10},{10,14},{3,7},{... | collective-permute-start | bytes 786440 | tf_op jit(solution)/shard_map/ppermute | solution.py:185
  10.3 9.3 %copy-start.5 = (s32[4096]{0:T(1024)S(1)}, s32[4096]{0:T(1024)}, u32[]{:S(2)}) copy-start(s32[4096]{0:T(1024)} %param.25) | copy-start | bytes 49156
  10.3 9.3 %copy-start.6 = (s32[4096]{0:T(1024)S(1)}, s32[4096]{0:T(1024)}, u32[]{:S(2)}) copy-start(s32[4096]{0:T(1024)} %param.24) | copy-start | bytes 49156
  20.9 58.6 %collective-permute-start.1 = (bf16[8,32,512]{2,1,0:T(8,128)(2,1)S(1)}, bf16[8,32,512]{2,1,0:T(8,128)(2,1)S(1)}, u32[]{:S(2)}, u32[]{:S(2)}) collective-permute-start(bf16[8,32,512]{2,1,0:T(8,128)(2,1)S(1)} %get-tuple-element.6), channel_id=1, source_target_pairs={{4,0},{8,4},{12,8},{5,1},{9,5},{13,9},{6,2},{10,6},{14,10},{7,3},{... | collective-permute-start | bytes 786440 | tf_op jit(solution)/shard_map/ppermute | solution.py:186
  70.2 9.4 %copy-start.2 = (f32[128,512,1,1]{1,0,3,2:T(8,128)S(1)}, f32[128,512,1,1]{1,0,3,2:T(8,128)}, u32[]{:S(2)}) copy-start(f32[128,512,1,1]{1,0,3,2:T(8,128)} %constant.78) | copy-start | bytes 786436
  81.1 48.4 %copy-start.1 = (f32[64,64]{1,0:T(8,128)S(1)}, f32[64,64]{1,0:T(8,128)}, u32[]{:S(2)}) copy-start(f32[64,64]{1,0:T(8,128)} %param.23) | copy-start | bytes 49156
  107.1 1.6 %collective-permute-start.2 = (f32[8,4096]{1,0:T(8,128)}, f32[8,4096]{1,0:T(8,128)S(1)}, u32[]{:S(2)}, u32[]{:S(2)}) collective-permute-start(f32[8,4096]{1,0:T(8,128)} %shard_map.155), channel_id=1, source_target_pairs={{0,1},{1,0},{2,3},{3,2},{4,5},{5,4},{6,7},{7,6},{8,9},{9,8},{10,11... | collective-permute-start | bytes 393224 | tf_op jit(solution)/shard_map/ppermute | solution.py:257
  109.6 6.5 %collective-permute-start.3 = (f32[8,4096]{1,0:T(8,128)S(1)}, f32[8,4096]{1,0:T(8,128)S(1)}, u32[]{:S(2)}, u32[]{:S(2)}) collective-permute-start(f32[8,4096]{1,0:T(8,128)S(1)} %add.61), channel_id=1, source_target_pairs={{0,4},{4,0},{8,12},{12,8},{1,5},{5,1},{9,13},{13,9},{2,6},{6,2},{1... | collective-permute-start | bytes 393224 | tf_op jit(solution)/shard_map/ppermute | solution.py:257
  116.1 8.8 %collective-permute-start.4 = (f32[8,4096]{1,0:T(8,128)S(1)}, f32[8,4096]{1,0:T(8,128)S(1)}, u32[]{:S(2)}, u32[]{:S(2)}) collective-permute-start(f32[8,4096]{1,0:T(8,128)S(1)} %add.62), channel_id=1, source_target_pairs={{0,8},{4,12},{8,0},{12,4},{1,9},{5,13},{9,1},{13,5},{2,10},{6,14},... | collective-permute-start | bytes 393224 | tf_op jit(solution)/shard_map/ppermute | solution.py:257

commit v19 on v18

--- a/solution.py
+++ b/solution.py
@@ -155,7 +155,7 @@
     kb, na_loc, lanes = t.shape
     na, depth = ca.shape
     count = row_index.shape[0]
-    block = 32
+    block = 64
     return pl.pallas_call(
         illiquid_kernel,
         grid_spec=pltpu.PrefetchScalarGridSpec(

time: 130 us -> 130 us (level)
  no operation moved by 1% of the time
where the time goes in v19:
time: 130 us
  Pallas kernels  71.5 us (55%)
  local copies, waits for them, and re-layouts  22 us (17%)
  starting transfers between devices  11.9 us (9%)
  waiting for transfers between devices  11.4 us (9%)
  other arithmetic  7.46 us (6%)
  matrix products  5.29 us (4%)
    pallas_call x1, Pallas kernels, liquid_step(): pl.pallas_call(step_kernel, grid=(nz // zb,), in_specs=[pl.BlockSpec(memo...  45.2 us
    pallas_call x1, Pallas kernels, illiquid_pick(): pl.pallas_call(illiquid_kernel, grid_spec=pltpu.PrefetchScalarGridSpec(nu...  26.3 us
    ppermute x3, waiting for transfers between devices, all_sum(): x = x + lax.ppermute(x, axis, [(i, i ^ step) for i in range(count)])  11.4 us
    reshape x1, local copies, waits for them, and re-layouts, body(): jnp.transpose(liquid_part, (3, 2, 0, 1))  9.3 us
    ppermute x3, starting transfers between devices, all_sum(): x = x + lax.ppermute(x, axis, [(i, i ^ step) for i in range(count)])  5.44 us
    ppermute x1, starting transfers between devices, edges(): lax.ppermute(tail, axis, [(i, (i + 1) % count) for i in range(ends)])  4.95 us
    dot_general x1, matrix products, body(): jnp.dot(pick_z, jnp.tile(folded, (1, columns)), precision=lax.Precision.H...  4.47 us
    slice x1, local copies, waits for them, and re-layouts, body(): head = values_in[:, :, 0, :].astype(jnp.float32)  3.06 us
  transfers between devices with their start and end apart: 5, of which 3 were waited for; matrix products, arithmetic and copies ran while one was open for 18% of the time, Pallas kernels for 35%

profile of v19, /device:TPU:0, one launch (start us, length us, event | category | flops | bytes accessed | tf_op | source)
XLA Modules:
  0.0 129.7 jit_solution(14655214314966345359)
XLA Ops:
  0.0 3.1 %fusion.7 = (bf16[8,32,1,512]{3,2,1,0:T(2,128)(2,1)S(1)}, bf16[8,32,1,512]{3,2,1,0:T(2,128)(2,1)S(1)}) fusion(bf16[8,32,64,512]{3,2,1,0:T(8,128)(2,1)} %vals_ref.1), kind=kLoop, calls=%fused_computation.39 | loop fusion | bytes 1048576 | tf_op jit(solution)/shard_map/slice | solution.py:210
  3.1 0.9 fusion.6
  4.0 4.9 %collective-permute-start = (bf16[8,32,512]{2,1,0:T(8,128)(2,1)S(1)}, bf16[8,32,512]{2,1,0:T(8,128)(2,1)S(1)}, u32[]{:S(2)}, u32[]{:S(2)}) collective-permute-start(bf16[8,32,512]{2,1,0:T(8,128)(2,1)S(1)} %get-tuple-element.8), channel_id=1, source_target_pairs={{0,4},{4,8},{8,12},{1,5},{5,9},{9,13},{2,6},{6,10},{10,14},{3,7},{... | collective-permute-start | bytes 786440 | tf_op jit(solution)/shard_map/ppermute | solution.py:185
  8.9 1.3 %fusion.9 = (f32[32,1,512]{2,1,0:T(1,128)S(1)}, f32[32,1,512]{2,1,0:T(1,128)S(1)}) fusion(f32[32,64,512]{2,1,0:T(8,128)} %ri_ref.1), kind=kLoop, calls=%fused_computation.41 | loop fusion | bytes 262144 | tf_op jit(solution)/shard_map/slice | solution.py:221
  10.3 1.3 %fusion.8 = (s32[32,1,512]{2,1,0:T(1,128)S(1)}, s32[32,1,512]{2,1,0:T(1,128)S(1)}) fusion(s32[32,64,512]{2,1,0:T(8,128)} %mi_ref.1), kind=kLoop, calls=%fused_computation.40 | loop fusion | bytes 262144 | tf_op jit(solution)/shard_map/slice | solution.py:221
  11.6 0.7 convert_bitcast_fusion
  12.9 1.8 %convert_reduce_fusion = s32[1024]{0:T(1024)S(1)} fusion(s32[4096]{0:T(1024)S(1)} %add_bitcast_fusion, s32[1024]{0:T(1024)S(1)} %iota_add_fusion), kind=kLoop, calls=%fused_computation.1 | loop fusion | flops 12581888 | bytes 24576 | tf_op jit(solution)/shard_map/reduce_sum | solution.py:247
  15.1 4.5 %fusion.w_ref = f32[4096,256]{1,0:T(8,128)} fusion(f32[64,256]{0,1:T(8,128)S(1)} %bitcast.45, s32[4096]{0:T(1024)S(1)} %copy-done.3), kind=kOutput, calls=%fused_computation.3 | convolution fusion | flops 805568512 | bytes 4276224 | tf_op jit(solution)/shard_map/dot_general | solution.py:233
  20.9 1.5 %collective-permute-start.1 = (bf16[8,32,512]{2,1,0:T(8,128)(2,1)S(1)}, bf16[8,32,512]{2,1,0:T(8,128)(2,1)S(1)}, u32[]{:S(2)}, u32[]{:S(2)}) collective-permute-start(bf16[8,32,512]{2,1,0:T(8,128)(2,1)S(1)} %get-tuple-element.6), channel_id=1, source_target_pairs={{4,0},{8,4},{12,8},{5,1},{9,5},{13,9},{6,2},{10,6},{14,10},{7,3},{... | collective-permute-start | bytes 786440 | tf_op jit(solution)/shard_map/ppermute | solution.py:186
  22.4 0.9 constant_dynamic-slice_fusion.1
  23.3 0.7 copy.48.ca_ref
  24.1 0.9 convert_element_type.21.lo_ref
  24.9 45.2 %shard_map.154 = f32[8,32,64,128]{3,2,1,0:T(8,128)} custom-call(f32[8]{0:T(128)} %load_ref.1, bf16[8,32,64,512]{3,2,1,0:T(8,128)(2,1)} %vals_ref.1, f32[8,32,512]{2,1,0:T(8,128)} %convert_element_type.21.lo_ref, f32[8,32,512]{2,1,0:T(8,128)} %get-tuple-element.7.up_ref, f32[32,64,512]{2,1,0:T(8,128)} %rl_ref.1, f32[32,64,512]{2,1,0:T(8,128)} %ri_ref.1, ...), custom_call_target="tpu_custom_call" | custom-call | tf_op jit(solution)/shard_map/pallas_call | solution.py:102
  70.2 9.3 %copy.49.t_ref = f32[128,64,256]{2,1,0:T(8,128)} copy(f32[128,64,256]{0,1,2:T(8,128)} %bitcast.43) | data formatting | bytes 16777216 | tf_op jit(solution)/shard_map/reshape | solution.py:227
  80.2 0.9 copy.50.rim_ref
  81.1 26.3 %shard_map.155 = f32[8,4096]{1,0:T(8,128)} custom-call(s32[4096]{0:T(1024)} %clamp_add_fusion.row_ref, bf16[256,192]{1,0:T(8,128)(2,1)} %copy.48.ca_ref, f32[128,64,256]{2,1,0:T(8,128)} %copy.49.t_ref, f32[128,2,256]{2,1,0:T(2,128)} %copy.50.rim_ref, f32[4096,256]{1,0:T(8,128)} %fusion.w_ref, bf16[8,256]{1,0:T(8,128)(2,1)} %fusion.5.group_ref), custom_call_target="tpu_custom_call" | custom-call | tf_op jit(solution)/shard_map/pallas_call | solution.py:159
  107.3 1.5 %collective-permute-done.2 = f32[8,4096]{1,0:T(8,128)S(1)} collective-permute-done((f32[8,4096]{1,0:T(8,128)}, f32[8,4096]{1,0:T(8,128)S(1)}, u32[]{:S(2)}, u32[]{:S(2)}) %collective-permute-start.2) | collective-permute-done | bytes 131104 | tf_op jit(solution)/shard_map/ppermute | solution.py:257
  108.9 0.9 add.61
  109.8 2.6 %collective-permute-start.3 = (f32[8,4096]{1,0:T(8,128)S(1)}, f32[8,4096]{1,0:T(8,128)S(1)}, u32[]{:S(2)}, u32[]{:S(2)}) collective-permute-start(f32[8,4096]{1,0:T(8,128)S(1)} %add.61), channel_id=1, source_target_pairs={{0,4},{4,0},{8,12},{12,8},{1,5},{5,1},{9,13},{13,9},{2,6},{6,2},{1... | collective-permute-start | bytes 393224 | tf_op jit(solution)/shard_map/ppermute | solution.py:257
  112.5 3.8 %collective-permute-done.3 = f32[8,4096]{1,0:T(8,128)S(1)} collective-permute-done((f32[8,4096]{1,0:T(8,128)S(1)}, f32[8,4096]{1,0:T(8,128)S(1)}, u32[]{:S(2)}, u32[]{:S(2)}) %collective-permute-start.3) | collective-permute-done | bytes 131104 | tf_op jit(solution)/shard_map/ppermute | solution.py:257
  116.3 2.8 %collective-permute-start.4 = (f32[8,4096]{1,0:T(8,128)S(1)}, f32[8,4096]{1,0:T(8,128)S(1)}, u32[]{:S(2)}, u32[]{:S(2)}) collective-permute-start(f32[8,4096]{1,0:T(8,128)S(1)} %add.62), channel_id=1, source_target_pairs={{0,8},{4,12},{8,0},{12,4},{1,9},{5,13},{9,1},{13,5},{2,10},{6,14},... | collective-permute-start | bytes 393224 | tf_op jit(solution)/shard_map/ppermute | solution.py:257
  119.1 6.0 %collective-permute-done.4 = f32[8,4096]{1,0:T(8,128)S(1)} collective-permute-done((f32[8,4096]{1,0:T(8,128)S(1)}, f32[8,4096]{1,0:T(8,128)S(1)}, u32[]{:S(2)}, u32[]{:S(2)}) %collective-permute-start.4) | collective-permute-done | bytes 131104 | tf_op jit(solution)/shard_map/ppermute | solution.py:257
  125.7 2.8 %gather_fusion = f32[1024,8]{1,0:T(8,128)S(1)} fusion(f32[8,4096]{0,1:T(8,128)S(1)} %copy.51, s32[1024]{0:T(1024)S(1)} %broadcast_clamp_fusion), kind=kCustom, calls=%fused_computation | custom fusion | bytes 69632 | tf_op jit(solution)/shard_map/jit(_take)/gather | solution.py:248
  128.9 0.8 copy.52
  (45 shorter events, 4.0 us)
Async XLA Ops:
  0.0 14.7 %copy-start = (f32[64,64]{1,0:T(8,128)S(1)}, f32[64,64]{1,0:T(8,128)}, u32[]{:S(2)}) copy-start(f32[64,64]{1,0:T(8,128)} %param.23) | copy-start | bytes 49156
  0.0 14.7 %copy-start.4 = (f32[64,64]{1,0:T(8,128)S(1)}, f32[64,64]{1,0:T(8,128)}, u32[]{:S(2)}) copy-start(f32[64,64]{1,0:T(8,128)} %constant.77.clone) | copy-start | bytes 49156
  0.0 15.0 %copy-start.3 = (s32[4096]{0:T(1024)S(1)}, s32[4096]{0:T(1024)}, u32[]{:S(2)}) copy-start(s32[4096]{0:T(1024)} %param.26) | copy-start | bytes 49156
  4.0 16.8 %collective-permute-start = (bf16[8,32,512]{2,1,0:T(8,128)(2,1)S(1)}, bf16[8,32,512]{2,1,0:T(8,128)(2,1)S(1)}, u32[]{:S(2)}, u32[]{:S(2)}) collective-permute-start(bf16[8,32,512]{2,1,0:T(8,128)(2,1)S(1)} %get-tuple-element.8), channel_id=1, source_target_pairs={{0,4},{4,8},{8,12},{1,5},{5,9},{9,13},{2,6},{6,10},{10,14},{3,7},{... | collective-permute-start | bytes 786440 | tf_op jit(solution)/shard_map/ppermute | solution.py:185
  10.3 9.3 %copy-start.5 = (s32[4096]{0:T(1024)S(1)}, s32[4096]{0:T(1024)}, u32[]{:S(2)}) copy-start(s32[4096]{0:T(1024)} %param.25) | copy-start | bytes 49156
  10.3 9.3 %copy-start.6 = (s32[4096]{0:T(1024)S(1)}, s32[4096]{0:T(1024)}, u32[]{:S(2)}) copy-start(s32[4096]{0:T(1024)} %param.24) | copy-start | bytes 49156
  20.9 58.6 %collective-permute-start.1 = (bf16[8,32,512]{2,1,0:T(8,128)(2,1)S(1)}, bf16[8,32,512]{2,1,0:T(8,128)(2,1)S(1)}, u32[]{:S(2)}, u32[]{:S(2)}) collective-permute-start(bf16[8,32,512]{2,1,0:T(8,128)(2,1)S(1)} %get-tuple-element.6), channel_id=1, source_target_pairs={{4,0},{8,4},{12,8},{5,1},{9,5},{13,9},{6,2},{10,6},{14,10},{7,3},{... | collective-permute-start | bytes 786440 | tf_op jit(solution)/shard_map/ppermute | solution.py:186
  70.2 9.4 %copy-start.2 = (f32[128,512,1,1]{1,0,3,2:T(8,128)S(1)}, f32[128,512,1,1]{1,0,3,2:T(8,128)}, u32[]{:S(2)}) copy-start(f32[128,512,1,1]{1,0,3,2:T(8,128)} %constant.78) | copy-start | bytes 786436
  81.1 48.6 %copy-start.1 = (f32[64,64]{1,0:T(8,128)S(1)}, f32[64,64]{1,0:T(8,128)}, u32[]{:S(2)}) copy-start(f32[64,64]{1,0:T(8,128)} %param.23) | copy-start | bytes 49156
  107.3 1.6 %collective-permute-start.2 = (f32[8,4096]{1,0:T(8,128)}, f32[8,4096]{1,0:T(8,128)S(1)}, u32[]{:S(2)}, u32[]{:S(2)}) collective-permute-start(f32[8,4096]{1,0:T(8,128)} %shard_map.155), channel_id=1, source_target_pairs={{0,1},{1,0},{2,3},{3,2},{4,5},{5,4},{6,7},{7,6},{8,9},{9,8},{10,11... | collective-permute-start | bytes 393224 | tf_op jit(solution)/shard_map/ppermute | solution.py:257
  109.8 6.4 %collective-permute-start.3 = (f32[8,4096]{1,0:T(8,128)S(1)}, f32[8,4096]{1,0:T(8,128)S(1)}, u32[]{:S(2)}, u32[]{:S(2)}) collective-permute-start(f32[8,4096]{1,0:T(8,128)S(1)} %add.61), channel_id=1, source_target_pairs={{0,4},{4,0},{8,12},{12,8},{1,5},{5,1},{9,13},{13,9},{2,6},{6,2},{1... | collective-permute-start | bytes 393224 | tf_op jit(solution)/shard_map/ppermute | solution.py:257
  116.3 8.8 %collective-permute-start.4 = (f32[8,4096]{1,0:T(8,128)S(1)}, f32[8,4096]{1,0:T(8,128)S(1)}, u32[]{:S(2)}, u32[]{:S(2)}) collective-permute-start(f32[8,4096]{1,0:T(8,128)S(1)} %add.62), channel_id=1, source_target_pairs={{0,8},{4,12},{8,0},{12,4},{1,9},{5,13},{9,1},{13,5},{2,10},{6,14},... | collective-permute-start | bytes 393224 | tf_op jit(solution)/shard_map/ppermute | solution.py:257

commit v20 on v18

--- a/solution.py
+++ b/solution.py
@@ -139,7 +139,7 @@
             picked[pl.ds(i, 1), :] = spectrum[pl.ds(row_ref[i], 1), :]
             return carry
 
-        lax.fori_loop(0, picked.shape[0], pick, 0, unroll=32)
+        lax.fori_loop(0, picked.shape[0], pick, 0, unroll=64)
         rest = picked[...] * w_ref[...]
         group = group_ref[...]
         total = None

time: 130 us -> 130 us (level)
  no operation moved by 1% of the time
where the time goes in v20:
time: 130 us; the launch traced here: 129 us
  Pallas kernels  71 us (55%)
  local copies, waits for them, and re-layouts  22 us (17%)
  starting transfers between devices  11.9 us (9%)
  waiting for transfers between devices  11.4 us (9%)
  other arithmetic  7.46 us (6%)
  matrix products  5.29 us (4%)
    pallas_call x1, Pallas kernels, liquid_step(): pl.pallas_call(step_kernel, grid=(nz // zb,), in_specs=[pl.BlockSpec(memo...  45.2 us
    pallas_call x1, Pallas kernels, illiquid_pick(): pl.pallas_call(illiquid_kernel, grid_spec=pltpu.PrefetchScalarGridSpec(nu...  25.7 us
    ppermute x3, waiting for transfers between devices, all_sum(): x = x + lax.ppermute(x, axis, [(i, i ^ step) for i in range(count)])  11.4 us
    reshape x1, local copies, waits for them, and re-layouts, body(): jnp.transpose(liquid_part, (3, 2, 0, 1))  9.3 us
    ppermute x3, starting transfers between devices, all_sum(): x = x + lax.ppermute(x, axis, [(i, i ^ step) for i in range(count)])  5.52 us
    ppermute x1, starting transfers between devices, edges(): lax.ppermute(tail, axis, [(i, (i + 1) % count) for i in range(ends)])  4.95 us
    dot_general x1, matrix products, body(): jnp.dot(pick_z, jnp.tile(folded, (1, columns)), precision=lax.Precision.H...  4.47 us
    slice x1, local copies, waits for them, and re-layouts, body(): head = values_in[:, :, 0, :].astype(jnp.float32)  3.06 us
  transfers between devices with their start and end apart: 5, of which 3 were waited for; matrix products, arithmetic and copies ran while one was open for 18% of the time, Pallas kernels for 35%

profile of v20, /device:TPU:0, one launch (start us, length us, event | category | flops | bytes accessed | tf_op | source)
XLA Modules:
  0.0 129.2 jit_solution(8148894902674856757)
XLA Ops:
  0.0 3.1 %fusion.7 = (bf16[8,32,1,512]{3,2,1,0:T(2,128)(2,1)S(1)}, bf16[8,32,1,512]{3,2,1,0:T(2,128)(2,1)S(1)}) fusion(bf16[8,32,64,512]{3,2,1,0:T(8,128)(2,1)} %vals_ref.1), kind=kLoop, calls=%fused_computation.39 | loop fusion | bytes 1048576 | tf_op jit(solution)/shard_map/slice | solution.py:210
  3.1 0.9 fusion.6
  4.0 4.9 %collective-permute-start = (bf16[8,32,512]{2,1,0:T(8,128)(2,1)S(1)}, bf16[8,32,512]{2,1,0:T(8,128)(2,1)S(1)}, u32[]{:S(2)}, u32[]{:S(2)}) collective-permute-start(bf16[8,32,512]{2,1,0:T(8,128)(2,1)S(1)} %get-tuple-element.8), channel_id=1, source_target_pairs={{0,4},{4,8},{8,12},{1,5},{5,9},{9,13},{2,6},{6,10},{10,14},{3,7},{... | collective-permute-start | bytes 786440 | tf_op jit(solution)/shard_map/ppermute | solution.py:185
  8.9 1.3 %fusion.9 = (f32[32,1,512]{2,1,0:T(1,128)S(1)}, f32[32,1,512]{2,1,0:T(1,128)S(1)}) fusion(f32[32,64,512]{2,1,0:T(8,128)} %ri_ref.1), kind=kLoop, calls=%fused_computation.41 | loop fusion | bytes 262144 | tf_op jit(solution)/shard_map/slice | solution.py:221
  10.3 1.3 %fusion.8 = (s32[32,1,512]{2,1,0:T(1,128)S(1)}, s32[32,1,512]{2,1,0:T(1,128)S(1)}) fusion(s32[32,64,512]{2,1,0:T(8,128)} %mi_ref.1), kind=kLoop, calls=%fused_computation.40 | loop fusion | bytes 262144 | tf_op jit(solution)/shard_map/slice | solution.py:221
  11.6 0.7 convert_bitcast_fusion
  12.9 1.8 %convert_reduce_fusion = s32[1024]{0:T(1024)S(1)} fusion(s32[4096]{0:T(1024)S(1)} %add_bitcast_fusion, s32[1024]{0:T(1024)S(1)} %iota_add_fusion), kind=kLoop, calls=%fused_computation.1 | loop fusion | flops 12581888 | bytes 24576 | tf_op jit(solution)/shard_map/reduce_sum | solution.py:247
  15.1 4.5 %fusion.w_ref = f32[4096,256]{1,0:T(8,128)} fusion(f32[64,256]{0,1:T(8,128)S(1)} %bitcast.45, s32[4096]{0:T(1024)S(1)} %copy-done.3), kind=kOutput, calls=%fused_computation.3 | convolution fusion | flops 805568512 | bytes 4276224 | tf_op jit(solution)/shard_map/dot_general | solution.py:233
  20.9 1.5 %collective-permute-start.1 = (bf16[8,32,512]{2,1,0:T(8,128)(2,1)S(1)}, bf16[8,32,512]{2,1,0:T(8,128)(2,1)S(1)}, u32[]{:S(2)}, u32[]{:S(2)}) collective-permute-start(bf16[8,32,512]{2,1,0:T(8,128)(2,1)S(1)} %get-tuple-element.6), channel_id=1, source_target_pairs={{4,0},{8,4},{12,8},{5,1},{9,5},{13,9},{6,2},{10,6},{14,10},{7,3},{... | collective-permute-start | bytes 786440 | tf_op jit(solution)/shard_map/ppermute | solution.py:186
  22.4 0.9 constant_dynamic-slice_fusion.1
  23.3 0.7 copy.48.ca_ref
  24.1 0.9 convert_element_type.21.lo_ref
  24.9 45.2 %shard_map.154 = f32[8,32,64,128]{3,2,1,0:T(8,128)} custom-call(f32[8]{0:T(128)} %load_ref.1, bf16[8,32,64,512]{3,2,1,0:T(8,128)(2,1)} %vals_ref.1, f32[8,32,512]{2,1,0:T(8,128)} %convert_element_type.21.lo_ref, f32[8,32,512]{2,1,0:T(8,128)} %get-tuple-element.7.up_ref, f32[32,64,512]{2,1,0:T(8,128)} %rl_ref.1, f32[32,64,512]{2,1,0:T(8,128)} %ri_ref.1, ...), custom_call_target="tpu_custom_call" | custom-call | tf_op jit(solution)/shard_map/pallas_call | solution.py:102
  70.2 9.3 %copy.49.t_ref = f32[128,64,256]{2,1,0:T(8,128)} copy(f32[128,64,256]{0,1,2:T(8,128)} %bitcast.43) | data formatting | bytes 16777216 | tf_op jit(solution)/shard_map/reshape | solution.py:227
  80.2 0.9 copy.50.rim_ref
  81.1 25.7 %shard_map.155 = f32[8,4096]{1,0:T(8,128)} custom-call(s32[4096]{0:T(1024)} %clamp_add_fusion.row_ref, bf16[256,192]{1,0:T(8,128)(2,1)} %copy.48.ca_ref, f32[128,64,256]{2,1,0:T(8,128)} %copy.49.t_ref, f32[128,2,256]{2,1,0:T(2,128)} %copy.50.rim_ref, f32[4096,256]{1,0:T(8,128)} %fusion.w_ref, bf16[8,256]{1,0:T(8,128)(2,1)} %fusion.5.group_ref), custom_call_target="tpu_custom_call" | custom-call | tf_op jit(solution)/shard_map/pallas_call | solution.py:159
  106.8 1.5 %collective-permute-done.2 = f32[8,4096]{1,0:T(8,128)S(1)} collective-permute-done((f32[8,4096]{1,0:T(8,128)}, f32[8,4096]{1,0:T(8,128)S(1)}, u32[]{:S(2)}, u32[]{:S(2)}) %collective-permute-start.2) | collective-permute-done | bytes 131104 | tf_op jit(solution)/shard_map/ppermute | solution.py:257
  108.4 0.9 add.61
  109.3 2.7 %collective-permute-start.3 = (f32[8,4096]{1,0:T(8,128)S(1)}, f32[8,4096]{1,0:T(8,128)S(1)}, u32[]{:S(2)}, u32[]{:S(2)}) collective-permute-start(f32[8,4096]{1,0:T(8,128)S(1)} %add.61), channel_id=1, source_target_pairs={{0,4},{4,0},{8,12},{12,8},{1,5},{5,1},{9,13},{13,9},{2,6},{6,2},{1... | collective-permute-start | bytes 393224 | tf_op jit(solution)/shard_map/ppermute | solution.py:257
  112.0 3.8 %collective-permute-done.3 = f32[8,4096]{1,0:T(8,128)S(1)} collective-permute-done((f32[8,4096]{1,0:T(8,128)S(1)}, f32[8,4096]{1,0:T(8,128)S(1)}, u32[]{:S(2)}, u32[]{:S(2)}) %collective-permute-start.3) | collective-permute-done | bytes 131104 | tf_op jit(solution)/shard_map/ppermute | solution.py:257
  115.8 2.8 %collective-permute-start.4 = (f32[8,4096]{1,0:T(8,128)S(1)}, f32[8,4096]{1,0:T(8,128)S(1)}, u32[]{:S(2)}, u32[]{:S(2)}) collective-permute-start(f32[8,4096]{1,0:T(8,128)S(1)} %add.62), channel_id=1, source_target_pairs={{0,8},{4,12},{8,0},{12,4},{1,9},{5,13},{9,1},{13,5},{2,10},{6,14},... | collective-permute-start | bytes 393224 | tf_op jit(solution)/shard_map/ppermute | solution.py:257
  118.7 6.0 %collective-permute-done.4 = f32[8,4096]{1,0:T(8,128)S(1)} collective-permute-done((f32[8,4096]{1,0:T(8,128)S(1)}, f32[8,4096]{1,0:T(8,128)S(1)}, u32[]{:S(2)}, u32[]{:S(2)}) %collective-permute-start.4) | collective-permute-done | bytes 131104 | tf_op jit(solution)/shard_map/ppermute | solution.py:257
  125.3 2.8 %gather_fusion = f32[1024,8]{1,0:T(8,128)S(1)} fusion(f32[8,4096]{0,1:T(8,128)S(1)} %copy.51, s32[1024]{0:T(1024)S(1)} %broadcast_clamp_fusion), kind=kCustom, calls=%fused_computation | custom fusion | bytes 69632 | tf_op jit(solution)/shard_map/jit(_take)/gather | solution.py:248
  128.5 0.8 copy.52
  (45 shorter events, 4.0 us)
Async XLA Ops:
  0.0 14.7 %copy-start = (f32[64,64]{1,0:T(8,128)S(1)}, f32[64,64]{1,0:T(8,128)}, u32[]{:S(2)}) copy-start(f32[64,64]{1,0:T(8,128)} %param.23) | copy-start | bytes 49156
  0.0 14.7 %copy-start.4 = (f32[64,64]{1,0:T(8,128)S(1)}, f32[64,64]{1,0:T(8,128)}, u32[]{:S(2)}) copy-start(f32[64,64]{1,0:T(8,128)} %constant.77.clone) | copy-start | bytes 49156
  0.0 15.0 %copy-start.3 = (s32[4096]{0:T(1024)S(1)}, s32[4096]{0:T(1024)}, u32[]{:S(2)}) copy-start(s32[4096]{0:T(1024)} %param.26) | copy-start | bytes 49156
  4.0 16.8 %collective-permute-start = (bf16[8,32,512]{2,1,0:T(8,128)(2,1)S(1)}, bf16[8,32,512]{2,1,0:T(8,128)(2,1)S(1)}, u32[]{:S(2)}, u32[]{:S(2)}) collective-permute-start(bf16[8,32,512]{2,1,0:T(8,128)(2,1)S(1)} %get-tuple-element.8), channel_id=1, source_target_pairs={{0,4},{4,8},{8,12},{1,5},{5,9},{9,13},{2,6},{6,10},{10,14},{3,7},{... | collective-permute-start | bytes 786440 | tf_op jit(solution)/shard_map/ppermute | solution.py:185
  10.3 9.3 %copy-start.5 = (s32[4096]{0:T(1024)S(1)}, s32[4096]{0:T(1024)}, u32[]{:S(2)}) copy-start(s32[4096]{0:T(1024)} %param.25) | copy-start | bytes 49156
  10.3 9.3 %copy-start.6 = (s32[4096]{0:T(1024)S(1)}, s32[4096]{0:T(1024)}, u32[]{:S(2)}) copy-start(s32[4096]{0:T(1024)} %param.24) | copy-start | bytes 49156
  20.9 58.6 %collective-permute-start.1 = (bf16[8,32,512]{2,1,0:T(8,128)(2,1)S(1)}, bf16[8,32,512]{2,1,0:T(8,128)(2,1)S(1)}, u32[]{:S(2)}, u32[]{:S(2)}) collective-permute-start(bf16[8,32,512]{2,1,0:T(8,128)(2,1)S(1)} %get-tuple-element.6), channel_id=1, source_target_pairs={{4,0},{8,4},{12,8},{5,1},{9,5},{13,9},{6,2},{10,6},{14,10},{7,3},{... | collective-permute-start | bytes 786440 | tf_op jit(solution)/shard_map/ppermute | solution.py:186
  70.2 9.4 %copy-start.2 = (f32[128,512,1,1]{1,0,3,2:T(8,128)S(1)}, f32[128,512,1,1]{1,0,3,2:T(8,128)}, u32[]{:S(2)}) copy-start(f32[128,512,1,1]{1,0,3,2:T(8,128)} %constant.78) | copy-start | bytes 786436
  81.1 48.2 %copy-start.1 = (f32[64,64]{1,0:T(8,128)S(1)}, f32[64,64]{1,0:T(8,128)}, u32[]{:S(2)}) copy-start(f32[64,64]{1,0:T(8,128)} %param.23) | copy-start | bytes 49156
  106.8 1.6 %collective-permute-start.2 = (f32[8,4096]{1,0:T(8,128)}, f32[8,4096]{1,0:T(8,128)S(1)}, u32[]{:S(2)}, u32[]{:S(2)}) collective-permute-start(f32[8,4096]{1,0:T(8,128)} %shard_map.155), channel_id=1, source_target_pairs={{0,1},{1,0},{2,3},{3,2},{4,5},{5,4},{6,7},{7,6},{8,9},{9,8},{10,11... | collective-permute-start | bytes 393224 | tf_op jit(solution)/shard_map/ppermute | solution.py:257
  109.3 6.5 %collective-permute-start.3 = (f32[8,4096]{1,0:T(8,128)S(1)}, f32[8,4096]{1,0:T(8,128)S(1)}, u32[]{:S(2)}, u32[]{:S(2)}) collective-permute-start(f32[8,4096]{1,0:T(8,128)S(1)} %add.61), channel_id=1, source_target_pairs={{0,4},{4,0},{8,12},{12,8},{1,5},{5,1},{9,13},{13,9},{2,6},{6,2},{1... | collective-permute-start | bytes 393224 | tf_op jit(solution)/shard_map/ppermute | solution.py:257
  115.8 8.8 %collective-permute-start.4 = (f32[8,4096]{1,0:T(8,128)S(1)}, f32[8,4096]{1,0:T(8,128)S(1)}, u32[]{:S(2)}, u32[]{:S(2)}) collective-permute-start(f32[8,4096]{1,0:T(8,128)S(1)} %add.62), channel_id=1, source_target_pairs={{0,8},{4,12},{8,0},{12,4},{1,9},{5,13},{9,1},{13,5},{2,10},{6,14},... | collective-permute-start | bytes 393224 | tf_op jit(solution)/shard_map/ppermute | solution.py:257

commit v21 on v20

--- a/solution.py
+++ b/solution.py
@@ -230,7 +230,7 @@
     folded = jnp.dot(jnp.asarray(cosine_constant(NZ)), jump_inverse, precision=lax.Precision.HIGHEST)
     folded = lax.dynamic_slice_in_dim(folded, inc_pos * nz_loc, nz_loc, axis=1)
     pick_z = (coef_income[:, None] == jnp.arange(NZ, dtype=jnp.int32)[None, :]).astype(jnp.float32)
-    weight = jnp.dot(pick_z, jnp.tile(folded, (1, columns)), precision=lax.Precision.HIGHEST)
+    weight = jnp.tile(jnp.dot(pick_z, folded, precision=lax.Precision.HIGHEST), (1, columns))
     lanes = columns * nz_loc
     group = (jnp.arange(lanes)[None, :] // nz_loc == jnp.arange(columns)[:, None]).astype(jnp.bfloat16)
     partial = illiquid_pick(

time: 130 us -> 135 us (1.038)
  local copies, waits for them, and re-layouts: 22 us -> 30 us
  matrix products: 5.29 us -> 2.26 us
    another operation x2 -> x3, local copies, waits for them, and re-layouts: 0.12 us -> 8.14 us  [the longest x2 8.03 us: body(): jnp.tile(jnp.dot(pick_z, folded, precision=lax.Precision.HIGHEST), (1, co...]
    dot_general x1, matrix products: 4.47 us -> 1.45 us  [body(): jnp.dot(pick_z, folded, precision=lax.Precision.HIGHEST)]
  transfers between devices with their start and end apart: 5 -> 5, of which waited for: 3 -> 3; matrix products, arithmetic and copies ran while one was open for 18% -> 21% of each run, Pallas kernels for 35% -> 34%
where the time goes in v21:
time: 135 us; the launch traced here: 134 us
  Pallas kernels  71 us (53%)
  local copies, waits for them, and re-layouts  30 us (22%)
  starting transfers between devices  11.9 us (9%)
  waiting for transfers between devices  11.4 us (8%)
  other arithmetic  7.47 us (6%)
  matrix products  2.26 us (2%)
    pallas_call x1, Pallas kernels, liquid_step(): pl.pallas_call(step_kernel, grid=(nz // zb,), in_specs=[pl.BlockSpec(memo...  45.2 us
    pallas_call x1, Pallas kernels, illiquid_pick(): pl.pallas_call(illiquid_kernel, grid_spec=pltpu.PrefetchScalarGridSpec(nu...  25.8 us
    ppermute x3, waiting for transfers between devices, all_sum(): x = x + lax.ppermute(x, axis, [(i, i ^ step) for i in range(count)])  11.4 us
    reshape x1, local copies, waits for them, and re-layouts, body(): jnp.transpose(liquid_part, (3, 2, 0, 1))  9.3 us
    another operation x2, local copies, waits for them, and re-layouts, body(): jnp.tile(jnp.dot(pick_z, folded, precision=lax.Precision.HIGHEST), (1, co...  8.03 us
    ppermute x3, starting transfers between devices, all_sum(): x = x + lax.ppermute(x, axis, [(i, i ^ step) for i in range(count)])  5.47 us
    ppermute x1, starting transfers between devices, edges(): lax.ppermute(tail, axis, [(i, (i + 1) % count) for i in range(ends)])  4.93 us
    slice x1, local copies, waits for them, and re-layouts, body(): head = values_in[:, :, 0, :].astype(jnp.float32)  3.11 us
  transfers between devices with their start and end apart: 5, of which 3 were waited for; matrix products, arithmetic and copies ran while one was open for 21% of the time, Pallas kernels for 34%

profile of v21, /device:TPU:0, one launch (start us, length us, event | category | flops | bytes accessed | tf_op | source)
XLA Modules:
  0.0 134.2 jit_solution(15174234258894914228)
XLA Ops:
  0.0 3.1 %fusion.9 = (bf16[8,32,1,512]{3,2,1,0:T(2,128)(2,1)S(1)}, bf16[8,32,1,512]{3,2,1,0:T(2,128)(2,1)S(1)}) fusion(bf16[8,32,64,512]{3,2,1,0:T(8,128)(2,1)} %vals_ref.1), kind=kLoop, calls=%fused_computation.40 | loop fusion | bytes 1048576 | tf_op jit(solution)/shard_map/slice | solution.py:210
  3.1 0.9 fusion.8
  4.0 4.9 %collective-permute-start = (bf16[8,32,512]{2,1,0:T(8,128)(2,1)S(1)}, bf16[8,32,512]{2,1,0:T(8,128)(2,1)S(1)}, u32[]{:S(2)}, u32[]{:S(2)}) collective-permute-start(bf16[8,32,512]{2,1,0:T(8,128)(2,1)S(1)} %get-tuple-element.8), channel_id=1, source_target_pairs={{0,4},{4,8},{8,12},{1,5},{5,9},{9,13},{2,6},{6,10},{10,14},{3,7},{... | collective-permute-start | bytes 786440 | tf_op jit(solution)/shard_map/ppermute | solution.py:185
  9.0 1.3 fusion.11
  10.3 1.3 fusion.10
  13.0 1.8 %convert_reduce_fusion = s32[1024]{0:T(1024)S(1)} fusion(s32[4096]{0:T(1024)S(1)} %add_bitcast_fusion, s32[1024]{0:T(1024)S(1)} %iota_add_fusion), kind=kLoop, calls=%fused_computation.1 | loop fusion | flops 12581888 | bytes 24576 | tf_op jit(solution)/shard_map/reduce_sum | solution.py:247
  16.3 1.4 %fusion = f32[4096,32]{0,1:T(8,128)S(1)} fusion(s32[4096]{0:T(1024)S(1)} %copy-done.6, f32[64,64]{0,1:T(8,128)S(1)} %fusion.12, s32[]{:T(128)S(6)} %select_n.69), kind=kOutput, calls=%fused_computation.3 | convolution fusion | flops 100925440 | bytes 557060 | tf_op jit(solution)/shard_map/dot_general | solution.py:233
  17.9 1.5 %collective-permute-start.1 = (bf16[8,32,512]{2,1,0:T(8,128)(2,1)S(1)}, bf16[8,32,512]{2,1,0:T(8,128)(2,1)S(1)}, u32[]{:S(2)}, u32[]{:S(2)}) collective-permute-start(bf16[8,32,512]{2,1,0:T(8,128)(2,1)S(1)} %get-tuple-element.6), channel_id=1, source_target_pairs={{4,0},{8,4},{12,8},{5,1},{9,5},{13,9},{6,2},{10,6},{14,10},{7,3},{... | collective-permute-start | bytes 786440 | tf_op jit(solution)/shard_map/ppermute | solution.py:186
  19.4 0.9 constant_dynamic-slice_fusion
  21.0 2.4 %tile.4 = f32[4096,8,32]{0,2,1:T(8,128)} broadcast(f32[4096,32]{0,1:T(8,128)S(1)} %fusion), dimensions={0,2} | broadcast | bytes 4718592 | tf_op jit(solution)/shard_map/tile | solution.py:233
  23.5 5.6 %copy.52.w_ref = f32[4096,256]{1,0:T(8,128)} copy(f32[4096,256]{0,1:T(8,128)} %bitcast.43) | data formatting | bytes 8388608 | tf_op jit(solution)/shard_map/tile | solution.py:233
  29.1 0.9 convert_element_type.21.lo_ref
  29.9 45.2 %shard_map.154 = f32[8,32,64,128]{3,2,1,0:T(8,128)} custom-call(f32[8]{0:T(128)} %load_ref.1, bf16[8,32,64,512]{3,2,1,0:T(8,128)(2,1)} %vals_ref.1, f32[8,32,512]{2,1,0:T(8,128)} %convert_element_type.21.lo_ref, f32[8,32,512]{2,1,0:T(8,128)} %get-tuple-element.7.up_ref, f32[32,64,512]{2,1,0:T(8,128)} %rl_ref.1, f32[32,64,512]{2,1,0:T(8,128)} %ri_ref.1, ...), custom_call_target="tpu_custom_call" | custom-call | tf_op jit(solution)/shard_map/pallas_call | solution.py:102
  75.2 9.3 %copy.50.t_ref = f32[128,64,256]{2,1,0:T(8,128)} copy(f32[128,64,256]{0,1,2:T(8,128)} %bitcast.42) | data formatting | bytes 16777216 | tf_op jit(solution)/shard_map/reshape | solution.py:227
  85.2 0.9 copy.51.rim_ref
  86.1 25.8 %shard_map.155 = f32[8,4096]{1,0:T(8,128)} custom-call(s32[4096]{0:T(1024)} %clamp_add_fusion.row_ref, bf16[256,192]{1,0:T(8,128)(2,1)} %copy.49.ca_ref, f32[128,64,256]{2,1,0:T(8,128)} %copy.50.t_ref, f32[128,2,256]{2,1,0:T(2,128)} %copy.51.rim_ref, f32[4096,256]{1,0:T(8,128)} %copy.52.w_ref, bf16[8,256]{1,0:T(8,128)(2,1)} %fusion.6.group_ref), custom_call_target="tpu_custom_call" | custom-call | tf_op jit(solution)/shard_map/pallas_call | solution.py:159
  111.9 1.5 %collective-permute-done.2 = f32[8,4096]{1,0:T(8,128)S(1)} collective-permute-done((f32[8,4096]{1,0:T(8,128)}, f32[8,4096]{1,0:T(8,128)S(1)}, u32[]{:S(2)}, u32[]{:S(2)}) %collective-permute-start.2) | collective-permute-done | bytes 131104 | tf_op jit(solution)/shard_map/ppermute | solution.py:257
  113.4 0.9 add.61
  114.3 2.7 %collective-permute-start.3 = (f32[8,4096]{1,0:T(8,128)S(1)}, f32[8,4096]{1,0:T(8,128)S(1)}, u32[]{:S(2)}, u32[]{:S(2)}) collective-permute-start(f32[8,4096]{1,0:T(8,128)S(1)} %add.61), channel_id=1, source_target_pairs={{0,4},{4,0},{8,12},{12,8},{1,5},{5,1},{9,13},{13,9},{2,6},{6,2},{1... | collective-permute-start | bytes 393224 | tf_op jit(solution)/shard_map/ppermute | solution.py:257
  117.0 3.8 %collective-permute-done.3 = f32[8,4096]{1,0:T(8,128)S(1)} collective-permute-done((f32[8,4096]{1,0:T(8,128)S(1)}, f32[8,4096]{1,0:T(8,128)S(1)}, u32[]{:S(2)}, u32[]{:S(2)}) %collective-permute-start.3) | collective-permute-done | bytes 131104 | tf_op jit(solution)/shard_map/ppermute | solution.py:257
  120.8 2.8 %collective-permute-start.4 = (f32[8,4096]{1,0:T(8,128)S(1)}, f32[8,4096]{1,0:T(8,128)S(1)}, u32[]{:S(2)}, u32[]{:S(2)}) collective-permute-start(f32[8,4096]{1,0:T(8,128)S(1)} %add.62), channel_id=1, source_target_pairs={{0,8},{4,12},{8,0},{12,4},{1,9},{5,13},{9,1},{13,5},{2,10},{6,14},... | collective-permute-start | bytes 393224 | tf_op jit(solution)/shard_map/ppermute | solution.py:257
  123.6 6.0 %collective-permute-done.4 = f32[8,4096]{1,0:T(8,128)S(1)} collective-permute-done((f32[8,4096]{1,0:T(8,128)S(1)}, f32[8,4096]{1,0:T(8,128)S(1)}, u32[]{:S(2)}, u32[]{:S(2)}) %collective-permute-start.4) | collective-permute-done | bytes 131104 | tf_op jit(solution)/shard_map/ppermute | solution.py:257
  130.3 2.8 %gather_fusion = f32[1024,8]{1,0:T(8,128)S(1)} fusion(f32[8,4096]{0,1:T(8,128)S(1)} %copy.53, s32[1024]{0:T(1024)S(1)} %broadcast_clamp_fusion), kind=kCustom, calls=%fused_computation | custom fusion | bytes 69632 | tf_op jit(solution)/shard_map/jit(_take)/gather | solution.py:248
  133.4 0.8 copy.54
  (45 shorter events, 5.4 us)
Async XLA Ops:
  0.0 14.8 %copy-start = (f32[64,64]{1,0:T(8,128)S(1)}, f32[64,64]{1,0:T(8,128)}, u32[]{:S(2)}) copy-start(f32[64,64]{1,0:T(8,128)} %param.23) | copy-start | bytes 49156
  0.0 14.8 %copy-start.3 = (f32[64,64]{1,0:T(8,128)S(1)}, f32[64,64]{1,0:T(8,128)}, u32[]{:S(2)}) copy-start(f32[64,64]{1,0:T(8,128)} %constant.77.clone) | copy-start | bytes 49156
  0.0 15.0 %copy-start.5 = (s32[4096]{0:T(1024)S(1)}, s32[4096]{0:T(1024)}, u32[]{:S(2)}) copy-start(s32[4096]{0:T(1024)} %param.24) | copy-start | bytes 49156
  0.0 15.1 %copy-start.4 = (s32[4096]{0:T(1024)S(1)}, s32[4096]{0:T(1024)}, u32[]{:S(2)}) copy-start(s32[4096]{0:T(1024)} %param.25) | copy-start | bytes 49156
  0.0 16.3 %copy-start.6 = (s32[4096]{0:T(1024)S(1)}, s32[4096]{0:T(1024)}, u32[]{:S(2)}) copy-start(s32[4096]{0:T(1024)} %param.26) | copy-start | bytes 49156
  4.0 13.7 %collective-permute-start = (bf16[8,32,512]{2,1,0:T(8,128)(2,1)S(1)}, bf16[8,32,512]{2,1,0:T(8,128)(2,1)S(1)}, u32[]{:S(2)}, u32[]{:S(2)}) collective-permute-start(bf16[8,32,512]{2,1,0:T(8,128)(2,1)S(1)} %get-tuple-element.8), channel_id=1, source_target_pairs={{0,4},{4,8},{8,12},{1,5},{5,9},{9,13},{2,6},{6,10},{10,14},{3,7},{... | collective-permute-start | bytes 786440 | tf_op jit(solution)/shard_map/ppermute | solution.py:185
  17.9 66.6 %collective-permute-start.1 = (bf16[8,32,512]{2,1,0:T(8,128)(2,1)S(1)}, bf16[8,32,512]{2,1,0:T(8,128)(2,1)S(1)}, u32[]{:S(2)}, u32[]{:S(2)}) collective-permute-start(bf16[8,32,512]{2,1,0:T(8,128)(2,1)S(1)} %get-tuple-element.6), channel_id=1, source_target_pairs={{4,0},{8,4},{12,8},{5,1},{9,5},{13,9},{6,2},{10,6},{14,10},{7,3},{... | collective-permute-start | bytes 786440 | tf_op jit(solution)/shard_map/ppermute | solution.py:186
  75.2 9.4 %copy-start.2 = (f32[128,512,1,1]{1,0,3,2:T(8,128)S(1)}, f32[128,512,1,1]{1,0,3,2:T(8,128)}, u32[]{:S(2)}) copy-start(f32[128,512,1,1]{1,0,3,2:T(8,128)} %constant.78) | copy-start | bytes 786436
  86.1 48.1 %copy-start.1 = (f32[64,64]{1,0:T(8,128)S(1)}, f32[64,64]{1,0:T(8,128)}, u32[]{:S(2)}) copy-start(f32[64,64]{1,0:T(8,128)} %param.23) | copy-start | bytes 49156
  111.8 1.6 %collective-permute-start.2 = (f32[8,4096]{1,0:T(8,128)}, f32[8,4096]{1,0:T(8,128)S(1)}, u32[]{:S(2)}, u32[]{:S(2)}) collective-permute-start(f32[8,4096]{1,0:T(8,128)} %shard_map.155), channel_id=1, source_target_pairs={{0,1},{1,0},{2,3},{3,2},{4,5},{5,4},{6,7},{7,6},{8,9},{9,8},{10,11... | collective-permute-start | bytes 393224 | tf_op jit(solution)/shard_map/ppermute | solution.py:257
  114.3 6.5 %collective-permute-start.3 = (f32[8,4096]{1,0:T(8,128)S(1)}, f32[8,4096]{1,0:T(8,128)S(1)}, u32[]{:S(2)}, u32[]{:S(2)}) collective-permute-start(f32[8,4096]{1,0:T(8,128)S(1)} %add.61), channel_id=1, source_target_pairs={{0,4},{4,0},{8,12},{12,8},{1,5},{5,1},{9,13},{13,9},{2,6},{6,2},{1... | collective-permute-start | bytes 393224 | tf_op jit(solution)/shard_map/ppermute | solution.py:257
  120.8 8.8 %collective-permute-start.4 = (f32[8,4096]{1,0:T(8,128)S(1)}, f32[8,4096]{1,0:T(8,128)S(1)}, u32[]{:S(2)}, u32[]{:S(2)}) collective-permute-start(f32[8,4096]{1,0:T(8,128)S(1)} %add.62), channel_id=1, source_target_pairs={{0,8},{4,12},{8,0},{12,4},{1,9},{5,13},{9,1},{13,5},{2,10},{6,14},... | collective-permute-start | bytes 393224 | tf_op jit(solution)/shard_map/ppermute | solution.py:257
